TPU v7x, 512 devices: a whole 4x8x8 slice. The times are simulated.
512 devices in a mesh: row: 16 (over z, core), col: 32 (over x, y).
Axes of the slice: x: 4, y: 8, z: 8, core: 2. Of those that a mesh axis runs over, the one named last changes fastest.
Arguments:
- pool: float32 [131072, 256], P(('row', 'col')), may hold values from -12 to 12
- row_pick: int32 [65536], replicated, may hold values from 0 to 8191, as said below
- length_scale: float32 [256], replicated, may hold values from 12 to 48
- panel_tile: int32 [1], replicated, may hold values from 0 to 959
Outputs:
- schur: float32 [65536, 4096], P('row', 'col')
- row_panel: float32 [65536, 64], P('row')
Inputs may be any that keep to these rules, and one draw needn't show every extreme that they name: `row_pick`: entry m indexes the 8192 pixels of tile-grid row m // 4096; entries of one tile-grid row are distinct, at most 160 of them lie in the 256 pixels of one device, and exactly 160 do for some device of each tile-grid row.
All inputs are finite; a program needn't handle non-finite values.
Results may differ from a plain program's by a relative error of at most 0.0003.
Values sent between devices are 32-bit elements; how exact they have to be, the bound alone decides.
No kernel may reach another device: no remote copies, remote signals or barrier semaphores. Data moves between devices by JAX's collectives and lax.ppermute only.
A program may use at most 64 MiB of HBM per device.

v0:
```python
import jax
import jax.numpy as jnp
from jax import lax
from jax.sharding import PartitionSpec as P

TB = 64
WT = 2


noise_level = 0.1
root_five = 5.0**0.5


def from_root(x, axis, root):
    mine = lax.axis_index(axis) == root
    return lax.psum(jnp.where(mine, x, jnp.zeros_like(x)), axis)


def kernel(left, right, left_index, right_index):
    left_sq = jnp.sum(left * left, axis=1)
    right_sq = jnp.sum(right * right, axis=1)
    cross = jnp.dot(
        left, right.T, precision=lax.Precision.HIGHEST, preferred_element_type=jnp.float32
    )
    dist_sq = jnp.maximum(left_sq[:, None] + right_sq[None, :] - 2.0 * cross, 0.0)
    radius = jnp.sqrt(dist_sq)
    value = (1.0 + root_five * radius + 5.0 / 3.0 * dist_sq) * jnp.exp(-root_five * radius)
    same = (left_index[:, None] == right_index[None, :]).astype(value.dtype)
    return value + noise_level * same


def panel_solve(factor, block):
    return lax.linalg.triangular_solve(factor, block, left_side=False, lower=True, transpose_a=True)


def body(pool, row_pick, length_scale, panel_tile):
    rows_count = lax.axis_size("row")
    cols_count = lax.axis_size("col")
    my_row = lax.axis_index("row")
    my_col = lax.axis_index("col")
    total_rows = row_pick.shape[0]
    local_rows = total_rows // rows_count
    my_pick = lax.dynamic_slice_in_dim(row_pick, my_row * local_rows, local_rows)
    gathered = lax.all_gather(pool, "col", axis=0, tiled=True)
    features = jnp.take(gathered, my_pick, axis=0)
    panel = panel_tile[0]
    tiles = panel + 1 + jnp.mod(my_col - panel - 1, cols_count) + cols_count * jnp.arange(WT)
    local_tiles = tiles // rows_count
    col_source = (local_tiles[:, None] * TB + jnp.arange(TB)[None, :]).reshape(-1)
    col_local = jnp.take(features, col_source, axis=0)
    col_feats = from_root(col_local, "row", my_col % rows_count)
    panel_row = panel % rows_count
    panel_local = panel // rows_count
    panel_rows = lax.dynamic_slice_in_dim(features, panel_local * TB, TB)
    panel_feats = from_root(panel_rows, "row", panel_row)
    inverse_scale = 1.0 / length_scale
    scaled_rows = features * inverse_scale
    scaled_cols = col_feats * inverse_scale
    scaled_panel = panel_feats * inverse_scale
    local_index = jnp.arange(local_rows)
    row_global = (local_index // TB * rows_count + my_row) * TB + local_index % TB
    col_global = (tiles[:, None] * TB + jnp.arange(TB)[None, :]).reshape(-1)
    panel_global = panel * TB + jnp.arange(TB)
    factor = jnp.linalg.cholesky(kernel(scaled_panel, scaled_panel, panel_global, panel_global))
    row_panel = panel_solve(factor, kernel(scaled_rows, scaled_panel, row_global, panel_global))
    col_panel = panel_solve(factor, kernel(scaled_cols, scaled_panel, col_global, panel_global))
    update = jnp.dot(
        row_panel, col_panel.T, precision=lax.Precision.HIGHEST, preferred_element_type=jnp.float32
    )
    schur = kernel(scaled_rows, scaled_cols, row_global, col_global) - update
    return (schur, row_panel)


def solution(mesh):
    in_specs = (P(("row", "col"), None), P(), P(), P())
    out_specs = (P("row", "col"), P("row", None))
    return jax.shard_map(body, mesh=mesh, in_specs=in_specs, out_specs=out_specs, check_vma=False)
```

profile of v0, /device:TPU:1, one launch (start us, length us, event | category | flops | bytes accessed | tf_op | source)
XLA Modules:
  0.0 298.0 jit_solution(12258355929983849131)
XLA Ops:
  7.2 0.0 all-gather.2.cloned.1.call-start
  7.2 0.7 all-gather.2.cloned.1.call-update
  7.9 0.0 all-reduce.3.cloned.1.call-start
  8.6 0.1 iota_add_fusion.1
  8.7 0.1 add.313
  8.8 0.1 add.310
  8.9 0.1 iota_add_fusion
  9.0 0.1 add.328
  9.1 0.7 compare_and_fusion
  9.8 0.7 fusion.75
  10.5 0.7 broadcast_divide_fusion
  11.2 107.6 %all-gather.2.cloned.1.call-done = f32[8192,256]{1,0:T(8,128)} async-done(((f32[256,256]{1,0:T(8,128)}), f32[8192,256]{1,0:T(8,128)}) %all-gather.2.cloned.1.call-update) | async-done | bytes 8388624 | tf_op jit(solution)/shard_map/all_gather | solution.py:44
  118.9 19.5 %gather_fusion = f32[4096,256]{1,0:T(8,128)} fusion(f32[8192,256]{1,0:T(8,128)} %all-gather.2.cloned.1.call-done, s32[4096]{0:T(1024)S(1)} %fusion.75), kind=kCustom, calls=%fused_computation | custom fusion | bytes 8404992 | tf_op jit(solution)/shard_map/jit(_take)/gather | solution.py:45
  138.3 4.1 %multiply_reduce_fusion = (f32[4096]{0:T(1024)S(1)}, f32[4096,256]{1,0:T(8,128)}) fusion(f32[256]{0:T(256)S(1)} %broadcast_divide_fusion, f32[4096,256]{1,0:T(8,128)} %gather_fusion, pred[4096]{0:T(1024)(128)(4,1)S(1)} %compare_and_fusion), kind=kLoop, calls=%fused_computation.9 | loop fusion | flops 4190208 | bytes 8410112 | tf_op jit(solution)/shard_map/reduce_sum | solution.py:20
  142.4 2.9 gather_fusion.1
  145.4 1.5 dynamic-slice_select_fusion
  146.8 0.7 select_select_fusion
  147.6 0.0 all-reduce.3.cloned.1.call-update
  147.6 110.7 %all-reduce.3.cloned.1.call-done = (f32[64,256]{1,0:T(8,128)}, f32[128,256]{1,0:T(8,128)}) async-done(((f32[64,256]{1,0:T(8,128)}, f32[128,256]{1,0:T(8,128)}), (f32[64,256]{1,0:T(8,128)}, f32[128,256]{1,0:T(8,128)})) %all-reduce.3.cloned.1.call-update) | async-done | bytes 196624 | tf_op jit(solution)/shard_map/psum | solution.py:16
  258.3 0.9 multiply_reduce_fusion.2
  259.3 1.1 fusion.91
  260.4 0.0 copy-start.1
  260.4 0.0 copy-start.2
  260.5 0.0 copy-start
  260.5 6.6 %fusion.3 = f32[4096,64]{0,1:T(8,128)S(1)} fusion(f32[4096,256]{1,0:T(8,128)} %get-tuple-element.7, f32[256]{0:T(256)S(1)} %broadcast_divide_fusion, f32[64]{0:T(128)S(1)} %multiply_reduce_fusion.2, f32[4096]{0:T(1024)S(1)} %get-tuple-element.6, f32[64,256]{1,0:T(8,128)} %get-tuple-element.2), kind=kOutput, calls=%fused_computation.8 | convolution fusion | flops 807419904 | bytes 5326080 | tf_op jit(solution)/shard_map/dot_general | solution.py:22
  267.1 0.0 copy-done.1
  267.1 0.1 multiply_reduce_fusion.1
  267.2 0.0 copy-done.2
  267.2 0.3 fusion.9
  267.5 0.0 copy-done
  267.5 3.4 %fusion.1 = f32[4096,128]{1,0:T(8,128)S(1)} fusion(f32[4096,256]{1,0:T(8,128)S(1)} %copy-done, f32[256]{0:T(256)S(1)} %broadcast_divide_fusion, f32[128]{0:T(128)S(1)} %multiply_reduce_fusion.1, f32[4096]{0:T(1024)S(1)} %get-tuple-element.6, f32[128,256]{1,0:T(8,128)S(1)} %copy-done.1), kind=kOutput, calls=%fused_computation.5 | convolution fusion | flops 1613791232 | bytes 6440448 | tf_op jit(solution)/shard_map/dot_general | solution.py:22
  270.9 0.1 copy.8
  271.0 0.1 copy.9
  271.1 0.1 copy.6
  271.2 0.1 add_multiply_fusion
  271.3 5.8 %cholesky.15 = f32[64,64]{1,0:T(8,128)S(1)} custom-call(f32[64,64]{1,0:T(8,128)S(1)} %add_multiply_fusion), custom_call_target="Cholesky" | custom-call | tf_op jit(solution)/shard_map/jit(cholesky)/cholesky | solution.py:64
  277.2 0.6 compare_reduce_fusion
  277.8 0.7 fusion.37
  278.5 4.9 %custom-call.8 = f32[1,64,64]{1,2,0:T(8,128)S(1)} custom-call(f32[1,64,64]{2,1,0:T(8,128)S(1)} %fusion.37), custom_call_target="InvertDiagBlocksLowerTriangular" | custom-call | tf_op jit(solution)/shard_map/triangular_solve | solution.py:33
  283.4 1.7 fusion.10
  285.1 0.0 copy-start.3
  285.1 0.4 fusion.38
  285.5 5.7 %convolution_subtract_fusion = f32[4096,128]{1,0:T(8,128)} fusion(f32[4096,64]{0,1:T(8,128)S(1)} %fusion.10, f32[128,64]{1,0:T(8,128)S(1)} %fusion.38, f32[4096,128]{1,0:T(8,128)S(1)} %fusion.1, s32[128]{0:T(128)S(1)} %add.328, s32[4096]{0:T(1024)S(1)} %fusion.65), kind=kOutput, calls=%fused_computation.2 | convolution fusion | flops 407896064 | bytes 5292544 | tf_op jit(solution)/shard_map/dot_general | solution.py:67
  291.1 0.0 copy-done.3
  (7 shorter events, 0.1 us)
Async XLA Ops:
  7.2 111.7 %all-gather.2.cloned.1.call-start = ((), (), s32[]{:S(2)}) async-start(), calls=%async_computation | async-start | bytes 8650752 | tf_op jit(solution)/shard_map/all_gather | solution.py:44
  7.9 250.4 %all-reduce.3.cloned.1.call-start = ((), (), s32[]{:S(2)}) async-start(), calls=%async_computation.1 | async-start | bytes 393216 | tf_op jit(solution)/shard_map/psum | solution.py:16
  260.4 6.7 %copy-start.1 = (f32[128,256]{1,0:T(8,128)S(1)}, f32[128,256]{1,0:T(8,128)}, u32[]{:S(2)}) copy-start(f32[128,256]{1,0:T(8,128)} %get-tuple-element.3) | copy-start | bytes 393220
  260.4 6.8 %copy-start.2 = (f32[64,256]{1,0:T(8,128)S(1)}, f32[64,256]{1,0:T(8,128)}, u32[]{:S(2)}) copy-start(f32[64,256]{1,0:T(8,128)} %get-tuple-element.2) | copy-start | bytes 196612
  260.5 7.0 %copy-start = (f32[4096,256]{1,0:T(8,128)S(1)}, f32[4096,256]{1,0:T(8,128)}, u32[]{:S(2)}) copy-start(f32[4096,256]{1,0:T(8,128)} %get-tuple-element.7) | copy-start | bytes 12582916
  285.1 6.0 %copy-start.3 = (f32[4096,64]{0,1:T(8,128)}, f32[4096,64]{0,1:T(8,128)S(1)}, u32[]{:S(2)}) copy-start(f32[4096,64]{0,1:T(8,128)S(1)} %fusion.10) | copy-start | bytes 3145732
Sparse Core Ops, SparseCore 0:
  11.1 107.6 all-gather.1
  147.7 110.5 all-reduce.2
where the time goes:
time: 298 us
  waiting for transfers between devices  219 us (73%)
  local copies, waits for them, and re-layouts  22.9 us (8%)
  other arithmetic  21.9 us (7%)
  matrix products  19.2 us (6%)
  between operations  14.9 us (5%)
    psum x1, waiting for transfers between devices, from_root(): return lax.psum(jnp.where(mine, x, jnp.zeros_like(x)), axis)  111 us
    all_gather x1, waiting for transfers between devices, body(): gathered = lax.all_gather(pool, 'col', axis=0, tiled=True)  108 us
    gather x1, local copies, waits for them, and re-layouts, body(): features = jnp.take(gathered, my_pick, axis=0)  19.5 us
    dot_general x4, matrix products, kernel(): jnp.dot(left, right.T, precision=lax.Precision.HIGHEST, preferred_element...  11.5 us
    another operation x3, other arithmetic, body(): jnp.linalg.cholesky(kernel(scaled_panel, scaled_panel, panel_global, pane...  6.52 us
  transfers between devices with their start and end apart: 2, of which 2 were waited for; matrix products, arithmetic and copies ran while one was open for 1% of the time, Pallas kernels for 0%

commit v1 on v0

--- a/solution.py
+++ b/solution.py
@@ -11,9 +11,25 @@
 root_five = 5.0**0.5
 
 
-def from_root(x, axis, root):
-    mine = lax.axis_index(axis) == root
-    return lax.psum(jnp.where(mine, x, jnp.zeros_like(x)), axis)
+def broadcast_rows(x, root, rows_count):
+    dist = jnp.mod(lax.axis_index("row") - root, rows_count)
+    step = 1
+    while step < rows_count:
+        perm = [(i, (i + step) % rows_count) for i in range(rows_count)]
+        got = lax.ppermute(x, "row", perm)
+        x = jnp.where((dist >= step) & (dist < 2 * step), got, x)
+        step *= 2
+    return x
+
+
+def window_perm(rows_count, cols_count):
+    pairs = []
+    for g in range(rows_count):
+        for c2 in range(cols_count):
+            r = c2 % rows_count
+            c = g + rows_count * (c2 // rows_count)
+            pairs.append((g * cols_count + c2, r * cols_count + c))
+    return pairs
 
 
 def kernel(left, right, left_index, right_index):
@@ -45,14 +61,16 @@
     features = jnp.take(gathered, my_pick, axis=0)
     panel = panel_tile[0]
     tiles = panel + 1 + jnp.mod(my_col - panel - 1, cols_count) + cols_count * jnp.arange(WT)
-    local_tiles = tiles // rows_count
+    served = my_row + rows_count * (my_col // rows_count)
+    served_tiles = panel + 1 + jnp.mod(served - panel - 1, cols_count) + cols_count * jnp.arange(WT)
+    local_tiles = served_tiles // rows_count
     col_source = (local_tiles[:, None] * TB + jnp.arange(TB)[None, :]).reshape(-1)
     col_local = jnp.take(features, col_source, axis=0)
-    col_feats = from_root(col_local, "row", my_col % rows_count)
+    col_feats = lax.ppermute(col_local, ("row", "col"), window_perm(rows_count, cols_count))
     panel_row = panel % rows_count
     panel_local = panel // rows_count
     panel_rows = lax.dynamic_slice_in_dim(features, panel_local * TB, TB)
-    panel_feats = from_root(panel_rows, "row", panel_row)
+    panel_feats = broadcast_rows(panel_rows, panel_row, rows_count)
     inverse_scale = 1.0 / length_scale
     scaled_rows = features * inverse_scale
     scaled_cols = col_feats * inverse_scale

time: 298 us -> 220 us (0.74)
  the two profiles are of different devices: /device:TPU:1 before, /device:TPU:66 now
where the time goes in v1:
time: 220 us; the launch traced here: 219 us
  waiting for transfers between devices  123 us (56%)
  local copies, waits for them, and re-layouts  25.4 us (12%)
  matrix products  19.6 us (9%)
  other arithmetic  18.6 us (8%)
  starting transfers between devices  17.9 us (8%)
  between operations  15 us (7%)
    all_gather x1, waiting for transfers between devices, body(): gathered = lax.all_gather(pool, 'col', axis=0, tiled=True)  105 us
    gather x1, local copies, waits for them, and re-layouts, body(): features = jnp.take(gathered, my_pick, axis=0)  19.5 us
    dot_general x4, matrix products, kernel(): jnp.dot(left, right.T, precision=lax.Precision.HIGHEST, preferred_element...  10.1 us
    ppermute x4, waiting for transfers between devices, broadcast_rows(): got = lax.ppermute(x, 'row', perm)  9.98 us
    ppermute x4, starting transfers between devices, broadcast_rows(): got = lax.ppermute(x, 'row', perm)  8.94 us
    ppermute x1, starting transfers between devices, body(): lax.ppermute(col_local, ('row', 'col'), window_perm(rows_count, cols_count))  8.93 us
    ppermute x1, waiting for transfers between devices, body(): lax.ppermute(col_local, ('row', 'col'), window_perm(rows_count, cols_count))  7.29 us
    dot_general x1, matrix products, body(): jnp.dot(row_panel, col_panel.T, precision=lax.Precision.HIGHEST, preferre...  6.73 us
  transfers between devices with their start and end apart: 6, of which 4 were waited for; matrix products, arithmetic and copies ran while one was open for 5% of the time, Pallas kernels for 0%

profile of v1, /device:TPU:66, one launch (start us, length us, event | category | flops | bytes accessed | tf_op | source)
XLA Modules:
  0.0 219.3 jit_solution(17571182219345366635)
XLA Ops:
  7.2 0.0 all-gather.2.cloned.1.call-start
  7.2 0.7 all-gather.2.cloned.1.call-update
  8.7 0.1 iota_add_fusion.1
  8.7 0.1 add.328
  8.8 0.1 add.325
  8.9 0.1 iota_add_fusion
  9.0 0.6 add.347
  9.6 0.7 compare_and_fusion
  10.3 0.7 fusion.70
  11.1 0.7 broadcast_divide_fusion
  11.8 105.0 %all-gather.2.cloned.1.call-done = f32[8192,256]{1,0:T(8,128)} async-done(((f32[256,256]{1,0:T(8,128)}), f32[8192,256]{1,0:T(8,128)}) %all-gather.2.cloned.1.call-update) | async-done | bytes 8388624 | tf_op jit(solution)/shard_map/all_gather | solution.py:60
  116.8 19.5 %gather_fusion = f32[4096,256]{1,0:T(8,128)} fusion(f32[8192,256]{1,0:T(8,128)} %all-gather.2.cloned.1.call-done, s32[4096]{0:T(1024)S(1)} %fusion.70), kind=kCustom, calls=%fused_computation | custom fusion | bytes 8404992 | tf_op jit(solution)/shard_map/jit(_take)/gather | solution.py:61
  136.2 2.9 %multiply_reduce_fusion = (f32[4096]{0:T(1024)S(1)}, f32[4096,256]{1,0:T(8,128)S(1)}) fusion(f32[256]{0:T(256)S(1)} %broadcast_divide_fusion, f32[4096,256]{1,0:T(8,128)} %gather_fusion, pred[4096]{0:T(1024)(128)(4,1)S(1)} %compare_and_fusion), kind=kLoop, calls=%fused_computation.7 | loop fusion | flops 4190208 | bytes 8410112 | tf_op jit(solution)/shard_map/reduce_sum | solution.py:36
  139.1 0.0 copy-start
  139.2 1.9 copy-done
  141.1 0.0 collective-permute-start.1
  141.1 2.9 %gather_fusion.1 = f32[128,256]{1,0:T(8,128)S(1)} fusion(f32[4096,256]{1,0:T(8,128)} %copy-done, s32[1024]{0:T(1024)S(1)} %pad_clamp_fusion), kind=kCustom, calls=%fused_computation.1 | custom fusion | bytes 262656 | tf_op jit(solution)/shard_map/jit(_take)/gather | solution.py:68
  144.0 0.7 collective-permute-done.1
  144.8 0.8 broadcast_select_fusion.2
  145.6 3.5 %collective-permute-start.2 = (f32[64,256]{1,0:T(8,128)S(1)}, f32[64,256]{1,0:T(8,128)S(1)}, u32[]{:S(2)}, u32[]{:S(2)}) collective-permute-start(f32[64,256]{1,0:T(8,128)S(1)} %broadcast_select_fusion.2), channel_id=1, source_target_pairs={{0,64},{32,96},{64,128},{96,160},{128,192},{160,224},{192,256},{22... | collective-permute-start | bytes 196616 | tf_op jit(solution)/shard_map/ppermute | solution.py:19
  149.2 0.1 broadcast_select_fusion.1
  149.3 8.9 %collective-permute-start = (f32[128,256]{1,0:T(8,128)S(1)}, f32[128,256]{1,0:T(8,128)S(1)}, u32[]{:S(2)}, u32[]{:S(2)}) collective-permute-start(f32[128,256]{1,0:T(8,128)S(1)} %broadcast_select_fusion.1), channel_id=1, source_target_pairs={{0,0},{1,32},{2,64},{3,96},{4,128},{5,160},{6,192},{7,224},{8,256}... | collective-permute-start | bytes 393224 | tf_op jit(solution)/shard_map/ppermute | solution.py:69
  158.2 0.0 collective-permute-done.2
  158.2 0.0 copy-start.1
  158.2 3.3 %collective-permute-start.3 = (f32[64,256]{1,0:T(8,128)S(1)}, f32[64,256]{1,0:T(8,128)S(1)}, u32[]{:S(2)}, u32[]{:S(2)}) collective-permute-start(f32[64,256]{1,0:T(8,128)S(1)} %broadcast_select_fusion.3), channel_id=1, source_target_pairs={{0,128},{32,160},{64,192},{96,224},{128,256},{160,288},{192,320},{... | collective-permute-start | bytes 196616 | tf_op jit(solution)/shard_map/ppermute | solution.py:19
  161.5 7.3 %collective-permute-done = f32[128,256]{1,0:T(8,128)S(1)} collective-permute-done((f32[128,256]{1,0:T(8,128)S(1)}, f32[128,256]{1,0:T(8,128)S(1)}, u32[]{:S(2)}, u32[]{:S(2)}) %collective-permute-start) | collective-permute-done | bytes 131104 | tf_op jit(solution)/shard_map/ppermute | solution.py:69
  168.8 5.3 %convolution_multiply_fusion = f32[4096,128]{1,0:T(8,128)S(1)} fusion(f32[4096,256]{1,0:T(8,128)} %copy-done, f32[256]{0:T(256)S(1)} %broadcast_divide_fusion, f32[128,256]{1,0:T(8,128)S(1)} %collective-permute-done), kind=kOutput, calls=%fused_computation.3 | convolution fusion | flops 1612218368 | bytes 6423552 | tf_op jit(solution)/shard_map/dot_general | solution.py:38
  174.1 0.0 collective-permute-done.3
  174.2 2.1 collective-permute-start.4
  176.3 0.1 multiply_reduce_fusion.1
  176.4 9.3 %collective-permute-done.4 = f32[64,256]{1,0:T(8,128)S(1)} collective-permute-done((f32[64,256]{1,0:T(8,128)S(1)}, f32[64,256]{1,0:T(8,128)S(1)}, u32[]{:S(2)}, u32[]{:S(2)}) %collective-permute-start.4) | collective-permute-done | bytes 65568 | tf_op jit(solution)/shard_map/ppermute | solution.py:19
  185.6 0.1 multiply_reduce_fusion.2
  185.7 0.2 fusion.85
  186.0 0.0 copy-done.1
  186.0 4.3 %fusion.1 = f32[4096,64]{0,1:T(8,128)S(1)} fusion(f32[64,256]{1,0:T(8,128)S(1)} %get-tuple-element.7, f32[4096,256]{1,0:T(8,128)S(1)} %copy-done.1, f32[256]{0:T(256)S(1)} %broadcast_divide_fusion, f32[64]{0:T(128)S(1)} %get-tuple-element.6, f32[4096]{0:T(1024)S(1)} %get-tuple-element.4), kind=kOutput, calls=%fused_computation.6 | convolution fusion | flops 807403520 | bytes 5326080 | tf_op jit(solution)/shard_map/dot_general | solution.py:38
  190.3 0.1 copy.8
  190.4 0.1 copy.9
  190.5 0.1 copy.6
  190.5 0.1 add_multiply_fusion
  190.6 5.8 %cholesky.15 = f32[64,64]{1,0:T(8,128)S(1)} custom-call(f32[64,64]{1,0:T(8,128)S(1)} %add_multiply_fusion), custom_call_target="Cholesky" | custom-call | tf_op jit(solution)/shard_map/jit(cholesky)/cholesky | solution.py:82
  196.5 0.6 compare_reduce_fusion
  197.2 0.7 fusion.30
  197.8 4.9 %custom-call.8 = f32[1,64,64]{1,2,0:T(8,128)S(1)} custom-call(f32[1,64,64]{2,1,0:T(8,128)S(1)} %fusion.30), custom_call_target="InvertDiagBlocksLowerTriangular" | custom-call | tf_op jit(solution)/shard_map/triangular_solve | solution.py:49
  202.7 1.7 fusion.6
  204.5 0.0 copy-start.2
  204.5 0.3 convolution_multiply_fusion.2
  204.7 1.0 fusion.31
  205.8 6.7 %convolution_subtract_fusion = f32[4096,128]{1,0:T(8,128)} fusion(f32[4096,64]{0,1:T(8,128)S(1)} %fusion.6, f32[128,64]{1,0:T(8,128)S(1)} %fusion.31, f32[4096,128]{1,0:T(8,128)S(1)} %convolution_multiply_fusion, s32[128]{0:T(128)} %add.347, f32[128]{0:T(128)S(1)} %multiply_reduce_fusion.1, f32[4096]{0:T(1024)S(1)} %get-tuple-element.4, s32[4096]{0:T(1024)S(1)} %fusion.58), kind=kOutput, calls=%fused_computation.2 | convolution fusion | flops 409468928 | bytes 5309440 | tf_op jit(solution)/shard_map/dot_general | solution.py:85
  (12 shorter events, 0.1 us)
Async XLA Ops:
  7.2 109.6 %all-gather.2.cloned.1.call-start = ((), (), s32[]{:S(2)}) async-start(), calls=%async_computation | async-start | bytes 8650752 | tf_op jit(solution)/shard_map/all_gather | solution.py:60
  139.1 1.9 copy-start
  141.1 3.7 %collective-permute-start.1 = (f32[64,256]{1,0:T(8,128)S(1)}, f32[64,256]{1,0:T(8,128)S(1)}, u32[]{:S(2)}, u32[]{:S(2)}) collective-permute-start(f32[64,256]{1,0:T(8,128)S(1)} %constant_dynamic-slice_fusion), channel_id=1, source_target_pairs={{0,32},{32,64},{64,96},{96,128},{128,160},{160,192},{192,224},{224... | collective-permute-start | bytes 196616 | tf_op jit(solution)/shard_map/ppermute | solution.py:19
  145.6 12.6 %collective-permute-start.2 = (f32[64,256]{1,0:T(8,128)S(1)}, f32[64,256]{1,0:T(8,128)S(1)}, u32[]{:S(2)}, u32[]{:S(2)}) collective-permute-start(f32[64,256]{1,0:T(8,128)S(1)} %broadcast_select_fusion.2), channel_id=1, source_target_pairs={{0,64},{32,96},{64,128},{96,160},{128,192},{160,224},{192,256},{22... | collective-permute-start | bytes 196616 | tf_op jit(solution)/shard_map/ppermute | solution.py:19
  149.3 19.6 %collective-permute-start = (f32[128,256]{1,0:T(8,128)S(1)}, f32[128,256]{1,0:T(8,128)S(1)}, u32[]{:S(2)}, u32[]{:S(2)}) collective-permute-start(f32[128,256]{1,0:T(8,128)S(1)} %broadcast_select_fusion.1), channel_id=1, source_target_pairs={{0,0},{1,32},{2,64},{3,96},{4,128},{5,160},{6,192},{7,224},{8,256}... | collective-permute-start | bytes 393224 | tf_op jit(solution)/shard_map/ppermute | solution.py:69
  158.2 27.7 %copy-start.1 = (f32[4096,256]{1,0:T(8,128)S(1)}, f32[4096,256]{1,0:T(8,128)}, u32[]{:S(2)}) copy-start(f32[4096,256]{1,0:T(8,128)} %copy-done) | copy-start | bytes 12582916
  158.2 15.9 %collective-permute-start.3 = (f32[64,256]{1,0:T(8,128)S(1)}, f32[64,256]{1,0:T(8,128)S(1)}, u32[]{:S(2)}, u32[]{:S(2)}) collective-permute-start(f32[64,256]{1,0:T(8,128)S(1)} %broadcast_select_fusion.3), channel_id=1, source_target_pairs={{0,128},{32,160},{64,192},{96,224},{128,256},{160,288},{192,320},{... | collective-permute-start | bytes 196616 | tf_op jit(solution)/shard_map/ppermute | solution.py:19
  174.2 11.5 %collective-permute-start.4 = (f32[64,256]{1,0:T(8,128)S(1)}, f32[64,256]{1,0:T(8,128)S(1)}, u32[]{:S(2)}, u32[]{:S(2)}) collective-permute-start(f32[64,256]{1,0:T(8,128)S(1)} %broadcast_select_fusion.4), channel_id=1, source_target_pairs={{0,256},{32,288},{64,320},{96,352},{128,384},{160,416},{192,448},{... | collective-permute-start | bytes 196616 | tf_op jit(solution)/shard_map/ppermute | solution.py:19
  204.5 8.0 %copy-start.2 = (f32[4096,64]{0,1:T(8,128)}, f32[4096,64]{0,1:T(8,128)S(1)}, u32[]{:S(2)}) copy-start(f32[4096,64]{0,1:T(8,128)S(1)} %fusion.6) | copy-start | bytes 3145732
Sparse Core Ops, SparseCore 0:
  11.1 105.5 all-gather.1

commit v2 on v1

--- a/solution.py
+++ b/solution.py
@@ -5,20 +5,27 @@
 
 TB = 64
 WT = 2
+CAP = 160
 
 
 noise_level = 0.1
 root_five = 5.0**0.5
 
 
-def broadcast_rows(x, root, rows_count):
+def broadcast_rows(x, root, rows_count, radix=4):
     dist = jnp.mod(lax.axis_index("row") - root, rows_count)
     step = 1
     while step < rows_count:
-        perm = [(i, (i + step) % rows_count) for i in range(rows_count)]
-        got = lax.ppermute(x, "row", perm)
-        x = jnp.where((dist >= step) & (dist < 2 * step), got, x)
-        step *= 2
+        new = x
+        for k in range(1, radix):
+            shift = k * step
+            if shift >= rows_count:
+                break
+            perm = [(i, (i + shift) % rows_count) for i in range(rows_count)]
+            got = lax.ppermute(x, "row", perm)
+            new = jnp.where((dist >= shift) & (dist < shift + step), got, new)
+        x = new
+        step *= radix
     return x
 
 
@@ -57,19 +64,29 @@
     total_rows = row_pick.shape[0]
     local_rows = total_rows // rows_count
     my_pick = lax.dynamic_slice_in_dim(row_pick, my_row * local_rows, local_rows)
-    gathered = lax.all_gather(pool, "col", axis=0, tiled=True)
-    features = jnp.take(gathered, my_pick, axis=0)
+    pool_rows = pool.shape[0]
+    group_pixels = pool_rows * cols_count
+    picked = jnp.zeros((group_pixels,), jnp.int32).at[my_pick].set(1, unique_indices=True)
+    counts = jnp.cumsum(picked.reshape(cols_count, pool_rows), axis=1)
+    mine = lax.dynamic_index_in_dim(counts, my_col, axis=0, keepdims=False)
+    slots = jnp.arange(CAP, dtype=jnp.int32)
+    local_idx = jnp.sum((mine[None, :] <= slots[:, None]).astype(jnp.int32), axis=1)
+    compact = jnp.take(pool, jnp.minimum(local_idx, pool_rows - 1), axis=0)
+    gathered = lax.all_gather(compact, "col", axis=0, tiled=True)
+    slot_of = (counts - 1).reshape(-1)
+    pick_idx = my_pick // pool_rows * CAP + jnp.take(slot_of, my_pick)
+    features = jnp.take(gathered, pick_idx, axis=0)
     panel = panel_tile[0]
     tiles = panel + 1 + jnp.mod(my_col - panel - 1, cols_count) + cols_count * jnp.arange(WT)
     served = my_row + rows_count * (my_col // rows_count)
     served_tiles = panel + 1 + jnp.mod(served - panel - 1, cols_count) + cols_count * jnp.arange(WT)
     local_tiles = served_tiles // rows_count
     col_source = (local_tiles[:, None] * TB + jnp.arange(TB)[None, :]).reshape(-1)
-    col_local = jnp.take(features, col_source, axis=0)
+    col_local = jnp.take(gathered, jnp.take(pick_idx, col_source), axis=0)
     col_feats = lax.ppermute(col_local, ("row", "col"), window_perm(rows_count, cols_count))
     panel_row = panel % rows_count
     panel_local = panel // rows_count
-    panel_rows = lax.dynamic_slice_in_dim(features, panel_local * TB, TB)
+    panel_rows = jnp.take(gathered, lax.dynamic_slice_in_dim(pick_idx, panel_local * TB, TB), axis=0)
     panel_feats = broadcast_rows(panel_rows, panel_row, rows_count)
     inverse_scale = 1.0 / length_scale
     scaled_rows = features * inverse_scale

time: 220 us -> 217 us (0.986)
  the two profiles are of different devices: /device:TPU:66 before, /device:TPU:1 now
where the time goes in v2:
time: 217 us; the launch traced here: 215 us
  waiting for transfers between devices  67 us (31%)
  local copies, waits for them, and re-layouts  66.3 us (31%)
  starting transfers between devices  29.1 us (13%)
  other arithmetic  18.9 us (9%)
  matrix products  18.6 us (9%)
  between operations  15.2 us (7%)
    all_gather x1, waiting for transfers between devices, body(): gathered = lax.all_gather(compact, 'col', axis=0, tiled=True)  66.3 us
    ppermute x6, starting transfers between devices, broadcast_rows(): got = lax.ppermute(x, 'row', perm)  25.7 us
    gather x1, local copies, waits for them, and re-layouts, body(): pick_idx = my_pick // pool_rows * CAP + jnp.take(slot_of, my_pick)  23 us
    gather x1, local copies, waits for them, and re-layouts, body(): features = jnp.take(gathered, pick_idx, axis=0)  18.6 us
    scatter x1, local copies, waits for them, and re-layouts, body(): jnp.zeros((group_pixels,), jnp.int32).at[my_pick]  15.5 us
    dot_general x4, matrix products, kernel(): jnp.dot(left, right.T, precision=lax.Precision.HIGHEST, preferred_element...  10.6 us
    another operation x3, other arithmetic, body(): jnp.linalg.cholesky(kernel(scaled_panel, scaled_panel, panel_global, pane...  6.52 us
    dot_general x1, matrix products, body(): jnp.dot(row_panel, col_panel.T, precision=lax.Precision.HIGHEST, preferre...  6.07 us
  transfers between devices with their start and end apart: 8, of which 2 were waited for; matrix products, arithmetic and copies ran while one was open for 33% of the time, Pallas kernels for 0%

profile of v2, /device:TPU:1, one launch (start us, length us, event | category | flops | bytes accessed | tf_op | source)
XLA Modules:
  0.0 215.1 jit_solution(8989804977687812215)
XLA Ops:
  7.2 0.8 broadcast_clamp_fusion
  8.0 15.5 %scatter_custom_fusion = s32[8192]{0:T(1024)S(1)} fusion(s32[4096]{0:T(1024)S(1)} %get-tuple-element.11, s32[4096]{0:T(1024)S(1)} %ne.96, s32[]{:T(128)} %constant.272.clone.1), kind=kCustom, calls=%fused_computation.118 | custom fusion | bytes 32772 | tf_op jit(solution)/shard_map/scatter | solution.py:69
  23.6 0.6 reduce-window.6
  24.1 0.2 slice_reduce_fusion
  24.4 0.1 add_add_fusion
  24.5 0.1 convert_reduce_fusion
  24.7 0.8 gather_fusion.1
  25.5 0.8 broadcast_select_fusion
  27.1 0.1 add.419
  27.2 0.1 add.416
  27.4 0.1 add.442
  27.5 23.0 %gather_fusion = s32[4096]{0:T(1024)S(1)} fusion(s32[8192]{0:T(1024)S(1)} %bitcast.46, s32[4096]{0:T(1024)S(1)} %get-tuple-element.10), kind=kCustom, calls=%fused_computation | custom fusion | bytes 49152 | tf_op jit(solution)/shard_map/jit(_take)/gather | solution.py:77
  50.6 0.7 compare_and_fusion
  51.4 1.1 gather_fusion.3
  52.5 0.1 compare_and_fusion.1
  52.7 66.3 %all-gather.2.cloned.1.call-done = f32[5120,256]{1,0:T(8,128)} async-done(((f32[160,256]{1,0:T(8,128)}), f32[5120,256]{1,0:T(8,128)}) %all-gather.2.cloned.1.call-update) | async-done | bytes 5242896 | tf_op jit(solution)/shard_map/all_gather | solution.py:75
  119.0 3.1 %gather_fusion.5 = f32[64,256]{1,0:T(8,128)S(1)} fusion(f32[5120,256]{1,0:T(8,128)} %all-gather.2.cloned.1.call-done, s32[1024]{0:T(1024)S(1)} %pad_clamp_fusion), kind=kCustom, calls=%fused_computation.5 | custom fusion | bytes 131328 | tf_op jit(solution)/shard_map/jit(_take)/gather | solution.py:89
  122.1 0.1 broadcast_select_fusion.2
  122.2 4.9 %collective-permute-start.3 = (f32[64,256]{1,0:T(8,128)S(1)}, f32[64,256]{1,0:T(8,128)S(1)}, u32[]{:S(2)}, u32[]{:S(2)}) collective-permute-start(f32[64,256]{1,0:T(8,128)S(1)} %broadcast_select_fusion.2), channel_id=1, source_target_pairs={{0,32},{32,64},{64,96},{96,128},{128,160},{160,192},{192,224},{224... | collective-permute-start | bytes 196616 | tf_op jit(solution)/shard_map/ppermute | solution.py:25
  127.1 3.3 %collective-permute-start.2 = (f32[64,256]{1,0:T(8,128)S(1)}, f32[64,256]{1,0:T(8,128)S(1)}, u32[]{:S(2)}, u32[]{:S(2)}) collective-permute-start(f32[64,256]{1,0:T(8,128)S(1)} %broadcast_select_fusion.2), channel_id=1, source_target_pairs={{0,64},{32,96},{64,128},{96,160},{128,192},{160,224},{192,256},{22... | collective-permute-start | bytes 196616 | tf_op jit(solution)/shard_map/ppermute | solution.py:25
  130.4 3.3 %collective-permute-start.1 = (f32[64,256]{1,0:T(8,128)S(1)}, f32[64,256]{1,0:T(8,128)S(1)}, u32[]{:S(2)}, u32[]{:S(2)}) collective-permute-start(f32[64,256]{1,0:T(8,128)S(1)} %broadcast_select_fusion.2), channel_id=1, source_target_pairs={{0,96},{32,128},{64,160},{96,192},{128,224},{160,256},{192,288},{2... | collective-permute-start | bytes 196616 | tf_op jit(solution)/shard_map/ppermute | solution.py:25
  133.7 3.2 %gather_fusion.4 = f32[128,256]{1,0:T(8,128)S(1)} fusion(f32[5120,256]{1,0:T(8,128)} %all-gather.2.cloned.1.call-done, s32[1024]{0:T(1024)S(1)} %pad_clamp_fusion.1), kind=kCustom, calls=%fused_computation.4 | custom fusion | bytes 262656 | tf_op jit(solution)/shard_map/jit(_take)/gather | solution.py:85
  137.0 0.1 broadcast_select_fusion.1
  137.0 3.4 %collective-permute-start = (f32[128,256]{1,0:T(8,128)S(1)}, f32[128,256]{1,0:T(8,128)S(1)}, u32[]{:S(2)}, u32[]{:S(2)}) collective-permute-start(f32[128,256]{1,0:T(8,128)S(1)} %broadcast_select_fusion.1), channel_id=1, source_target_pairs={{0,0},{1,32},{2,64},{3,96},{4,128},{5,160},{6,192},{7,224},{8,256}... | collective-permute-start | bytes 393224 | tf_op jit(solution)/shard_map/ppermute | solution.py:86
  140.4 18.6 %gather_fusion.2 = f32[4096,256]{1,0:T(8,128)} fusion(f32[5120,256]{1,0:T(8,128)} %all-gather.2.cloned.1.call-done, s32[4096]{0:T(1024)S(1)} %fusion.78), kind=kCustom, calls=%fused_computation.2 | custom fusion | bytes 8404992 | tf_op jit(solution)/shard_map/jit(_take)/gather | solution.py:78
  159.0 0.1 select_select_fusion
  159.1 5.3 %collective-permute-start.6 = (f32[64,256]{1,0:T(8,128)S(1)}, f32[64,256]{1,0:T(8,128)S(1)}, u32[]{:S(2)}, u32[]{:S(2)}) collective-permute-start(f32[64,256]{1,0:T(8,128)S(1)} %select_select_fusion), channel_id=1, source_target_pairs={{0,128},{32,160},{64,192},{96,224},{128,256},{160,288},{192,320},{... | collective-permute-start | bytes 196616 | tf_op jit(solution)/shard_map/ppermute | solution.py:25
  164.4 4.9 %collective-permute-start.5 = (f32[64,256]{1,0:T(8,128)S(1)}, f32[64,256]{1,0:T(8,128)S(1)}, u32[]{:S(2)}, u32[]{:S(2)}) collective-permute-start(f32[64,256]{1,0:T(8,128)S(1)} %select_select_fusion), channel_id=1, source_target_pairs={{0,256},{32,288},{64,320},{96,352},{128,384},{160,416},{192,448},{... | collective-permute-start | bytes 196616 | tf_op jit(solution)/shard_map/ppermute | solution.py:25
  169.3 4.1 %collective-permute-start.4 = (f32[64,256]{1,0:T(8,128)S(1)}, f32[64,256]{1,0:T(8,128)S(1)}, u32[]{:S(2)}, u32[]{:S(2)}) collective-permute-start(f32[64,256]{1,0:T(8,128)S(1)} %select_select_fusion), channel_id=1, source_target_pairs={{0,384},{32,416},{64,448},{96,480},{128,0},{160,32},{192,64},{224,... | collective-permute-start | bytes 196616 | tf_op jit(solution)/shard_map/ppermute | solution.py:25
  173.4 2.9 %multiply_reduce_fusion = f32[4096]{0:T(1024)S(1)} fusion(f32[4096,256]{1,0:T(8,128)} %gather_fusion.2, f32[256]{0:T(256)S(1)} %broadcast_divide_fusion, pred[4096]{0:T(1024)(128)(4,1)S(1)} %get-tuple-element.6), kind=kLoop, calls=%fused_computation.12 | loop fusion | flops 4190208 | bytes 4215808 | tf_op jit(solution)/shard_map/reduce_sum | solution.py:43
  176.3 0.6 collective-permute-done.4
  176.9 0.1 multiply_reduce_fusion.2
  177.0 0.2 fusion.96
  177.2 0.1 copy.24
  177.3 0.1 copy.25
  177.4 0.1 copy.22
  177.5 0.1 add_multiply_fusion
  177.6 5.8 %cholesky.15 = f32[64,64]{1,0:T(8,128)S(1)} custom-call(f32[64,64]{1,0:T(8,128)S(1)} %add_multiply_fusion), custom_call_target="Cholesky" | custom-call | tf_op jit(solution)/shard_map/jit(cholesky)/cholesky | solution.py:99
  183.5 0.6 compare_reduce_fusion
  184.1 0.7 fusion.32
  184.8 4.9 %custom-call.8 = f32[1,64,64]{1,2,0:T(8,128)S(1)} custom-call(f32[1,64,64]{2,1,0:T(8,128)S(1)} %fusion.32), custom_call_target="InvertDiagBlocksLowerTriangular" | custom-call | tf_op jit(solution)/shard_map/triangular_solve | solution.py:56
  189.7 6.6 %fusion.1 = f32[4096,64]{0,1:T(8,128)S(1)} fusion(f32[64,256]{1,0:T(8,128)S(1)} %get-tuple-element.5, f32[4096,256]{1,0:T(8,128)} %gather_fusion.2, f32[256]{0:T(256)S(1)} %broadcast_divide_fusion, pred[4096]{0:T(1024)(128)(4,1)S(1)} %get-tuple-element.6, f32[64]{0:T(128)S(1)} %get-tuple-element.4, f32[4096]{0:T(1024)S(1)} %multiply_reduce_fusion), kind=kOutput, calls=%fused_computation.11 | convolution fusion | flops 808452096 | bytes 5330176 | tf_op jit(solution)/shard_map/dot_general | solution.py:45
  196.3 1.7 fusion.8
  198.0 0.1 multiply_reduce_fusion.1
  198.1 0.3 convolution_multiply_fusion.2
  198.4 0.3 fusion.33
  198.7 3.5 %convolution_multiply_fusion = f32[4096,128]{1,0:T(8,128)S(1)} fusion(f32[4096,256]{1,0:T(8,128)S(1)} %copy-done.1, f32[256]{0:T(256)S(1)} %broadcast_divide_fusion, pred[4096]{0:T(1024)(128)(4,1)S(1)} %get-tuple-element.6, f32[128,256]{1,0:T(8,128)S(1)} %collective-permute-done), kind=kOutput, calls=%fused_computation.8 | convolution fusion | flops 1613266944 | bytes 6427648 | tf_op jit(solution)/shard_map/dot_general | solution.py:45
  202.2 6.1 %convolution_subtract_fusion = f32[4096,128]{1,0:T(8,128)} fusion(f32[4096,64]{0,1:T(8,128)S(1)} %fusion.8, f32[128,64]{0,1:T(8,128)S(1)} %fusion.33, f32[4096,128]{1,0:T(8,128)S(1)} %convolution_multiply_fusion, s32[128]{0:T(128)S(1)} %add.442, f32[128]{0:T(128)S(1)} %multiply_reduce_fusion.1, f32[4096]{0:T(1024)S(1)} %multiply_reduce_fusion, ...), kind=kOutput, calls=%fused_computation.7 | convolution fusion | flops 409468928 | bytes 5309440 | tf_op jit(solution)/shard_map/dot_general | solution.py:102
  (42 shorter events, 0.5 us)
Async XLA Ops:
  7.2 17.5 %copy-start = (f32[256,256]{1,0:T(8,128)S(1)}, f32[256,256]{1,0:T(8,128)}, u32[]{:S(2)}) copy-start(f32[256,256]{1,0:T(8,128)} %param.4) | copy-start | bytes 786436
  7.2 111.8 %all-gather.2.cloned.1.call-start = ((), (), s32[]{:S(2)}) async-start(), calls=%async_computation | async-start | bytes 5406720 | tf_op jit(solution)/shard_map/all_gather | solution.py:75
  27.5 25.2 %copy-start.2 = (f32[256]{0:T(256)S(1)}, f32[256]{0:T(256)}, u32[]{:S(2)}) copy-start(f32[256]{0:T(256)} %param.6) | copy-start | bytes 3076
  122.2 36.8 %collective-permute-start.3 = (f32[64,256]{1,0:T(8,128)S(1)}, f32[64,256]{1,0:T(8,128)S(1)}, u32[]{:S(2)}, u32[]{:S(2)}) collective-permute-start(f32[64,256]{1,0:T(8,128)S(1)} %broadcast_select_fusion.2), channel_id=1, source_target_pairs={{0,32},{32,64},{64,96},{96,128},{128,160},{160,192},{192,224},{224... | collective-permute-start | bytes 196616 | tf_op jit(solution)/shard_map/ppermute | solution.py:25
  127.1 31.8 %collective-permute-start.2 = (f32[64,256]{1,0:T(8,128)S(1)}, f32[64,256]{1,0:T(8,128)S(1)}, u32[]{:S(2)}, u32[]{:S(2)}) collective-permute-start(f32[64,256]{1,0:T(8,128)S(1)} %broadcast_select_fusion.2), channel_id=1, source_target_pairs={{0,64},{32,96},{64,128},{96,160},{128,192},{160,224},{192,256},{22... | collective-permute-start | bytes 196616 | tf_op jit(solution)/shard_map/ppermute | solution.py:25
  130.4 28.6 %collective-permute-start.1 = (f32[64,256]{1,0:T(8,128)S(1)}, f32[64,256]{1,0:T(8,128)S(1)}, u32[]{:S(2)}, u32[]{:S(2)}) collective-permute-start(f32[64,256]{1,0:T(8,128)S(1)} %broadcast_select_fusion.2), channel_id=1, source_target_pairs={{0,96},{32,128},{64,160},{96,192},{128,224},{160,256},{192,288},{2... | collective-permute-start | bytes 196616 | tf_op jit(solution)/shard_map/ppermute | solution.py:25
  137.0 61.0 %collective-permute-start = (f32[128,256]{1,0:T(8,128)S(1)}, f32[128,256]{1,0:T(8,128)S(1)}, u32[]{:S(2)}, u32[]{:S(2)}) collective-permute-start(f32[128,256]{1,0:T(8,128)S(1)} %broadcast_select_fusion.1), channel_id=1, source_target_pairs={{0,0},{1,32},{2,64},{3,96},{4,128},{5,160},{6,192},{7,224},{8,256}... | collective-permute-start | bytes 393224 | tf_op jit(solution)/shard_map/ppermute | solution.py:86
  159.1 17.2 %collective-permute-start.6 = (f32[64,256]{1,0:T(8,128)S(1)}, f32[64,256]{1,0:T(8,128)S(1)}, u32[]{:S(2)}, u32[]{:S(2)}) collective-permute-start(f32[64,256]{1,0:T(8,128)S(1)} %select_select_fusion), channel_id=1, source_target_pairs={{0,128},{32,160},{64,192},{96,224},{128,256},{160,288},{192,320},{... | collective-permute-start | bytes 196616 | tf_op jit(solution)/shard_map/ppermute | solution.py:25
  164.4 11.9 %collective-permute-start.5 = (f32[64,256]{1,0:T(8,128)S(1)}, f32[64,256]{1,0:T(8,128)S(1)}, u32[]{:S(2)}, u32[]{:S(2)}) collective-permute-start(f32[64,256]{1,0:T(8,128)S(1)} %select_select_fusion), channel_id=1, source_target_pairs={{0,256},{32,288},{64,320},{96,352},{128,384},{160,416},{192,448},{... | collective-permute-start | bytes 196616 | tf_op jit(solution)/shard_map/ppermute | solution.py:25
  169.3 7.6 %collective-permute-start.4 = (f32[64,256]{1,0:T(8,128)S(1)}, f32[64,256]{1,0:T(8,128)S(1)}, u32[]{:S(2)}, u32[]{:S(2)}) collective-permute-start(f32[64,256]{1,0:T(8,128)S(1)} %select_select_fusion), channel_id=1, source_target_pairs={{0,384},{32,416},{64,448},{96,480},{128,0},{160,32},{192,64},{224,... | collective-permute-start | bytes 196616 | tf_op jit(solution)/shard_map/ppermute | solution.py:25
  189.7 9.0 %copy-start.1 = (f32[4096,256]{1,0:T(8,128)S(1)}, f32[4096,256]{1,0:T(8,128)}, u32[]{:S(2)}) copy-start(f32[4096,256]{1,0:T(8,128)} %gather_fusion.2) | copy-start | bytes 12582916
  198.0 4.2 %copy-start.3 = (f32[4096,64]{0,1:T(8,128)}, f32[4096,64]{0,1:T(8,128)S(1)}, u32[]{:S(2)}) copy-start(f32[4096,64]{0,1:T(8,128)S(1)} %fusion.8) | copy-start | bytes 3145732
Sparse Core Ops, SparseCore 0:
  26.4 92.5 all-gather.1

commit v3 on v2

--- a/solution.py
+++ b/solution.py
@@ -66,15 +66,19 @@
     my_pick = lax.dynamic_slice_in_dim(row_pick, my_row * local_rows, local_rows)
     pool_rows = pool.shape[0]
     group_pixels = pool_rows * cols_count
-    picked = jnp.zeros((group_pixels,), jnp.int32).at[my_pick].set(1, unique_indices=True)
-    counts = jnp.cumsum(picked.reshape(cols_count, pool_rows), axis=1)
+    owner = my_pick // pool_rows
+    owner_hot = (owner[:, None] == jnp.arange(cols_count)[None, :]).astype(jnp.bfloat16)
+    pixel_hot = (my_pick[:, None] % pool_rows == jnp.arange(pool_rows)[None, :]).astype(jnp.bfloat16)
+    picked = jnp.dot(owner_hot.T, pixel_hot, preferred_element_type=jnp.float32)
+    counts = jnp.cumsum(picked, axis=1)
     mine = lax.dynamic_index_in_dim(counts, my_col, axis=0, keepdims=False)
-    slots = jnp.arange(CAP, dtype=jnp.int32)
+    slots = jnp.arange(CAP, dtype=jnp.float32)
     local_idx = jnp.sum((mine[None, :] <= slots[:, None]).astype(jnp.int32), axis=1)
     compact = jnp.take(pool, jnp.minimum(local_idx, pool_rows - 1), axis=0)
     gathered = lax.all_gather(compact, "col", axis=0, tiled=True)
-    slot_of = (counts - 1).reshape(-1)
-    pick_idx = my_pick // pool_rows * CAP + jnp.take(slot_of, my_pick)
+    row_counts = jnp.dot(owner_hot, counts.astype(jnp.bfloat16), preferred_element_type=jnp.float32)
+    slot = jnp.sum(row_counts * pixel_hot.astype(jnp.float32), axis=1).astype(jnp.int32) - 1
+    pick_idx = owner * CAP + slot
     features = jnp.take(gathered, pick_idx, axis=0)
     panel = panel_tile[0]
     tiles = panel + 1 + jnp.mod(my_col - panel - 1, cols_count) + cols_count * jnp.arange(WT)
@@ -87,7 +91,9 @@
     panel_row = panel % rows_count
     panel_local = panel // rows_count
     panel_rows = jnp.take(gathered, lax.dynamic_slice_in_dim(pick_idx, panel_local * TB, TB), axis=0)
-    panel_feats = broadcast_rows(panel_rows, panel_row, rows_count)
+    panel_feats = lax.dynamic_index_in_dim(
+        lax.all_gather(panel_rows, "row", axis=0), panel_row, axis=0, keepdims=False
+    )
     inverse_scale = 1.0 / length_scale
     scaled_rows = features * inverse_scale
     scaled_cols = col_feats * inverse_scale

time: 217 us -> 191 us (0.88)
  local copies, waits for them, and re-layouts: 66.3 us -> 27.8 us
  waiting for transfers between devices: 67 us -> 97.2 us
  starting transfers between devices: 29.1 us -> 6.9 us
  matrix products: 18.6 us -> 22.1 us
    ppermute x6 -> x0, starting transfers between devices: 25.7 us -> none  [broadcast_rows(): got = lax.ppermute(x, 'row', perm)]
    gather x1 -> x0, local copies, waits for them, and re-layouts: 23 us -> none  [body(): pick_idx = my_pick // pool_rows * CAP + jnp.take(slot_of, my_pick)]
    all_gather x1, waiting for transfers between devices: 66.3 us -> 89.1 us  [body(): gathered = lax.all_gather(compact, 'col', axis=0, tiled=True)]
    scatter x1 -> x0, local copies, waits for them, and re-layouts: 15.5 us -> none  [body(): jnp.zeros((group_pixels,), jnp.int32).at[my_pick]]
    all_gather x0 -> x1, waiting for transfers between devices: none -> 8.01 us  [body(): lax.all_gather(panel_rows, 'row', axis=0)]
    ppermute x1, starting transfers between devices: 3.35 us -> 6.82 us  [body(): lax.ppermute(col_local, ('row', 'col'), window_perm(rows_count, cols_count))]
  transfers between devices with their start and end apart: 8 -> 3, of which waited for: 2 -> 2; matrix products, arithmetic and copies ran while one was open for 33% -> 17% of each run, Pallas kernels for 0% -> 0%
where the time goes in v3:
time: 191 us; the launch traced here: 190 us
  waiting for transfers between devices  97.2 us (51%)
  local copies, waits for them, and re-layouts  27.8 us (15%)
  matrix products  22.1 us (12%)
  other arithmetic  20.5 us (11%)
  between operations  15.1 us (8%)
  starting transfers between devices  6.9 us (4%)
    all_gather x1, waiting for transfers between devices, body(): gathered = lax.all_gather(compact, 'col', axis=0, tiled=True)  89.1 us
    gather x1, local copies, waits for them, and re-layouts, body(): features = jnp.take(gathered, pick_idx, axis=0)  18.6 us
    dot_general x4, matrix products, kernel(): jnp.dot(left, right.T, precision=lax.Precision.HIGHEST, preferred_element...  12.2 us
    all_gather x1, waiting for transfers between devices, body(): lax.all_gather(panel_rows, 'row', axis=0)  8.01 us
    ppermute x1, starting transfers between devices, body(): lax.ppermute(col_local, ('row', 'col'), window_perm(rows_count, cols_count))  6.82 us
    another operation x3, other arithmetic, body(): jnp.linalg.cholesky(kernel(scaled_panel, scaled_panel, panel_global, pane...  6.52 us
    dot_general x1, matrix products, body(): jnp.dot(row_panel, col_panel.T, precision=lax.Precision.HIGHEST, preferre...  6.04 us
    another operation x2, other arithmetic, panel_solve(): lax.linalg.triangular_solve(factor, block, left_side=False, lower=True, t...  5.55 us
  transfers between devices with their start and end apart: 3, of which 2 were waited for; matrix products, arithmetic and copies ran while one was open for 17% of the time, Pallas kernels for 0%

profile of v3, /device:TPU:1, one launch (start us, length us, event | category | flops | bytes accessed | tf_op | source)
XLA Modules:
  0.0 189.6 jit_solution(4491112763661043613)
XLA Ops:
  7.2 0.0 all-gather.3.cloned.1.call-start
  7.2 0.8 add_select_fusion.2
  8.0 0.7 add_select_fusion.1
  8.7 0.8 fusion.12
  9.6 0.6 reduce-window.6
  10.2 0.2 slice_reduce_fusion
  10.4 0.1 copy_bitcast_fusion
  10.5 0.1 convert_reduce_fusion
  10.6 0.8 gather_fusion
  11.5 0.8 broadcast_select_fusion
  12.2 0.0 all-gather.3.cloned.1.call-update
  12.3 0.0 all-gather.5.cloned.1.call-start
  13.1 0.1 iota_add_fusion.1
  13.1 0.1 add.414
  13.2 0.1 add.411
  13.3 0.1 iota_add_fusion
  13.4 0.1 add.437
  13.5 1.1 fusion.11
  14.6 1.1 gather_fusion.2
  15.7 0.1 compare_and_fusion.1
  15.8 89.1 %all-gather.3.cloned.1.call-done = f32[5120,256]{1,0:T(8,128)} async-done(((f32[160,256]{1,0:T(8,128)}), f32[5120,256]{1,0:T(8,128)}) %all-gather.3.cloned.1.call-update) | async-done | bytes 5242896 | tf_op jit(solution)/shard_map/all_gather | solution.py:78
  105.0 3.1 %gather_fusion.4 = f32[64,256]{1,0:T(8,128)S(1)} fusion(f32[5120,256]{1,0:T(8,128)} %all-gather.3.cloned.1.call-done, s32[1024]{0:T(1024)S(1)} %pad_clamp_fusion), kind=kCustom, calls=%fused_computation.4 | custom fusion | bytes 131328 | tf_op jit(solution)/shard_map/jit(_take)/gather | solution.py:93
  108.1 0.7 bitcast_select_fusion
  108.8 0.0 all-gather.5.cloned.1.call-update
  108.9 3.2 %gather_fusion.3 = f32[128,256]{1,0:T(8,128)S(1)} fusion(f32[5120,256]{1,0:T(8,128)} %all-gather.3.cloned.1.call-done, s32[1024]{0:T(1024)S(1)} %pad_clamp_fusion.1), kind=kCustom, calls=%fused_computation.3 | custom fusion | bytes 262656 | tf_op jit(solution)/shard_map/jit(_take)/gather | solution.py:89
  112.2 0.1 broadcast_select_fusion.1
  112.3 6.8 %collective-permute-start = (f32[128,256]{1,0:T(8,128)S(1)}, f32[128,256]{1,0:T(8,128)S(1)}, u32[]{:S(2)}, u32[]{:S(2)}) collective-permute-start(f32[128,256]{1,0:T(8,128)S(1)} %broadcast_select_fusion.1), channel_id=1, source_target_pairs={{0,0},{1,32},{2,64},{3,96},{4,128},{5,160},{6,192},{7,224},{8,256}... | collective-permute-start | bytes 393224 | tf_op jit(solution)/shard_map/ppermute | solution.py:90
  119.1 18.6 %gather_fusion.1 = f32[4096,256]{1,0:T(8,128)} fusion(f32[5120,256]{1,0:T(8,128)} %all-gather.3.cloned.1.call-done, s32[4096]{0:T(1024)S(1)} %fusion.87), kind=kCustom, calls=%fused_computation.1 | custom fusion | bytes 8404992 | tf_op jit(solution)/shard_map/jit(_take)/gather | solution.py:82
  137.7 3.1 %multiply_reduce_fusion = f32[4096]{0:T(1024)S(1)} fusion(f32[4096,256]{1,0:T(8,128)} %gather_fusion.1, f32[256]{0:T(256)S(1)} %broadcast_divide_fusion, pred[4096]{0:T(1024)(128)(4,1)S(1)} %get-tuple-element.6), kind=kLoop, calls=%fused_computation.11 | loop fusion | flops 4190208 | bytes 4215808 | tf_op jit(solution)/shard_map/reduce_sum | solution.py:43
  140.8 0.1 multiply_reduce_fusion.1
  140.9 0.2 copy-done.1
  141.1 3.5 %convolution_multiply_fusion.1 = f32[4096,128]{1,0:T(8,128)S(1)} fusion(f32[4096,256]{1,0:T(8,128)S(1)} %copy-done.1, f32[256]{0:T(256)S(1)} %broadcast_divide_fusion, pred[4096]{0:T(1024)(128)(4,1)S(1)} %get-tuple-element.6, f32[128,256]{1,0:T(8,128)S(1)} %collective-permute-done), kind=kOutput, calls=%fused_computation.7 | convolution fusion | flops 1613266944 | bytes 6427648 | tf_op jit(solution)/shard_map/dot_general | solution.py:45
  144.6 8.0 %all-gather.5.cloned.1.call-done = f32[16,64,256]{2,1,0:T(8,128)} async-done(((f32[1,64,256]{2,1,0:T(8,128)}), f32[16,64,256]{2,1,0:T(8,128)}) %all-gather.5.cloned.1.call-update) | async-done | bytes 1048592 | tf_op jit(solution)/shard_map/all_gather | solution.py:95
  152.6 0.9 multiply_reduce_fusion.2
  153.6 1.1 fusion.109
  154.7 0.1 copy.30
  154.8 0.1 copy.31
  154.9 0.1 copy.28
  155.0 0.1 add_multiply_fusion
  155.1 5.8 %cholesky.15 = f32[64,64]{1,0:T(8,128)S(1)} custom-call(f32[64,64]{1,0:T(8,128)S(1)} %add_multiply_fusion), custom_call_target="Cholesky" | custom-call | tf_op jit(solution)/shard_map/jit(cholesky)/cholesky | solution.py:105
  160.9 0.6 compare_reduce_fusion
  161.6 0.7 fusion.42
  162.2 4.9 %custom-call.8 = f32[1,64,64]{1,2,0:T(8,128)S(1)} custom-call(f32[1,64,64]{2,1,0:T(8,128)S(1)} %fusion.42), custom_call_target="InvertDiagBlocksLowerTriangular" | custom-call | tf_op jit(solution)/shard_map/triangular_solve | solution.py:56
  167.1 6.4 %fusion.1 = f32[4096,64]{0,1:T(8,128)S(1)} fusion(f32[4096,256]{1,0:T(8,128)} %gather_fusion.1, f32[256]{0:T(256)S(1)} %broadcast_divide_fusion, pred[4096]{0:T(1024)(128)(4,1)S(1)} %get-tuple-element.6, f32[64]{0:T(128)S(1)} %multiply_reduce_fusion.2, f32[4096]{0:T(1024)S(1)} %multiply_reduce_fusion, f32[16,64,256]{2,1,0:T(8,128)} %all-gather.5.cloned.1.call-done, ...), kind=kOutput, calls=%fused_computation.10 | convolution fusion | flops 808468480 | bytes 5331460 | tf_op jit(solution)/shard_map/dot_general | solution.py:45
  173.5 1.7 fusion.13
  175.3 1.2 convolution_multiply_fusion.3
  176.4 0.3 fusion.43
  176.7 6.0 %convolution_subtract_fusion = f32[4096,128]{1,0:T(8,128)} fusion(f32[4096,64]{0,1:T(8,128)S(1)} %fusion.13, f32[128,64]{0,1:T(8,128)S(1)} %fusion.43, f32[4096,128]{1,0:T(8,128)S(1)} %convolution_multiply_fusion.1, s32[128]{0:T(128)S(1)} %add.437, f32[128]{0:T(128)S(1)} %multiply_reduce_fusion.1, f32[4096]{0:T(1024)S(1)} %multiply_reduce_fusion, ...), kind=kOutput, calls=%fused_computation.6 | convolution fusion | flops 409468928 | bytes 5309440 | tf_op jit(solution)/shard_map/dot_general | solution.py:108
  (30 shorter events, 0.2 us)
Async XLA Ops:
  7.2 3.5 %copy-start = (f32[256,256]{1,0:T(8,128)S(1)}, f32[256,256]{1,0:T(8,128)}, u32[]{:S(2)}) copy-start(f32[256,256]{1,0:T(8,128)} %param.4) | copy-start | bytes 786436
  7.2 97.8 %all-gather.3.cloned.1.call-start = ((), (), s32[]{:S(2)}) async-start(), calls=%async_computation | async-start | bytes 5406720 | tf_op jit(solution)/shard_map/all_gather | solution.py:78
  7.2 101.7 %copy-start.2 = (f32[256]{0:T(256)S(1)}, f32[256]{0:T(256)}, u32[]{:S(2)}) copy-start(f32[256]{0:T(256)} %param.6) | copy-start | bytes 3076
  12.3 140.4 %all-gather.5.cloned.1.call-start = ((), (), s32[]{:S(2)}) async-start(), calls=%async_computation.1 | async-start | bytes 1114112 | tf_op jit(solution)/shard_map/all_gather | solution.py:95
  112.3 28.5 %collective-permute-start = (f32[128,256]{1,0:T(8,128)S(1)}, f32[128,256]{1,0:T(8,128)S(1)}, u32[]{:S(2)}, u32[]{:S(2)}) collective-permute-start(f32[128,256]{1,0:T(8,128)S(1)} %broadcast_select_fusion.1), channel_id=1, source_target_pairs={{0,0},{1,32},{2,64},{3,96},{4,128},{5,160},{6,192},{7,224},{8,256}... | collective-permute-start | bytes 393224 | tf_op jit(solution)/shard_map/ppermute | solution.py:90
  137.7 3.4 %copy-start.1 = (f32[4096,256]{1,0:T(8,128)S(1)}, f32[4096,256]{1,0:T(8,128)}, u32[]{:S(2)}) copy-start(f32[4096,256]{1,0:T(8,128)} %gather_fusion.1) | copy-start | bytes 12582916
  175.3 7.5 %copy-start.3 = (f32[4096,64]{0,1:T(8,128)}, f32[4096,64]{0,1:T(8,128)S(1)}, u32[]{:S(2)}) copy-start(f32[4096,64]{0,1:T(8,128)S(1)} %fusion.13) | copy-start | bytes 3145732
Sparse Core Ops, SparseCore 0:
  12.4 92.5 all-gather.2
  109.0 43.6 all-gather.4

commit v4 on v3

--- a/solution.py
+++ b/solution.py
@@ -27,6 +27,41 @@
         x = new
         step *= radix
     return x
+
+
+def shift_perm(cols_count, span, stride, shift):
+    pairs = []
+    for c in range(cols_count):
+        pos = c // stride % span
+        dst = c + ((pos + shift) % span - pos) * stride
+        pairs.append((c, dst))
+    return pairs
+
+
+def ring_gather(x, cols_count, span, stride):
+    fwd_perm = shift_perm(cols_count, span, stride, 1)
+    bwd_perm = shift_perm(cols_count, span, stride, -1)
+    blocks = [x]
+    fwd, bwd = x, x
+    for _ in range(span // 2 - 1):
+        fwd = lax.ppermute(fwd, "col", fwd_perm)
+        bwd = lax.ppermute(bwd, "col", bwd_perm)
+        blocks += [fwd, bwd]
+    half = x.shape[0] // 2
+    last_fwd = lax.ppermute(fwd[:half], "col", fwd_perm)
+    last_bwd = lax.ppermute(bwd[half:], "col", bwd_perm)
+    blocks.append(jnp.concatenate([last_fwd, last_bwd], axis=0))
+    return jnp.concatenate(blocks, axis=0)
+
+
+def ring_order(span):
+    order = [0] * span
+    order[0] = 0
+    for s in range(1, span // 2):
+        order[(-s) % span] = 2 * s - 1
+        order[s % span] = 2 * s
+    order[span // 2] = span - 1
+    return order
 
 
 def window_perm(rows_count, cols_count):
@@ -75,10 +110,23 @@
     slots = jnp.arange(CAP, dtype=jnp.float32)
     local_idx = jnp.sum((mine[None, :] <= slots[:, None]).astype(jnp.int32), axis=1)
     compact = jnp.take(pool, jnp.minimum(local_idx, pool_rows - 1), axis=0)
-    gathered = lax.all_gather(compact, "col", axis=0, tiled=True)
+    span_y = 8 if cols_count % 8 == 0 else cols_count
+    span_x = cols_count // span_y
+    half = CAP // 2
+    part_a = ring_gather(ring_gather(compact[:half], cols_count, span_y, 1), cols_count, span_x, span_y)
+    part_b = ring_gather(ring_gather(compact[half:], cols_count, span_x, span_y), cols_count, span_y, 1)
+    gathered = jnp.concatenate([part_a, part_b], axis=0)
     row_counts = jnp.dot(owner_hot, counts.astype(jnp.bfloat16), preferred_element_type=jnp.float32)
     slot = jnp.sum(row_counts * pixel_hot.astype(jnp.float32), axis=1).astype(jnp.int32) - 1
-    pick_idx = owner * CAP + slot
+    order_y = jnp.array(ring_order(span_y), jnp.int32)
+    order_x = jnp.array(ring_order(span_x), jnp.int32)
+    ky = jnp.take(order_y, jnp.mod(owner % span_y - my_col % span_y, span_y))
+    kx = jnp.take(order_x, jnp.mod(owner // span_y - my_col // span_y, span_x))
+    pick_idx = jnp.where(
+        slot < half,
+        (kx * span_y + ky) * half + slot,
+        cols_count * half + (ky * span_x + kx) * half + slot - half,
+    )
     features = jnp.take(gathered, pick_idx, axis=0)
     panel = panel_tile[0]
     tiles = panel + 1 + jnp.mod(my_col - panel - 1, cols_count) + cols_count * jnp.arange(WT)
@@ -91,9 +139,7 @@
     panel_row = panel % rows_count
     panel_local = panel // rows_count
     panel_rows = jnp.take(gathered, lax.dynamic_slice_in_dim(pick_idx, panel_local * TB, TB), axis=0)
-    panel_feats = lax.dynamic_index_in_dim(
-        lax.all_gather(panel_rows, "row", axis=0), panel_row, axis=0, keepdims=False
-    )
+    panel_feats = broadcast_rows(panel_rows, panel_row, rows_count)
     inverse_scale = 1.0 / length_scale
     scaled_rows = features * inverse_scale
     scaled_cols = col_feats * inverse_scale

time: 191 us -> 232 us (1.21)
  the two profiles are of different devices: /device:TPU:1 before, /device:TPU:2 now
where the time goes in v4:
time: 232 us; the launch traced here: 231 us
  starting transfers between devices  121 us (52%)
  local copies, waits for them, and re-layouts  45.8 us (20%)
  waiting for transfers between devices  23.2 us (10%)
  matrix products  20.6 us (9%)
  other arithmetic  18.3 us (8%)
    ppermute x8, starting transfers between devices, ring_gather(): bwd = lax.ppermute(bwd, 'col', bwd_perm)  39.8 us
    ppermute x6, starting transfers between devices, broadcast_rows(): got = lax.ppermute(x, 'row', perm)  23.8 us
    gather x1, local copies, waits for them, and re-layouts, body(): features = jnp.take(gathered, pick_idx, axis=0)  18.7 us
    ppermute x8, starting transfers between devices, ring_gather(): fwd = lax.ppermute(fwd, 'col', fwd_perm)  18.4 us
    ppermute x4, starting transfers between devices, ring_gather(): last_bwd = lax.ppermute(bwd[half:], 'col', bwd_perm)  18.2 us
    unnamed x31, local copies, waits for them, and re-layouts  16.1 us
    ppermute x8, waiting for transfers between devices, ring_gather(): fwd = lax.ppermute(fwd, 'col', fwd_perm)  15.7 us
    ppermute x1, starting transfers between devices, body(): lax.ppermute(col_local, ('row', 'col'), window_perm(rows_count, cols_count))  10.7 us
  transfers between devices with their start and end apart: 31, of which 10 were waited for; matrix products, arithmetic and copies ran while one was open for 28% of the time, Pallas kernels for 0%

profile of v4, /device:TPU:2, one launch (start us, length us, event | category | flops | bytes accessed | tf_op | source)
XLA Modules:
  0.0 231.0 jit_solution(14938238382926604150)
XLA Ops:
  5.6 3.5 %collective-permute-start = (f32[80,256]{1,0:T(8,128)S(1)}, f32[80,256]{1,0:T(8,128)S(1)}, u32[]{:S(2)}, u32[]{:S(2)}) collective-permute-start(f32[80,256]{1,0:T(8,128)S(1)} %get-tuple-element.16), channel_id=1, source_target_pairs={{0,1},{1,2},{2,3},{3,4},{4,5},{5,6},{6,7},{7,0},{8,9},{9,10},{10,1... | collective-permute-start | bytes 245768 | tf_op jit(solution)/shard_map/ppermute | solution.py:47
  9.1 3.8 %collective-permute-start.1 = (f32[80,256]{1,0:T(8,128)S(1)}, f32[80,256]{1,0:T(8,128)S(1)}, u32[]{:S(2)}, u32[]{:S(2)}) collective-permute-start(f32[80,256]{1,0:T(8,128)S(1)} %get-tuple-element.16), channel_id=1, source_target_pairs={{0,7},{1,0},{2,1},{3,2},{4,3},{5,4},{6,5},{7,6},{8,15},{9,8},{10,9... | collective-permute-start | bytes 245768 | tf_op jit(solution)/shard_map/ppermute | solution.py:48
  12.9 3.4 %collective-permute-start.12 = (f32[80,256]{1,0:T(8,128)S(1)}, f32[80,256]{1,0:T(8,128)S(1)}, u32[]{:S(2)}, u32[]{:S(2)}) collective-permute-start(f32[80,256]{1,0:T(8,128)S(1)} %get-tuple-element.15), channel_id=1, source_target_pairs={{0,8},{1,9},{2,10},{3,11},{4,12},{5,13},{6,14},{7,15},{8,16},{9,17... | collective-permute-start | bytes 245768 | tf_op jit(solution)/shard_map/ppermute | solution.py:47
  16.4 6.1 %collective-permute-start.13 = (f32[80,256]{1,0:T(8,128)S(1)}, f32[80,256]{1,0:T(8,128)S(1)}, u32[]{:S(2)}, u32[]{:S(2)}) collective-permute-start(f32[80,256]{1,0:T(8,128)S(1)} %get-tuple-element.15), channel_id=1, source_target_pairs={{0,24},{1,25},{2,26},{3,27},{4,28},{5,29},{6,30},{7,31},{8,0},{9,1... | collective-permute-start | bytes 245768 | tf_op jit(solution)/shard_map/ppermute | solution.py:48
  23.1 1.1 fusion.11
  24.8 1.1 gather_fusion.2
  26.0 1.9 collective-permute-start.2
  27.9 5.1 %collective-permute-start.3 = (f32[80,256]{1,0:T(8,128)S(1)}, f32[80,256]{1,0:T(8,128)S(1)}, u32[]{:S(2)}, u32[]{:S(2)}) collective-permute-start(f32[80,256]{1,0:T(8,128)S(1)} %collective-permute-done.1), channel_id=1, source_target_pairs={{0,7},{1,0},{2,1},{3,2},{4,3},{5,4},{6,5},{7,6},{8,15},{9,8},{10,9... | collective-permute-start | bytes 245768 | tf_op jit(solution)/shard_map/ppermute | solution.py:48
  34.3 1.9 collective-permute-start.4
  36.2 5.1 %collective-permute-start.5 = (f32[80,256]{1,0:T(8,128)S(1)}, f32[80,256]{1,0:T(8,128)S(1)}, u32[]{:S(2)}, u32[]{:S(2)}) collective-permute-start(f32[80,256]{1,0:T(8,128)S(1)} %collective-permute-done.3), channel_id=1, source_target_pairs={{0,7},{1,0},{2,1},{3,2},{4,3},{5,4},{6,5},{7,6},{8,15},{9,8},{10,9... | collective-permute-start | bytes 245768 | tf_op jit(solution)/shard_map/ppermute | solution.py:48
  42.7 1.9 collective-permute-start.6
  44.6 5.1 %collective-permute-start.7 = (f32[40,256]{1,0:T(8,128)S(1)}, f32[40,256]{1,0:T(8,128)S(1)}, u32[]{:S(2)}, u32[]{:S(2)}) collective-permute-start(f32[40,256]{1,0:T(8,128)S(1)} %slice.89), channel_id=1, source_target_pairs={{0,7},{1,0},{2,1},{3,2},{4,3},{5,4},{6,5},{7,6},{8,15},{9,8},{10,9... | collective-permute-start | bytes 122888 | tf_op jit(solution)/shard_map/ppermute | solution.py:52
  52.3 1.9 collective-permute-start.8
  54.2 5.1 %collective-permute-start.9 = (f32[640,256]{1,0:T(8,128)S(1)}, f32[640,256]{1,0:T(8,128)S(1)}, u32[]{:S(2)}, u32[]{:S(2)}) collective-permute-start(f32[640,256]{1,0:T(8,128)S(1)} %get-tuple-element.37), channel_id=1, source_target_pairs={{0,24},{1,25},{2,26},{3,27},{4,28},{5,29},{6,30},{7,31},{8,0},{9,1... | collective-permute-start | bytes 1966088 | tf_op jit(solution)/shard_map/ppermute | solution.py:48
  59.5 9.4 %collective-permute-done.8 = f32[640,256]{1,0:T(8,128)S(1)} collective-permute-done((f32[640,256]{1,0:T(8,128)S(1)}, f32[640,256]{1,0:T(8,128)S(1)}, u32[]{:S(2)}, u32[]{:S(2)}) %collective-permute-start.8) | collective-permute-done | bytes 655392 | tf_op jit(solution)/shard_map/ppermute | solution.py:47
  68.9 1.9 collective-permute-start.10
  70.9 4.3 %collective-permute-start.14 = (f32[40,256]{1,0:T(8,128)S(1)}, f32[40,256]{1,0:T(8,128)S(1)}, u32[]{:S(2)}, u32[]{:S(2)}) collective-permute-start(f32[40,256]{1,0:T(8,128)S(1)} %slice.93), channel_id=1, source_target_pairs={{0,8},{1,9},{2,10},{3,11},{4,12},{5,13},{6,14},{7,15},{8,16},{9,17... | collective-permute-start | bytes 122888 | tf_op jit(solution)/shard_map/ppermute | solution.py:51
  75.2 3.0 %collective-permute-start.15 = (f32[40,256]{1,0:T(8,128)S(1)}, f32[40,256]{1,0:T(8,128)S(1)}, u32[]{:S(2)}, u32[]{:S(2)}) collective-permute-start(f32[40,256]{1,0:T(8,128)S(1)} %slice.94), channel_id=1, source_target_pairs={{0,24},{1,25},{2,26},{3,27},{4,28},{5,29},{6,30},{7,31},{8,0},{9,1... | collective-permute-start | bytes 122888 | tf_op jit(solution)/shard_map/ppermute | solution.py:52
  78.3 5.1 %collective-permute-start.11 = (f32[320,256]{1,0:T(8,128)S(1)}, f32[320,256]{1,0:T(8,128)S(1)}, u32[]{:S(2)}, u32[]{:S(2)}) collective-permute-start(f32[320,256]{1,0:T(8,128)S(1)} %slice.91), channel_id=1, source_target_pairs={{0,24},{1,25},{2,26},{3,27},{4,28},{5,29},{6,30},{7,31},{8,0},{9,1... | collective-permute-start | bytes 983048 | tf_op jit(solution)/shard_map/ppermute | solution.py:52
  86.0 2.0 collective-permute-done.11
  91.9 1.9 collective-permute-start.16
  93.8 5.4 %collective-permute-start.17 = (f32[320,256]{1,0:T(8,128)S(1)}, f32[320,256]{1,0:T(8,128)S(1)}, u32[]{:S(2)}, u32[]{:S(2)}) collective-permute-start(f32[320,256]{1,0:T(8,128)S(1)} %get-tuple-element.33), channel_id=1, source_target_pairs={{0,7},{1,0},{2,1},{3,2},{4,3},{5,4},{6,5},{7,6},{8,15},{9,8},{10,9... | collective-permute-start | bytes 983048 | tf_op jit(solution)/shard_map/ppermute | solution.py:48
  99.3 3.1 %collective-permute-done.16 = f32[320,256]{1,0:T(8,128)S(1)} collective-permute-done((f32[320,256]{1,0:T(8,128)S(1)}, f32[320,256]{1,0:T(8,128)S(1)}, u32[]{:S(2)}, u32[]{:S(2)}) %collective-permute-start.16) | collective-permute-done | bytes 327712 | tf_op jit(solution)/shard_map/ppermute | solution.py:47
  102.4 2.0 collective-permute-start.18
  104.9 4.5 %collective-permute-start.19 = (f32[320,256]{1,0:T(8,128)S(1)}, f32[320,256]{1,0:T(8,128)S(1)}, u32[]{:S(2)}, u32[]{:S(2)}) collective-permute-start(f32[320,256]{1,0:T(8,128)S(1)} %collective-permute-done.17), channel_id=1, source_target_pairs={{0,7},{1,0},{2,1},{3,2},{4,3},{5,4},{6,5},{7,6},{8,15},{9,8},{10,9... | collective-permute-start | bytes 983048 | tf_op jit(solution)/shard_map/ppermute | solution.py:48
  110.2 2.3 %collective-permute-done.18 = f32[320,256]{1,0:T(8,128)S(1)} collective-permute-done((f32[320,256]{1,0:T(8,128)S(1)}, f32[320,256]{1,0:T(8,128)S(1)}, u32[]{:S(2)}, u32[]{:S(2)}) %collective-permute-start.18) | collective-permute-done | bytes 327712 | tf_op jit(solution)/shard_map/ppermute | solution.py:47
  112.6 1.9 collective-permute-start.20
  115.1 4.5 %collective-permute-start.21 = (f32[320,256]{1,0:T(8,128)S(1)}, f32[320,256]{1,0:T(8,128)S(1)}, u32[]{:S(2)}, u32[]{:S(2)}) collective-permute-start(f32[320,256]{1,0:T(8,128)S(1)} %collective-permute-done.19), channel_id=1, source_target_pairs={{0,7},{1,0},{2,1},{3,2},{4,3},{5,4},{6,5},{7,6},{8,15},{9,8},{10,9... | collective-permute-start | bytes 983048 | tf_op jit(solution)/shard_map/ppermute | solution.py:48
  122.8 1.9 collective-permute-start.22
  124.9 4.9 %collective-permute-start.23 = (f32[160,256]{1,0:T(8,128)S(1)}, f32[160,256]{1,0:T(8,128)S(1)}, u32[]{:S(2)}, u32[]{:S(2)}) collective-permute-start(f32[160,256]{1,0:T(8,128)S(1)} %slice.96), channel_id=1, source_target_pairs={{0,7},{1,0},{2,1},{3,2},{4,3},{5,4},{6,5},{7,6},{8,15},{9,8},{10,9... | collective-permute-start | bytes 491528 | tf_op jit(solution)/shard_map/ppermute | solution.py:52
  133.4 3.1 %gather_fusion.4 = f32[64,256]{1,0:T(8,128)S(1)} fusion(f32[5120,256]{1,0:T(8,128)} %constant_dynamic-update-slice_fusion.14, s32[1024]{0:T(1024)S(1)} %get-tuple-element.43), kind=kCustom, calls=%fused_computation.4 | custom fusion | bytes 131328 | tf_op jit(solution)/shard_map/jit(_take)/gather | solution.py:141
  136.6 1.9 collective-permute-start.25
  138.5 3.5 %collective-permute-start.26 = (f32[64,256]{1,0:T(8,128)S(1)}, f32[64,256]{1,0:T(8,128)S(1)}, u32[]{:S(2)}, u32[]{:S(2)}) collective-permute-start(f32[64,256]{1,0:T(8,128)S(1)} %broadcast_select_fusion.2), channel_id=1, source_target_pairs={{0,64},{32,96},{64,128},{96,160},{128,192},{160,224},{192,256},{22... | collective-permute-start | bytes 196616 | tf_op jit(solution)/shard_map/ppermute | solution.py:25
  142.1 4.0 %collective-permute-start.27 = (f32[64,256]{1,0:T(8,128)S(1)}, f32[64,256]{1,0:T(8,128)S(1)}, u32[]{:S(2)}, u32[]{:S(2)}) collective-permute-start(f32[64,256]{1,0:T(8,128)S(1)} %broadcast_select_fusion.2), channel_id=1, source_target_pairs={{0,32},{32,64},{64,96},{96,128},{128,160},{160,192},{192,224},{224... | collective-permute-start | bytes 196616 | tf_op jit(solution)/shard_map/ppermute | solution.py:25
  146.1 3.2 %gather_fusion.3 = f32[128,256]{1,0:T(8,128)S(1)} fusion(f32[5120,256]{1,0:T(8,128)} %constant_dynamic-update-slice_fusion.14, s32[1024]{0:T(1024)S(1)} %get-tuple-element.44), kind=kCustom, calls=%fused_computation.3 | custom fusion | bytes 262656 | tf_op jit(solution)/shard_map/jit(_take)/gather | solution.py:137
  149.4 10.7 %collective-permute-start.24 = (f32[128,256]{1,0:T(8,128)S(1)}, f32[128,256]{1,0:T(8,128)S(1)}, u32[]{:S(2)}, u32[]{:S(2)}) collective-permute-start(f32[128,256]{1,0:T(8,128)S(1)} %broadcast_select_fusion.1), channel_id=1, source_target_pairs={{0,0},{1,32},{2,64},{3,96},{4,128},{5,160},{6,192},{7,224},{8,256}... | collective-permute-start | bytes 393224 | tf_op jit(solution)/shard_map/ppermute | solution.py:138
  160.1 18.7 %gather_fusion.1 = f32[4096,256]{1,0:T(8,128)} fusion(f32[5120,256]{1,0:T(8,128)} %constant_dynamic-update-slice_fusion.14, s32[4096]{0:T(1024)S(1)} %fusion.86), kind=kCustom, calls=%fused_computation.1 | custom fusion | bytes 8404992 | tf_op jit(solution)/shard_map/jit(_take)/gather | solution.py:130
  178.9 4.3 %collective-permute-start.28 = (f32[64,256]{1,0:T(8,128)S(1)}, f32[64,256]{1,0:T(8,128)S(1)}, u32[]{:S(2)}, u32[]{:S(2)}) collective-permute-start(f32[64,256]{1,0:T(8,128)S(1)} %select_select_fusion), channel_id=1, source_target_pairs={{0,384},{32,416},{64,448},{96,480},{128,0},{160,32},{192,64},{224,... | collective-permute-start | bytes 196616 | tf_op jit(solution)/shard_map/ppermute | solution.py:25
  183.1 8.0 %collective-permute-start.29 = (f32[64,256]{1,0:T(8,128)S(1)}, f32[64,256]{1,0:T(8,128)S(1)}, u32[]{:S(2)}, u32[]{:S(2)}) collective-permute-start(f32[64,256]{1,0:T(8,128)S(1)} %select_select_fusion), channel_id=1, source_target_pairs={{0,256},{32,288},{64,320},{96,352},{128,384},{160,416},{192,448},{... | collective-permute-start | bytes 196616 | tf_op jit(solution)/shard_map/ppermute | solution.py:25
  191.1 2.1 collective-permute-start.30
  193.3 2.9 %multiply_reduce_fusion = f32[4096]{0:T(1024)S(1)} fusion(f32[4096,256]{1,0:T(8,128)} %gather_fusion.1, f32[256]{0:T(256)S(1)} %broadcast_divide_fusion, pred[4096]{0:T(1024)(128)(4,1)S(1)} %get-tuple-element.6), kind=kLoop, calls=%fused_computation.11 | loop fusion | flops 4190208 | bytes 4215808 | tf_op jit(solution)/shard_map/reduce_sum | solution.py:78
  196.2 3.4 %collective-permute-done.30 = f32[64,256]{1,0:T(8,128)S(1)} collective-permute-done((f32[64,256]{1,0:T(8,128)S(1)}, f32[64,256]{1,0:T(8,128)S(1)}, u32[]{:S(2)}, u32[]{:S(2)}) %collective-permute-start.30) | collective-permute-done | bytes 65568 | tf_op jit(solution)/shard_map/ppermute | solution.py:25
  200.3 5.8 %cholesky.15 = f32[64,64]{1,0:T(8,128)S(1)} custom-call(f32[64,64]{1,0:T(8,128)S(1)} %add_multiply_fusion), custom_call_target="Cholesky" | custom-call | tf_op jit(solution)/shard_map/jit(cholesky)/cholesky | solution.py:151
  207.4 4.9 %custom-call.8 = f32[1,64,64]{1,2,0:T(8,128)S(1)} custom-call(f32[1,64,64]{2,1,0:T(8,128)S(1)} %fusion.39), custom_call_target="InvertDiagBlocksLowerTriangular" | custom-call | tf_op jit(solution)/shard_map/triangular_solve | solution.py:91
  212.4 6.6 %fusion.1 = f32[4096,64]{0,1:T(8,128)S(1)} fusion(f32[64,256]{1,0:T(8,128)S(1)} %get-tuple-element.5, f32[4096,256]{1,0:T(8,128)} %gather_fusion.1, f32[256]{0:T(256)S(1)} %broadcast_divide_fusion, pred[4096]{0:T(1024)(128)(4,1)S(1)} %get-tuple-element.6, f32[64]{0:T(128)S(1)} %get-tuple-element.4, f32[4096]{0:T(1024)S(1)} %multiply_reduce_fusion), kind=kOutput, calls=%fused_computation.10 | convolution fusion | flops 808452096 | bytes 5330176 | tf_op jit(solution)/shard_map/dot_general | solution.py:80
  219.0 1.7 fusion.13
  221.4 3.5 %convolution_multiply_fusion.1 = f32[4096,128]{1,0:T(8,128)S(1)} fusion(f32[4096,256]{1,0:T(8,128)S(1)} %copy-done.1, f32[256]{0:T(256)S(1)} %broadcast_divide_fusion, pred[4096]{0:T(1024)(128)(4,1)S(1)} %get-tuple-element.6, f32[128,256]{1,0:T(8,128)S(1)} %collective-permute-done.24), kind=kOutput, calls=%fused_computation.7 | convolution fusion | flops 1613266944 | bytes 6427648 | tf_op jit(solution)/shard_map/dot_general | solution.py:80
  224.9 6.1 %convolution_subtract_fusion = f32[4096,128]{1,0:T(8,128)} fusion(f32[4096,64]{0,1:T(8,128)S(1)} %fusion.13, f32[128,64]{0,1:T(8,128)S(1)} %fusion.40, f32[4096,128]{1,0:T(8,128)S(1)} %convolution_multiply_fusion.1, s32[128]{0:T(128)S(1)} %add.524, f32[128]{0:T(128)S(1)} %multiply_reduce_fusion.1, f32[4096]{0:T(1024)S(1)} %multiply_reduce_fusion, ...), kind=kOutput, calls=%fused_computation.6 | convolution fusion | flops 409468928 | bytes 5309440 | tf_op jit(solution)/shard_map/dot_general | solution.py:154
  (118 shorter events, 28.9 us)
Async XLA Ops:
  0.6 3.4 %copy-start = (f32[256,256]{1,0:T(8,128)S(1)}, f32[256,256]{1,0:T(8,128)}, u32[]{:S(2)}) copy-start(f32[256,256]{1,0:T(8,128)} %param.6) | copy-start | bytes 786436
  0.6 58.8 %copy-start.2 = (f32[256]{0:T(256)S(1)}, f32[256]{0:T(256)}, u32[]{:S(2)}) copy-start(f32[256]{0:T(256)} %param.8) | copy-start | bytes 3076
  5.6 20.3 %collective-permute-start = (f32[80,256]{1,0:T(8,128)S(1)}, f32[80,256]{1,0:T(8,128)S(1)}, u32[]{:S(2)}, u32[]{:S(2)}) collective-permute-start(f32[80,256]{1,0:T(8,128)S(1)} %get-tuple-element.16), channel_id=1, source_target_pairs={{0,1},{1,2},{2,3},{3,4},{4,5},{5,6},{6,7},{7,0},{8,9},{9,10},{10,1... | collective-permute-start | bytes 245768 | tf_op jit(solution)/shard_map/ppermute | solution.py:47
  9.1 18.8 %collective-permute-start.1 = (f32[80,256]{1,0:T(8,128)S(1)}, f32[80,256]{1,0:T(8,128)S(1)}, u32[]{:S(2)}, u32[]{:S(2)}) collective-permute-start(f32[80,256]{1,0:T(8,128)S(1)} %get-tuple-element.16), channel_id=1, source_target_pairs={{0,7},{1,0},{2,1},{3,2},{4,3},{5,4},{6,5},{7,6},{8,15},{9,8},{10,9... | collective-permute-start | bytes 245768 | tf_op jit(solution)/shard_map/ppermute | solution.py:48
  12.9 57.9 %collective-permute-start.12 = (f32[80,256]{1,0:T(8,128)S(1)}, f32[80,256]{1,0:T(8,128)S(1)}, u32[]{:S(2)}, u32[]{:S(2)}) collective-permute-start(f32[80,256]{1,0:T(8,128)S(1)} %get-tuple-element.15), channel_id=1, source_target_pairs={{0,8},{1,9},{2,10},{3,11},{4,12},{5,13},{6,14},{7,15},{8,16},{9,17... | collective-permute-start | bytes 245768 | tf_op jit(solution)/shard_map/ppermute | solution.py:47
  16.4 58.9 %collective-permute-start.13 = (f32[80,256]{1,0:T(8,128)S(1)}, f32[80,256]{1,0:T(8,128)S(1)}, u32[]{:S(2)}, u32[]{:S(2)}) collective-permute-start(f32[80,256]{1,0:T(8,128)S(1)} %get-tuple-element.15), channel_id=1, source_target_pairs={{0,24},{1,25},{2,26},{3,27},{4,28},{5,29},{6,30},{7,31},{8,0},{9,1... | collective-permute-start | bytes 245768 | tf_op jit(solution)/shard_map/ppermute | solution.py:48
  26.0 8.4 %collective-permute-start.2 = (f32[80,256]{1,0:T(8,128)S(1)}, f32[80,256]{1,0:T(8,128)S(1)}, u32[]{:S(2)}, u32[]{:S(2)}) collective-permute-start(f32[80,256]{1,0:T(8,128)S(1)} %collective-permute-done), channel_id=1, source_target_pairs={{0,1},{1,2},{2,3},{3,4},{4,5},{5,6},{6,7},{7,0},{8,9},{9,10},{10,1... | collective-permute-start | bytes 245768 | tf_op jit(solution)/shard_map/ppermute | solution.py:47
  27.9 8.3 %collective-permute-start.3 = (f32[80,256]{1,0:T(8,128)S(1)}, f32[80,256]{1,0:T(8,128)S(1)}, u32[]{:S(2)}, u32[]{:S(2)}) collective-permute-start(f32[80,256]{1,0:T(8,128)S(1)} %collective-permute-done.1), channel_id=1, source_target_pairs={{0,7},{1,0},{2,1},{3,2},{4,3},{5,4},{6,5},{7,6},{8,15},{9,8},{10,9... | collective-permute-start | bytes 245768 | tf_op jit(solution)/shard_map/ppermute | solution.py:48
  34.3 8.3 %collective-permute-start.4 = (f32[80,256]{1,0:T(8,128)S(1)}, f32[80,256]{1,0:T(8,128)S(1)}, u32[]{:S(2)}, u32[]{:S(2)}) collective-permute-start(f32[80,256]{1,0:T(8,128)S(1)} %collective-permute-done.2), channel_id=1, source_target_pairs={{0,1},{1,2},{2,3},{3,4},{4,5},{5,6},{6,7},{7,0},{8,9},{9,10},{10,1... | collective-permute-start | bytes 245768 | tf_op jit(solution)/shard_map/ppermute | solution.py:47
  36.2 8.3 %collective-permute-start.5 = (f32[80,256]{1,0:T(8,128)S(1)}, f32[80,256]{1,0:T(8,128)S(1)}, u32[]{:S(2)}, u32[]{:S(2)}) collective-permute-start(f32[80,256]{1,0:T(8,128)S(1)} %collective-permute-done.3), channel_id=1, source_target_pairs={{0,7},{1,0},{2,1},{3,2},{4,3},{5,4},{6,5},{7,6},{8,15},{9,8},{10,9... | collective-permute-start | bytes 245768 | tf_op jit(solution)/shard_map/ppermute | solution.py:48
  42.7 8.4 %collective-permute-start.6 = (f32[40,256]{1,0:T(8,128)S(1)}, f32[40,256]{1,0:T(8,128)S(1)}, u32[]{:S(2)}, u32[]{:S(2)}) collective-permute-start(f32[40,256]{1,0:T(8,128)S(1)} %slice.88), channel_id=1, source_target_pairs={{0,1},{1,2},{2,3},{3,4},{4,5},{5,6},{6,7},{7,0},{8,9},{9,10},{10,1... | collective-permute-start | bytes 122888 | tf_op jit(solution)/shard_map/ppermute | solution.py:51
  44.6 7.1 %collective-permute-start.7 = (f32[40,256]{1,0:T(8,128)S(1)}, f32[40,256]{1,0:T(8,128)S(1)}, u32[]{:S(2)}, u32[]{:S(2)}) collective-permute-start(f32[40,256]{1,0:T(8,128)S(1)} %slice.89), channel_id=1, source_target_pairs={{0,7},{1,0},{2,1},{3,2},{4,3},{5,4},{6,5},{7,6},{8,15},{9,8},{10,9... | collective-permute-start | bytes 122888 | tf_op jit(solution)/shard_map/ppermute | solution.py:52
  52.3 16.6 %collective-permute-start.8 = (f32[640,256]{1,0:T(8,128)S(1)}, f32[640,256]{1,0:T(8,128)S(1)}, u32[]{:S(2)}, u32[]{:S(2)}) collective-permute-start(f32[640,256]{1,0:T(8,128)S(1)} %get-tuple-element.37), channel_id=1, source_target_pairs={{0,8},{1,9},{2,10},{3,11},{4,12},{5,13},{6,14},{7,15},{8,16},{9,17... | collective-permute-start | bytes 1966088 | tf_op jit(solution)/shard_map/ppermute | solution.py:47
  54.2 24.1 %collective-permute-start.9 = (f32[640,256]{1,0:T(8,128)S(1)}, f32[640,256]{1,0:T(8,128)S(1)}, u32[]{:S(2)}, u32[]{:S(2)}) collective-permute-start(f32[640,256]{1,0:T(8,128)S(1)} %get-tuple-element.37), channel_id=1, source_target_pairs={{0,24},{1,25},{2,26},{3,27},{4,28},{5,29},{6,30},{7,31},{8,0},{9,1... | collective-permute-start | bytes 1966088 | tf_op jit(solution)/shard_map/ppermute | solution.py:48
  68.9 16.3 %collective-permute-start.10 = (f32[320,256]{1,0:T(8,128)S(1)}, f32[320,256]{1,0:T(8,128)S(1)}, u32[]{:S(2)}, u32[]{:S(2)}) collective-permute-start(f32[320,256]{1,0:T(8,128)S(1)} %slice.90), channel_id=1, source_target_pairs={{0,8},{1,9},{2,10},{3,11},{4,12},{5,13},{6,14},{7,15},{8,16},{9,17... | collective-permute-start | bytes 983048 | tf_op jit(solution)/shard_map/ppermute | solution.py:51
  70.9 19.8 %collective-permute-start.14 = (f32[40,256]{1,0:T(8,128)S(1)}, f32[40,256]{1,0:T(8,128)S(1)}, u32[]{:S(2)}, u32[]{:S(2)}) collective-permute-start(f32[40,256]{1,0:T(8,128)S(1)} %slice.93), channel_id=1, source_target_pairs={{0,8},{1,9},{2,10},{3,11},{4,12},{5,13},{6,14},{7,15},{8,16},{9,17... | collective-permute-start | bytes 122888 | tf_op jit(solution)/shard_map/ppermute | solution.py:51
  75.2 16.1 %collective-permute-start.15 = (f32[40,256]{1,0:T(8,128)S(1)}, f32[40,256]{1,0:T(8,128)S(1)}, u32[]{:S(2)}, u32[]{:S(2)}) collective-permute-start(f32[40,256]{1,0:T(8,128)S(1)} %slice.94), channel_id=1, source_target_pairs={{0,24},{1,25},{2,26},{3,27},{4,28},{5,29},{6,30},{7,31},{8,0},{9,1... | collective-permute-start | bytes 122888 | tf_op jit(solution)/shard_map/ppermute | solution.py:52
  78.3 9.7 %collective-permute-start.11 = (f32[320,256]{1,0:T(8,128)S(1)}, f32[320,256]{1,0:T(8,128)S(1)}, u32[]{:S(2)}, u32[]{:S(2)}) collective-permute-start(f32[320,256]{1,0:T(8,128)S(1)} %slice.91), channel_id=1, source_target_pairs={{0,24},{1,25},{2,26},{3,27},{4,28},{5,29},{6,30},{7,31},{8,0},{9,1... | collective-permute-start | bytes 983048 | tf_op jit(solution)/shard_map/ppermute | solution.py:52
  91.9 10.5 %collective-permute-start.16 = (f32[320,256]{1,0:T(8,128)S(1)}, f32[320,256]{1,0:T(8,128)S(1)}, u32[]{:S(2)}, u32[]{:S(2)}) collective-permute-start(f32[320,256]{1,0:T(8,128)S(1)} %get-tuple-element.33), channel_id=1, source_target_pairs={{0,1},{1,2},{2,3},{3,4},{4,5},{5,6},{6,7},{7,0},{8,9},{9,10},{10,1... | collective-permute-start | bytes 983048 | tf_op jit(solution)/shard_map/ppermute | solution.py:47
  93.8 11.1 %collective-permute-start.17 = (f32[320,256]{1,0:T(8,128)S(1)}, f32[320,256]{1,0:T(8,128)S(1)}, u32[]{:S(2)}, u32[]{:S(2)}) collective-permute-start(f32[320,256]{1,0:T(8,128)S(1)} %get-tuple-element.33), channel_id=1, source_target_pairs={{0,7},{1,0},{2,1},{3,2},{4,3},{5,4},{6,5},{7,6},{8,15},{9,8},{10,9... | collective-permute-start | bytes 983048 | tf_op jit(solution)/shard_map/ppermute | solution.py:48
  102.4 10.2 %collective-permute-start.18 = (f32[320,256]{1,0:T(8,128)S(1)}, f32[320,256]{1,0:T(8,128)S(1)}, u32[]{:S(2)}, u32[]{:S(2)}) collective-permute-start(f32[320,256]{1,0:T(8,128)S(1)} %collective-permute-done.16), channel_id=1, source_target_pairs={{0,1},{1,2},{2,3},{3,4},{4,5},{5,6},{6,7},{7,0},{8,9},{9,10},{10,1... | collective-permute-start | bytes 983048 | tf_op jit(solution)/shard_map/ppermute | solution.py:47
  104.9 10.2 %collective-permute-start.19 = (f32[320,256]{1,0:T(8,128)S(1)}, f32[320,256]{1,0:T(8,128)S(1)}, u32[]{:S(2)}, u32[]{:S(2)}) collective-permute-start(f32[320,256]{1,0:T(8,128)S(1)} %collective-permute-done.17), channel_id=1, source_target_pairs={{0,7},{1,0},{2,1},{3,2},{4,3},{5,4},{6,5},{7,6},{8,15},{9,8},{10,9... | collective-permute-start | bytes 983048 | tf_op jit(solution)/shard_map/ppermute | solution.py:48
  112.6 10.2 %collective-permute-start.20 = (f32[320,256]{1,0:T(8,128)S(1)}, f32[320,256]{1,0:T(8,128)S(1)}, u32[]{:S(2)}, u32[]{:S(2)}) collective-permute-start(f32[320,256]{1,0:T(8,128)S(1)} %collective-permute-done.18), channel_id=1, source_target_pairs={{0,1},{1,2},{2,3},{3,4},{4,5},{5,6},{6,7},{7,0},{8,9},{9,10},{10,1... | collective-permute-start | bytes 983048 | tf_op jit(solution)/shard_map/ppermute | solution.py:47
  115.1 9.8 %collective-permute-start.21 = (f32[320,256]{1,0:T(8,128)S(1)}, f32[320,256]{1,0:T(8,128)S(1)}, u32[]{:S(2)}, u32[]{:S(2)}) collective-permute-start(f32[320,256]{1,0:T(8,128)S(1)} %collective-permute-done.19), channel_id=1, source_target_pairs={{0,7},{1,0},{2,1},{3,2},{4,3},{5,4},{6,5},{7,6},{8,15},{9,8},{10,9... | collective-permute-start | bytes 983048 | tf_op jit(solution)/shard_map/ppermute | solution.py:48
  122.8 8.6 %collective-permute-start.22 = (f32[160,256]{1,0:T(8,128)S(1)}, f32[160,256]{1,0:T(8,128)S(1)}, u32[]{:S(2)}, u32[]{:S(2)}) collective-permute-start(f32[160,256]{1,0:T(8,128)S(1)} %slice.95), channel_id=1, source_target_pairs={{0,1},{1,2},{2,3},{3,4},{4,5},{5,6},{6,7},{7,0},{8,9},{9,10},{10,1... | collective-permute-start | bytes 491528 | tf_op jit(solution)/shard_map/ppermute | solution.py:51
  124.9 7.8 %collective-permute-start.23 = (f32[160,256]{1,0:T(8,128)S(1)}, f32[160,256]{1,0:T(8,128)S(1)}, u32[]{:S(2)}, u32[]{:S(2)}) collective-permute-start(f32[160,256]{1,0:T(8,128)S(1)} %slice.96), channel_id=1, source_target_pairs={{0,7},{1,0},{2,1},{3,2},{4,3},{5,4},{6,5},{7,6},{8,15},{9,8},{10,9... | collective-permute-start | bytes 491528 | tf_op jit(solution)/shard_map/ppermute | solution.py:52
  136.6 42.2 %collective-permute-start.25 = (f32[64,256]{1,0:T(8,128)S(1)}, f32[64,256]{1,0:T(8,128)S(1)}, u32[]{:S(2)}, u32[]{:S(2)}) collective-permute-start(f32[64,256]{1,0:T(8,128)S(1)} %broadcast_select_fusion.2), channel_id=1, source_target_pairs={{0,96},{32,128},{64,160},{96,192},{128,224},{160,256},{192,288},{2... | collective-permute-start | bytes 196616 | tf_op jit(solution)/shard_map/ppermute | solution.py:25
  138.5 40.2 %collective-permute-start.26 = (f32[64,256]{1,0:T(8,128)S(1)}, f32[64,256]{1,0:T(8,128)S(1)}, u32[]{:S(2)}, u32[]{:S(2)}) collective-permute-start(f32[64,256]{1,0:T(8,128)S(1)} %broadcast_select_fusion.2), channel_id=1, source_target_pairs={{0,64},{32,96},{64,128},{96,160},{128,192},{160,224},{192,256},{22... | collective-permute-start | bytes 196616 | tf_op jit(solution)/shard_map/ppermute | solution.py:25
  142.1 36.7 %collective-permute-start.27 = (f32[64,256]{1,0:T(8,128)S(1)}, f32[64,256]{1,0:T(8,128)S(1)}, u32[]{:S(2)}, u32[]{:S(2)}) collective-permute-start(f32[64,256]{1,0:T(8,128)S(1)} %broadcast_select_fusion.2), channel_id=1, source_target_pairs={{0,32},{32,64},{64,96},{96,128},{128,160},{160,192},{192,224},{224... | collective-permute-start | bytes 196616 | tf_op jit(solution)/shard_map/ppermute | solution.py:25
  149.4 71.3 %collective-permute-start.24 = (f32[128,256]{1,0:T(8,128)S(1)}, f32[128,256]{1,0:T(8,128)S(1)}, u32[]{:S(2)}, u32[]{:S(2)}) collective-permute-start(f32[128,256]{1,0:T(8,128)S(1)} %broadcast_select_fusion.1), channel_id=1, source_target_pairs={{0,0},{1,32},{2,64},{3,96},{4,128},{5,160},{6,192},{7,224},{8,256}... | collective-permute-start | bytes 393224 | tf_op jit(solution)/shard_map/ppermute | solution.py:138
  178.9 17.3 %collective-permute-start.28 = (f32[64,256]{1,0:T(8,128)S(1)}, f32[64,256]{1,0:T(8,128)S(1)}, u32[]{:S(2)}, u32[]{:S(2)}) collective-permute-start(f32[64,256]{1,0:T(8,128)S(1)} %select_select_fusion), channel_id=1, source_target_pairs={{0,384},{32,416},{64,448},{96,480},{128,0},{160,32},{192,64},{224,... | collective-permute-start | bytes 196616 | tf_op jit(solution)/shard_map/ppermute | solution.py:25
  183.1 13.0 %collective-permute-start.29 = (f32[64,256]{1,0:T(8,128)S(1)}, f32[64,256]{1,0:T(8,128)S(1)}, u32[]{:S(2)}, u32[]{:S(2)}) collective-permute-start(f32[64,256]{1,0:T(8,128)S(1)} %select_select_fusion), channel_id=1, source_target_pairs={{0,256},{32,288},{64,320},{96,352},{128,384},{160,416},{192,448},{... | collective-permute-start | bytes 196616 | tf_op jit(solution)/shard_map/ppermute | solution.py:25
  191.1 8.4 %collective-permute-start.30 = (f32[64,256]{1,0:T(8,128)S(1)}, f32[64,256]{1,0:T(8,128)S(1)}, u32[]{:S(2)}, u32[]{:S(2)}) collective-permute-start(f32[64,256]{1,0:T(8,128)S(1)} %select_select_fusion), channel_id=1, source_target_pairs={{0,128},{32,160},{64,192},{96,224},{128,256},{160,288},{192,320},{... | collective-permute-start | bytes 196616 | tf_op jit(solution)/shard_map/ppermute | solution.py:25
  212.3 9.1 %copy-start.1 = (f32[4096,256]{1,0:T(8,128)S(1)}, f32[4096,256]{1,0:T(8,128)}, u32[]{:S(2)}) copy-start(f32[4096,256]{1,0:T(8,128)} %gather_fusion.1) | copy-start | bytes 12582916
  220.7 10.3 %copy-start.3 = (f32[4096,64]{0,1:T(8,128)}, f32[4096,64]{0,1:T(8,128)S(1)}, u32[]{:S(2)}) copy-start(f32[4096,64]{0,1:T(8,128)S(1)} %fusion.13) | copy-start | bytes 3145732

commit v5 on v3

--- a/solution.py
+++ b/solution.py
@@ -86,11 +86,16 @@
     served_tiles = panel + 1 + jnp.mod(served - panel - 1, cols_count) + cols_count * jnp.arange(WT)
     local_tiles = served_tiles // rows_count
     col_source = (local_tiles[:, None] * TB + jnp.arange(TB)[None, :]).reshape(-1)
-    col_local = jnp.take(gathered, jnp.take(pick_idx, col_source), axis=0)
-    col_feats = lax.ppermute(col_local, ("row", "col"), window_perm(rows_count, cols_count))
+
     panel_row = panel % rows_count
     panel_local = panel // rows_count
-    panel_rows = jnp.take(gathered, lax.dynamic_slice_in_dim(pick_idx, panel_local * TB, TB), axis=0)
+    both_idx = jnp.concatenate(
+        [lax.dynamic_slice_in_dim(pick_idx, panel_local * TB, TB), jnp.take(pick_idx, col_source)]
+    )
+    both_rows = jnp.take(gathered, both_idx, axis=0)
+    panel_rows = both_rows[:TB]
+    col_local = both_rows[TB:]
+    col_feats = lax.ppermute(col_local, ("row", "col"), window_perm(rows_count, cols_count))
     panel_feats = lax.dynamic_index_in_dim(
         lax.all_gather(panel_rows, "row", axis=0), panel_row, axis=0, keepdims=False
     )
@@ -105,10 +110,11 @@
     factor = jnp.linalg.cholesky(kernel(scaled_panel, scaled_panel, panel_global, panel_global))
     row_panel = panel_solve(factor, kernel(scaled_rows, scaled_panel, row_global, panel_global))
     col_panel = panel_solve(factor, kernel(scaled_cols, scaled_panel, col_global, panel_global))
+    window = lax.optimization_barrier(kernel(scaled_rows, scaled_cols, row_global, col_global))
     update = jnp.dot(
         row_panel, col_panel.T, precision=lax.Precision.HIGHEST, preferred_element_type=jnp.float32
     )
-    schur = kernel(scaled_rows, scaled_cols, row_global, col_global) - update
+    schur = window - update
     return (schur, row_panel)
 
 

time: 191 us -> 201 us (1.052)
  other arithmetic: 20.5 us -> 26.2 us
    gather x3 -> x2, local copies, waits for them, and re-layouts: 7.52 us -> 4.49 us  [the longest x1 3.35 us: body(): both_rows = jnp.take(gathered, both_idx, axis=0)]
    another operation x2, other arithmetic: 5.55 us -> 8.3 us  [panel_solve(): lax.linalg.triangular_solve(factor, block, left_side=False, lower=True, t...]
    another operation x3, other arithmetic: 6.52 us -> 8.65 us  [body(): jnp.linalg.cholesky(kernel(scaled_panel, scaled_panel, panel_global, pane...]
  transfers between devices with their start and end apart: 3 -> 3, of which waited for: 2 -> 2; matrix products, arithmetic and copies ran while one was open for 17% -> 14% of each run, Pallas kernels for 0% -> 0%
where the time goes in v5:
time: 201 us; the launch traced here: 200 us
  waiting for transfers between devices  98.7 us (49%)
  local copies, waits for them, and re-layouts  29.7 us (15%)
  other arithmetic  26.2 us (13%)
  matrix products  24 us (12%)
  between operations  15 us (7%)
  starting transfers between devices  6.72 us (3%)
    all_gather x1, waiting for transfers between devices, body(): gathered = lax.all_gather(compact, 'col', axis=0, tiled=True)  89.1 us
    gather x1, local copies, waits for them, and re-layouts, body(): features = jnp.take(gathered, pick_idx, axis=0)  18.6 us
    dot_general x4, matrix products, kernel(): jnp.dot(left, right.T, precision=lax.Precision.HIGHEST, preferred_element...  13.8 us
    all_gather x1, waiting for transfers between devices, body(): lax.all_gather(panel_rows, 'row', axis=0)  9.54 us
    another operation x3, other arithmetic, body(): jnp.linalg.cholesky(kernel(scaled_panel, scaled_panel, panel_global, pane...  8.65 us
    another operation x2, other arithmetic, panel_solve(): lax.linalg.triangular_solve(factor, block, left_side=False, lower=True, t...  8.3 us
    ppermute x1, starting transfers between devices, body(): lax.ppermute(col_local, ('row', 'col'), window_perm(rows_count, cols_count))  6.64 us
    dot_general x1, matrix products, body(): jnp.dot(row_panel, col_panel.T, precision=lax.Precision.HIGHEST, preferre...  4.8 us
  transfers between devices with their start and end apart: 3, of which 2 were waited for; matrix products, arithmetic and copies ran while one was open for 14% of the time, Pallas kernels for 0%

profile of v5, /device:TPU:1, one launch (start us, length us, event | category | flops | bytes accessed | tf_op | source)
XLA Modules:
  0.0 200.3 jit_solution(1781804803899013215)
XLA Ops:
  7.2 0.8 add_select_fusion.2
  8.0 0.7 add_select_fusion.1
  8.7 0.8 fusion.12
  9.6 0.6 reduce-window.6
  10.1 0.2 slice_reduce_fusion
  10.4 0.1 copy_bitcast_fusion
  10.5 0.1 convert_reduce_fusion
  10.6 0.8 gather_fusion
  11.5 0.8 broadcast_select_fusion.1
  12.2 0.0 all-gather.6.cloned.1.call-start
  13.0 0.1 iota_add_fusion.1
  13.1 0.1 add.419
  13.2 0.1 add.416
  13.3 1.1 fusion.11
  14.4 1.1 gather_fusion.2
  15.5 0.1 dynamic_slice.16
  15.6 0.1 dynamic-slice_bitcast_fusion
  15.7 0.1 compare_and_fusion.1
  15.8 0.1 compare_select_fusion.1
  15.9 89.1 %all-gather.4.cloned.1.call-done = f32[5120,256]{1,0:T(8,128)} async-done(((f32[160,256]{1,0:T(8,128)}), f32[5120,256]{1,0:T(8,128)}) %all-gather.4.cloned.1.call-update) | async-done | bytes 5242896 | tf_op jit(solution)/shard_map/all_gather | solution.py:78
  105.0 3.3 %gather_fusion.3 = f32[192,256]{1,0:T(8,128)S(1)} fusion(f32[5120,256]{1,0:T(8,128)} %all-gather.4.cloned.1.call-done, s32[1024]{0:T(1024)S(1)} %pad_clamp_fusion), kind=kCustom, calls=%fused_computation.3 | custom fusion | bytes 393984 | tf_op jit(solution)/shard_map/jit(_take)/gather | solution.py:95
  108.3 0.1 broadcast_select_fusion
  108.4 0.6 slice.40
  109.1 0.1 iota_add_fusion
  109.2 0.1 add.442
  109.3 6.6 %collective-permute-start = (f32[128,256]{1,0:T(8,128)S(1)}, f32[128,256]{1,0:T(8,128)S(1)}, u32[]{:S(2)}, u32[]{:S(2)}) collective-permute-start(f32[128,256]{1,0:T(8,128)S(1)} %slice.39), channel_id=1, source_target_pairs={{0,0},{1,32},{2,64},{3,96},{4,128},{5,160},{6,192},{7,224},{8,256}... | collective-permute-start | bytes 393224 | tf_op jit(solution)/shard_map/ppermute | solution.py:98
  116.0 18.6 %gather_fusion.1 = f32[4096,256]{1,0:T(8,128)} fusion(f32[5120,256]{1,0:T(8,128)} %all-gather.4.cloned.1.call-done, s32[4096]{0:T(1024)S(1)} %fusion.87), kind=kCustom, calls=%fused_computation.1 | custom fusion | bytes 8404992 | tf_op jit(solution)/shard_map/jit(_take)/gather | solution.py:82
  134.6 3.1 %multiply_reduce_fusion = f32[4096]{0:T(1024)S(1)} fusion(f32[4096,256]{1,0:T(8,128)} %gather_fusion.1, f32[256]{0:T(256)S(1)} %broadcast_divide_fusion, pred[4096]{0:T(1024)(128)(4,1)S(1)} %get-tuple-element.4), kind=kLoop, calls=%fused_computation.10 | loop fusion | flops 4190208 | bytes 4215808 | tf_op jit(solution)/shard_map/reduce_sum | solution.py:43
  137.7 0.1 multiply_reduce_fusion.1
  137.8 0.2 copy-done.1
  138.0 4.2 %select_add_fusion = f32[4096,128]{1,0:T(8,128)S(1)} fusion(f32[4096,256]{1,0:T(8,128)S(1)} %copy-done.1, f32[256]{0:T(256)S(1)} %broadcast_divide_fusion, pred[4096]{0:T(1024)(128)(4,1)S(1)} %get-tuple-element.4, s32[128]{0:T(128)S(1)} %add.442, f32[128]{0:T(128)S(1)} %multiply_reduce_fusion.1, f32[4096]{0:T(1024)S(1)} %multiply_reduce_fusion, ...), kind=kOutput, calls=%fused_computation.15 | convolution fusion | flops 1619558400 | bytes 6461440 | tf_op jit(solution)/shard_map/dot_general | solution.py:45
  142.3 9.5 %all-gather.6.cloned.1.call-done = f32[1024,256]{1,0:T(8,128)} async-done(((f32[64,256]{1,0:T(8,128)}), f32[1024,256]{1,0:T(8,128)}) %all-gather.6.cloned.1.call-update) | async-done | bytes 1048592 | tf_op jit(solution)/shard_map/all_gather | solution.py:100
  151.8 0.9 multiply_reduce_fusion.2
  152.8 6.6 %fusion.1 = f32[4096,64]{0,1:T(8,128)S(1)} fusion(f32[4096,256]{1,0:T(8,128)} %gather_fusion.1, f32[256]{0:T(256)S(1)} %broadcast_divide_fusion, pred[4096]{0:T(1024)(128)(4,1)S(1)} %get-tuple-element.4, f32[64]{0:T(128)S(1)} %multiply_reduce_fusion.2, f32[4096]{0:T(1024)} %copy-done.3, f32[16,64,256]{2,1,0:T(8,128)} %bitcast.61, s32[]{:T(128)S(6)} %select_n.194), kind=kOutput, calls=%fused_computation.9 | convolution fusion | flops 808468480 | bytes 5331460 | tf_op jit(solution)/shard_map/dot_general | solution.py:45
  159.4 1.8 fusion.108
  161.1 1.4 copy.23
  162.6 1.5 copy.24
  164.0 1.5 copy.21
  165.5 1.5 add_multiply_fusion
  167.0 7.2 %cholesky.15 = f32[64,64]{1,0:T(8,128)} custom-call(f32[64,64]{1,0:T(8,128)} %add_multiply_fusion), custom_call_target="Cholesky" | custom-call | tf_op jit(solution)/shard_map/jit(cholesky)/cholesky | solution.py:110
  174.2 0.8 select_reduce_fusion
  175.0 0.6 compare_reduce_fusion
  175.6 2.0 %fusion.42 = f32[1,64,64]{2,1,0:T(8,128)} fusion(f32[64,64]{1,0:T(8,128)} %cholesky.15, pred[]{:T(512)} %compare_reduce_fusion), kind=kLoop, calls=%fused_computation.66 | loop fusion | flops 16384 | bytes 32769 | tf_op jit(solution)/shard_map/triangular_solve | solution.py:56
  177.7 6.3 %custom-call.8 = f32[1,64,64]{1,2,0:T(8,128)} custom-call(f32[1,64,64]{2,1,0:T(8,128)} %fusion.42), custom_call_target="InvertDiagBlocksLowerTriangular" | custom-call | tf_op jit(solution)/shard_map/triangular_solve | solution.py:56
  183.9 2.5 %fusion.13 = f32[4096,64]{0,1:T(8,128)S(1)} fusion(f32[4096,64]{0,1:T(8,128)S(1)} %fusion.1, s32[4096]{0:T(1024)} %copy-done.4, s32[64]{0:T(128)S(1)} %iota_add_fusion.2, f32[1,64,64]{1,2,0:T(8,128)} %custom-call.8), kind=kOutput, calls=%fused_computation.27 | convolution fusion | flops 203685888 | bytes 2130176 | tf_op jit(solution)/shard_map/triangular_solve | solution.py:56
  186.4 1.2 convolution_multiply_fusion.3
  187.6 1.0 fusion.43
  188.6 4.8 %convolution_subtract_fusion = f32[4096,128]{1,0:T(8,128)} fusion(f32[4096,128]{1,0:T(8,128)S(1)} %select_add_fusion, f32[4096,64]{0,1:T(8,128)S(1)} %fusion.13, f32[128,64]{0,1:T(8,128)S(1)} %fusion.43), kind=kOutput, calls=%fused_computation.5 | convolution fusion | flops 403177472 | bytes 5275648 | tf_op jit(solution)/shard_map/dot_general | solution.py:114
  (39 shorter events, 0.3 us)
Async XLA Ops:
  7.2 3.5 %copy-start = (f32[256,256]{1,0:T(8,128)S(1)}, f32[256,256]{1,0:T(8,128)}, u32[]{:S(2)}) copy-start(f32[256,256]{1,0:T(8,128)} %param.4) | copy-start | bytes 786436
  7.2 97.8 %all-gather.4.cloned.1.call-start = ((), (), s32[]{:S(2)}) async-start(), calls=%async_computation | async-start | bytes 5406720 | tf_op jit(solution)/shard_map/all_gather | solution.py:78
  10.3 99.0 %copy-start.5 = (f32[256]{0:T(256)S(1)}, f32[256]{0:T(256)}, u32[]{:S(2)}) copy-start(f32[256]{0:T(256)} %param.6) | copy-start | bytes 3076
  12.2 139.6 %all-gather.6.cloned.1.call-start = ((), (), s32[]{:S(2)}) async-start(), calls=%async_computation.1 | async-start | bytes 1114112 | tf_op jit(solution)/shard_map/all_gather | solution.py:100
  109.3 28.5 %copy-start.7 = (s32[128]{0:T(128)}, s32[128]{0:T(128)S(1)}, u32[]{:S(2)}) copy-start(s32[128]{0:T(128)S(1)} %add.442) | copy-start | bytes 1540
  109.3 28.5 %copy-start.4 = (s32[4096]{0:T(1024)}, s32[4096]{0:T(1024)S(1)}, u32[]{:S(2)}) copy-start(s32[4096]{0:T(1024)S(1)} %fusion.73) | copy-start | bytes 49156
  109.3 28.3 %collective-permute-start = (f32[128,256]{1,0:T(8,128)S(1)}, f32[128,256]{1,0:T(8,128)S(1)}, u32[]{:S(2)}, u32[]{:S(2)}) collective-permute-start(f32[128,256]{1,0:T(8,128)S(1)} %slice.39), channel_id=1, source_target_pairs={{0,0},{1,32},{2,64},{3,96},{4,128},{5,160},{6,192},{7,224},{8,256}... | collective-permute-start | bytes 393224 | tf_op jit(solution)/shard_map/ppermute | solution.py:98
  134.6 3.5 %copy-start.1 = (f32[4096,256]{1,0:T(8,128)S(1)}, f32[4096,256]{1,0:T(8,128)}, u32[]{:S(2)}) copy-start(f32[4096,256]{1,0:T(8,128)} %gather_fusion.1) | copy-start | bytes 12582916
  137.6 4.6 %copy-start.3 = (f32[4096]{0:T(1024)}, f32[4096]{0:T(1024)S(1)}, u32[]{:S(2)}) copy-start(f32[4096]{0:T(1024)S(1)} %multiply_reduce_fusion) | copy-start | bytes 49156
  138.0 4.3 %copy-start.6 = (f32[128]{0:T(128)}, f32[128]{0:T(128)S(1)}, u32[]{:S(2)}) copy-start(f32[128]{0:T(128)S(1)} %multiply_reduce_fusion.1) | copy-start | bytes 1540
  186.4 7.0 %copy-start.2 = (f32[4096,64]{0,1:T(8,128)}, f32[4096,64]{0,1:T(8,128)S(1)}, u32[]{:S(2)}) copy-start(f32[4096,64]{0,1:T(8,128)S(1)} %fusion.13) | copy-start | bytes 3145732
Sparse Core Ops, SparseCore 0:
  12.4 92.5 all-gather.3
  109.2 42.5 all-gather.5

commit v6 on v5

--- a/solution.py
+++ b/solution.py
@@ -110,11 +110,10 @@
     factor = jnp.linalg.cholesky(kernel(scaled_panel, scaled_panel, panel_global, panel_global))
     row_panel = panel_solve(factor, kernel(scaled_rows, scaled_panel, row_global, panel_global))
     col_panel = panel_solve(factor, kernel(scaled_cols, scaled_panel, col_global, panel_global))
-    window = lax.optimization_barrier(kernel(scaled_rows, scaled_cols, row_global, col_global))
     update = jnp.dot(
         row_panel, col_panel.T, precision=lax.Precision.HIGHEST, preferred_element_type=jnp.float32
     )
-    schur = window - update
+    schur = kernel(scaled_rows, scaled_cols, row_global, col_global) - update
     return (schur, row_panel)
 
 

time: 201 us -> 203 us (level)
  transfers between devices with their start and end apart: 3 -> 3, of which waited for: 2 -> 2; matrix products, arithmetic and copies ran while one was open for 14% -> 15% of each run, Pallas kernels for 0% -> 0%
where the time goes in v6:
time: 203 us; the launch traced here: 202 us
  waiting for transfers between devices  97.2 us (48%)
  local copies, waits for them, and re-layouts  30 us (15%)
  other arithmetic  28 us (14%)
  matrix products  25 us (12%)
  between operations  15 us (7%)
  starting transfers between devices  6.9 us (3%)
    all_gather x1, waiting for transfers between devices, body(): gathered = lax.all_gather(compact, 'col', axis=0, tiled=True)  89.1 us
    gather x1, local copies, waits for them, and re-layouts, body(): features = jnp.take(gathered, pick_idx, axis=0)  18.6 us
    dot_general x4, matrix products, kernel(): jnp.dot(left, right.T, precision=lax.Precision.HIGHEST, preferred_element...  12.8 us
    another operation x3, other arithmetic, body(): jnp.linalg.cholesky(kernel(scaled_panel, scaled_panel, panel_global, pane...  8.65 us
    another operation x2, other arithmetic, panel_solve(): lax.linalg.triangular_solve(factor, block, left_side=False, lower=True, t...  8.3 us
    all_gather x1, waiting for transfers between devices, body(): lax.all_gather(panel_rows, 'row', axis=0)  8.06 us
    ppermute x1, starting transfers between devices, body(): lax.ppermute(col_local, ('row', 'col'), window_perm(rows_count, cols_count))  6.82 us
    dot_general x1, matrix products, body(): jnp.dot(row_panel, col_panel.T, precision=lax.Precision.HIGHEST, preferre...  6.79 us
  transfers between devices with their start and end apart: 3, of which 2 were waited for; matrix products, arithmetic and copies ran while one was open for 15% of the time, Pallas kernels for 0%

profile of v6, /device:TPU:1, one launch (start us, length us, event | category | flops | bytes accessed | tf_op | source)
XLA Modules:
  0.0 202.0 jit_solution(13588914687452918237)
XLA Ops:
  7.2 0.8 add_select_fusion.2
  8.0 0.7 add_select_fusion.1
  8.7 0.8 fusion.12
  9.6 0.6 reduce-window.6
  10.1 0.2 slice_reduce_fusion
  10.4 0.1 copy_bitcast_fusion
  10.5 0.1 convert_reduce_fusion
  10.6 0.8 gather_fusion
  11.5 0.8 broadcast_select_fusion.1
  12.2 0.0 all-gather.6.cloned.1.call-start
  13.0 0.1 iota_add_fusion.1
  13.1 0.1 add.419
  13.2 0.1 add.416
  13.2 1.1 fusion.11
  14.3 1.1 gather_fusion.2
  15.5 0.1 dynamic_slice.16
  15.6 0.1 dynamic-slice_bitcast_fusion
  15.7 0.1 compare_and_fusion.1
  15.7 0.1 compare_select_fusion.1
  15.8 89.1 %all-gather.4.cloned.1.call-done = f32[5120,256]{1,0:T(8,128)} async-done(((f32[160,256]{1,0:T(8,128)}), f32[5120,256]{1,0:T(8,128)}) %all-gather.4.cloned.1.call-update) | async-done | bytes 5242896 | tf_op jit(solution)/shard_map/all_gather | solution.py:78
  105.0 3.3 %gather_fusion.3 = f32[192,256]{1,0:T(8,128)S(1)} fusion(f32[5120,256]{1,0:T(8,128)} %all-gather.4.cloned.1.call-done, s32[1024]{0:T(1024)S(1)} %pad_clamp_fusion), kind=kCustom, calls=%fused_computation.3 | custom fusion | bytes 393984 | tf_op jit(solution)/shard_map/jit(_take)/gather | solution.py:95
  108.3 0.1 broadcast_select_fusion
  108.4 0.6 slice.40
  109.1 0.1 iota_add_fusion
  109.2 0.6 add.442
  109.8 0.6 fusion.73
  110.4 6.8 %collective-permute-start = (f32[128,256]{1,0:T(8,128)S(1)}, f32[128,256]{1,0:T(8,128)S(1)}, u32[]{:S(2)}, u32[]{:S(2)}) collective-permute-start(f32[128,256]{1,0:T(8,128)S(1)} %slice.39), channel_id=1, source_target_pairs={{0,0},{1,32},{2,64},{3,96},{4,128},{5,160},{6,192},{7,224},{8,256}... | collective-permute-start | bytes 393224 | tf_op jit(solution)/shard_map/ppermute | solution.py:98
  117.2 18.6 %gather_fusion.1 = f32[4096,256]{1,0:T(8,128)} fusion(f32[5120,256]{1,0:T(8,128)} %all-gather.4.cloned.1.call-done, s32[4096]{0:T(1024)S(1)} %fusion.87), kind=kCustom, calls=%fused_computation.1 | custom fusion | bytes 8404992 | tf_op jit(solution)/shard_map/jit(_take)/gather | solution.py:82
  135.8 3.7 %multiply_reduce_fusion = f32[4096]{0:T(1024)} fusion(f32[4096,256]{1,0:T(8,128)} %gather_fusion.1, f32[256]{0:T(256)S(1)} %broadcast_divide_fusion, pred[4096]{0:T(1024)(128)(4,1)S(1)} %get-tuple-element.4), kind=kLoop, calls=%fused_computation.10 | loop fusion | flops 4190208 | bytes 4215808 | tf_op jit(solution)/shard_map/reduce_sum | solution.py:43
  139.5 0.7 multiply_reduce_fusion.1
  140.2 3.5 %convolution_multiply_fusion.1 = f32[4096,128]{1,0:T(8,128)S(1)} fusion(f32[4096,256]{1,0:T(8,128)S(1)} %copy-done.1, f32[256]{0:T(256)S(1)} %broadcast_divide_fusion, pred[4096]{0:T(1024)(128)(4,1)S(1)} %get-tuple-element.4, f32[128,256]{1,0:T(8,128)S(1)} %collective-permute-done), kind=kOutput, calls=%fused_computation.6 | convolution fusion | flops 1613266944 | bytes 6427648 | tf_op jit(solution)/shard_map/dot_general | solution.py:45
  143.7 8.1 %all-gather.6.cloned.1.call-done = f32[1024,256]{1,0:T(8,128)} async-done(((f32[64,256]{1,0:T(8,128)}), f32[1024,256]{1,0:T(8,128)}) %all-gather.6.cloned.1.call-update) | async-done | bytes 1048592 | tf_op jit(solution)/shard_map/all_gather | solution.py:100
  151.8 0.9 multiply_reduce_fusion.2
  152.7 1.8 fusion.108
  154.5 6.4 %fusion.1 = f32[4096,64]{0,1:T(8,128)S(1)} fusion(f32[4096,256]{1,0:T(8,128)} %gather_fusion.1, f32[256]{0:T(256)S(1)} %broadcast_divide_fusion, pred[4096]{0:T(1024)(128)(4,1)S(1)} %get-tuple-element.4, f32[64]{0:T(128)S(1)} %multiply_reduce_fusion.2, f32[4096]{0:T(1024)} %multiply_reduce_fusion, f32[16,64,256]{2,1,0:T(8,128)} %bitcast.62, s32[]{:T(128)S(6)} %select_n.194), kind=kOutput, calls=%fused_computation.9 | convolution fusion | flops 808468480 | bytes 5331460 | tf_op jit(solution)/shard_map/dot_general | solution.py:45
  160.9 1.4 copy.23
  162.3 1.5 copy.24
  163.8 1.5 copy.21
  165.2 1.5 add_multiply_fusion
  166.7 7.2 %cholesky.15 = f32[64,64]{1,0:T(8,128)} custom-call(f32[64,64]{1,0:T(8,128)} %add_multiply_fusion), custom_call_target="Cholesky" | custom-call | tf_op jit(solution)/shard_map/jit(cholesky)/cholesky | solution.py:110
  173.9 0.8 select_reduce_fusion
  174.7 0.6 compare_reduce_fusion
  175.4 2.0 %fusion.42 = f32[1,64,64]{2,1,0:T(8,128)} fusion(f32[64,64]{1,0:T(8,128)} %cholesky.15, pred[]{:T(512)} %compare_reduce_fusion), kind=kLoop, calls=%fused_computation.65 | loop fusion | flops 16384 | bytes 32769 | tf_op jit(solution)/shard_map/triangular_solve | solution.py:56
  177.4 6.3 %custom-call.8 = f32[1,64,64]{1,2,0:T(8,128)} custom-call(f32[1,64,64]{2,1,0:T(8,128)} %fusion.42), custom_call_target="InvertDiagBlocksLowerTriangular" | custom-call | tf_op jit(solution)/shard_map/triangular_solve | solution.py:56
  183.7 2.5 %fusion.13 = f32[4096,64]{0,1:T(8,128)S(1)} fusion(f32[4096,64]{0,1:T(8,128)S(1)} %fusion.1, s32[4096]{0:T(1024)} %fusion.73, s32[64]{0:T(128)S(1)} %iota_add_fusion.2, f32[1,64,64]{1,2,0:T(8,128)} %custom-call.8), kind=kOutput, calls=%fused_computation.26 | convolution fusion | flops 203685888 | bytes 2130176 | tf_op jit(solution)/shard_map/triangular_solve | solution.py:56
  186.2 1.2 convolution_multiply_fusion.3
  187.3 1.0 fusion.43
  188.4 6.8 %convolution_subtract_fusion = f32[4096,128]{1,0:T(8,128)} fusion(f32[4096,64]{0,1:T(8,128)S(1)} %fusion.13, f32[128,64]{0,1:T(8,128)S(1)} %fusion.43, f32[4096,128]{1,0:T(8,128)S(1)} %convolution_multiply_fusion.1, s32[128]{0:T(128)} %add.442, f32[128]{0:T(128)} %multiply_reduce_fusion.1, f32[4096]{0:T(1024)} %multiply_reduce_fusion, s32[4096]{0:T(1024)} %fusion.73), kind=kOutput, calls=%fused_computation.5 | convolution fusion | flops 409468928 | bytes 5309440 | tf_op jit(solution)/shard_map/dot_general | solution.py:113
  (31 shorter events, 0.3 us)
Async XLA Ops:
  7.2 3.5 %copy-start = (f32[256,256]{1,0:T(8,128)S(1)}, f32[256,256]{1,0:T(8,128)}, u32[]{:S(2)}) copy-start(f32[256,256]{1,0:T(8,128)} %param.4) | copy-start | bytes 786436
  7.2 97.8 %all-gather.4.cloned.1.call-start = ((), (), s32[]{:S(2)}) async-start(), calls=%async_computation | async-start | bytes 5406720 | tf_op jit(solution)/shard_map/all_gather | solution.py:78
  10.3 100.1 %copy-start.2 = (f32[256]{0:T(256)S(1)}, f32[256]{0:T(256)}, u32[]{:S(2)}) copy-start(f32[256]{0:T(256)} %param.6) | copy-start | bytes 3076
  12.2 139.5 %all-gather.6.cloned.1.call-start = ((), (), s32[]{:S(2)}) async-start(), calls=%async_computation.1 | async-start | bytes 1114112 | tf_op jit(solution)/shard_map/all_gather | solution.py:100
  110.4 29.1 %collective-permute-start = (f32[128,256]{1,0:T(8,128)S(1)}, f32[128,256]{1,0:T(8,128)S(1)}, u32[]{:S(2)}, u32[]{:S(2)}) collective-permute-start(f32[128,256]{1,0:T(8,128)S(1)} %slice.39), channel_id=1, source_target_pairs={{0,0},{1,32},{2,64},{3,96},{4,128},{5,160},{6,192},{7,224},{8,256}... | collective-permute-start | bytes 393224 | tf_op jit(solution)/shard_map/ppermute | solution.py:98
  135.8 4.4 %copy-start.1 = (f32[4096,256]{1,0:T(8,128)S(1)}, f32[4096,256]{1,0:T(8,128)}, u32[]{:S(2)}) copy-start(f32[4096,256]{1,0:T(8,128)} %gather_fusion.1) | copy-start | bytes 12582916
  186.1 9.0 %copy-start.3 = (f32[4096,64]{0,1:T(8,128)}, f32[4096,64]{0,1:T(8,128)S(1)}, u32[]{:S(2)}) copy-start(f32[4096,64]{0,1:T(8,128)S(1)} %fusion.13) | copy-start | bytes 3145732
Sparse Core Ops, SparseCore 0:
  12.4 92.5 all-gather.3
  109.2 42.5 all-gather.5

commit v7 on v3

--- a/solution.py
+++ b/solution.py
@@ -1,6 +1,7 @@
 import jax
 import jax.numpy as jnp
 from jax import lax
+from jax.experimental import pallas as pl
 from jax.sharding import PartitionSpec as P
 
 TB = 64
@@ -52,8 +53,36 @@
     return value + noise_level * same
 
 
-def panel_solve(factor, block):
-    return lax.linalg.triangular_solve(factor, block, left_side=False, lower=True, transpose_a=True)
+def factor_kernel(a_ref, low_ref, inv_ref):
+    n = a_ref.shape[0]
+    rows = lax.broadcasted_iota(jnp.int32, (n, n), 0)
+    cols = lax.broadcasted_iota(jnp.int32, (n, n), 1)
+    rcol = lax.broadcasted_iota(jnp.int32, (n, 1), 0)
+    ccol = lax.broadcasted_iota(jnp.int32, (1, n), 1)
+    m = a_ref[...]
+    low = jnp.zeros((n, n), jnp.float32)
+    inv = (rows == cols).astype(jnp.float32)
+    for k in range(n):
+        d = jnp.sqrt(m[k : k + 1, k : k + 1])
+        lc = jnp.where(rcol >= k, m[:, k : k + 1] / d, 0.0)
+        lr = jnp.where(ccol >= k, m[k : k + 1, :] / d, 0.0)
+        m = m - lc * lr
+        low = jnp.where(cols == k, lc, low)
+        xk = inv[k : k + 1, :] / d
+        inv = jnp.where(rows == k, xk, inv) - jnp.where(rcol > k, lc, 0.0) * xk
+    low_ref[...] = low
+    inv_ref[...] = inv
+
+
+def factor_and_inverse(a):
+    shape = jax.ShapeDtypeStruct(a.shape, jnp.float32)
+    return pl.pallas_call(factor_kernel, out_shape=(shape, shape))(a)
+
+
+def panel_solve(inverse, block):
+    return jnp.dot(
+        block, inverse.T, precision=lax.Precision.HIGHEST, preferred_element_type=jnp.float32
+    )
 
 
 def body(pool, row_pick, length_scale, panel_tile):
@@ -102,9 +131,9 @@
     row_global = (local_index // TB * rows_count + my_row) * TB + local_index % TB
     col_global = (tiles[:, None] * TB + jnp.arange(TB)[None, :]).reshape(-1)
     panel_global = panel * TB + jnp.arange(TB)
-    factor = jnp.linalg.cholesky(kernel(scaled_panel, scaled_panel, panel_global, panel_global))
-    row_panel = panel_solve(factor, kernel(scaled_rows, scaled_panel, row_global, panel_global))
-    col_panel = panel_solve(factor, kernel(scaled_cols, scaled_panel, col_global, panel_global))
+    factor, inverse = factor_and_inverse(kernel(scaled_panel, scaled_panel, panel_global, panel_global))
+    row_panel = panel_solve(inverse, kernel(scaled_rows, scaled_panel, row_global, panel_global))
+    col_panel = panel_solve(inverse, kernel(scaled_cols, scaled_panel, col_global, panel_global))
     update = jnp.dot(
         row_panel, col_panel.T, precision=lax.Precision.HIGHEST, preferred_element_type=jnp.float32
     )

time: 191 us -> 187 us (0.979)
  other arithmetic: 20.5 us -> 8.37 us
  Pallas kernels: 0 us -> 7.57 us
    another operation x8 -> x3, other arithmetic: 12.8 us -> 0.71 us  [the longest x3 6.52 us: body(): jnp.linalg.cholesky(kernel(scaled_panel, scaled_panel, panel_global, pane...]
    pallas_call x0 -> x1, Pallas kernels: none -> 7.57 us  [factor_and_inverse(): return pl.pallas_call(factor_kernel, out_shape=(shape, shape))(a)]
    another operation x2 -> x0, matrix products: 1.98 us -> none  [panel_solve(): lax.linalg.triangular_solve(factor, block, left_side=False, lower=True, t...]
    dot_general x0 -> x2, matrix products: none -> 1.96 us  [panel_solve(): jnp.dot(block, inverse.T, precision=lax.Precision.HIGHEST, preferred_elem...]
where the time goes in v7:
time: 187 us; the launch traced here: 185 us
  waiting for transfers between devices  97.2 us (52%)
  local copies, waits for them, and re-layouts  27.6 us (15%)
  matrix products  22.7 us (12%)
  between operations  15 us (8%)
  other arithmetic  8.37 us (4%)
  Pallas kernels  7.57 us (4%)
  starting transfers between devices  6.9 us (4%)
    all_gather x1, waiting for transfers between devices, body(): gathered = lax.all_gather(compact, 'col', axis=0, tiled=True)  89.1 us
    gather x1, local copies, waits for them, and re-layouts, body(): features = jnp.take(gathered, pick_idx, axis=0)  18.6 us
    dot_general x4, matrix products, kernel(): jnp.dot(left, right.T, precision=lax.Precision.HIGHEST, preferred_element...  12.8 us
    all_gather x1, waiting for transfers between devices, body(): lax.all_gather(panel_rows, 'row', axis=0)  8.02 us
    pallas_call x1, Pallas kernels, factor_and_inverse(): return pl.pallas_call(factor_kernel, out_shape=(shape, shape))(a)  7.57 us
    ppermute x1, starting transfers between devices, body(): lax.ppermute(col_local, ('row', 'col'), window_perm(rows_count, cols_count))  6.82 us
    dot_general x1, matrix products, body(): jnp.dot(row_panel, col_panel.T, precision=lax.Precision.HIGHEST, preferre...  6.04 us
    gather x2, local copies, waits for them, and re-layouts, body(): col_local = jnp.take(gathered, jnp.take(pick_idx, col_source), axis=0)  4.39 us
  transfers between devices with their start and end apart: 3, of which 2 were waited for; matrix products, arithmetic and copies ran while one was open for 17% of the time, Pallas kernels for 0%

profile of v7, /device:TPU:1, one launch (start us, length us, event | category | flops | bytes accessed | tf_op | source)
XLA Modules:
  0.0 185.4 jit_solution(14342328733984824239)
XLA Ops:
  7.2 0.0 copy-start
  7.2 0.0 all-gather.3.cloned.1.call-start
  7.2 0.0 copy-start.2
  7.2 0.8 add_select_fusion.2
  8.0 0.7 add_select_fusion.1
  8.7 0.8 fusion.12
  9.6 0.6 reduce-window.6
  10.2 0.2 slice_reduce_fusion
  10.4 0.1 copy_bitcast_fusion
  10.5 0.1 convert_reduce_fusion
  10.6 0.0 copy-done
  10.6 0.8 gather_fusion
  11.5 0.8 broadcast_select_fusion
  12.2 0.0 all-gather.3.cloned.1.call-update
  12.3 0.0 all-gather.5.cloned.1.call-start
  13.1 0.1 iota_add_fusion.1
  13.1 0.1 add.391
  13.2 0.1 add.388
  13.3 0.1 iota_add_fusion
  13.4 0.1 add.414
  13.5 1.1 fusion.11
  14.6 1.1 gather_fusion.2
  15.7 0.1 compare_and_fusion.1
  15.8 89.1 %all-gather.3.cloned.1.call-done = f32[5120,256]{1,0:T(8,128)} async-done(((f32[160,256]{1,0:T(8,128)}), f32[5120,256]{1,0:T(8,128)}) %all-gather.3.cloned.1.call-update) | async-done | bytes 5242896 | tf_op jit(solution)/shard_map/all_gather | solution.py:107
  105.0 3.1 %gather_fusion.4 = f32[64,256]{1,0:T(8,128)S(1)} fusion(f32[5120,256]{1,0:T(8,128)} %all-gather.3.cloned.1.call-done, s32[1024]{0:T(1024)S(1)} %pad_clamp_fusion), kind=kCustom, calls=%fused_computation.4 | custom fusion | bytes 131328 | tf_op jit(solution)/shard_map/jit(_take)/gather | solution.py:122
  108.1 0.7 bitcast_select_fusion
  108.8 0.0 all-gather.5.cloned.1.call-update
  108.9 3.2 %gather_fusion.3 = f32[128,256]{1,0:T(8,128)S(1)} fusion(f32[5120,256]{1,0:T(8,128)} %all-gather.3.cloned.1.call-done, s32[1024]{0:T(1024)S(1)} %pad_clamp_fusion.1), kind=kCustom, calls=%fused_computation.3 | custom fusion | bytes 262656 | tf_op jit(solution)/shard_map/jit(_take)/gather | solution.py:118
  112.2 0.1 broadcast_select_fusion.1
  112.3 6.8 %collective-permute-start = (f32[128,256]{1,0:T(8,128)S(1)}, f32[128,256]{1,0:T(8,128)S(1)}, u32[]{:S(2)}, u32[]{:S(2)}) collective-permute-start(f32[128,256]{1,0:T(8,128)S(1)} %broadcast_select_fusion.1), channel_id=1, source_target_pairs={{0,0},{1,32},{2,64},{3,96},{4,128},{5,160},{6,192},{7,224},{8,256}... | collective-permute-start | bytes 393224 | tf_op jit(solution)/shard_map/ppermute | solution.py:119
  119.1 18.6 %gather_fusion.1 = f32[4096,256]{1,0:T(8,128)} fusion(f32[5120,256]{1,0:T(8,128)} %all-gather.3.cloned.1.call-done, s32[4096]{0:T(1024)S(1)} %fusion.87), kind=kCustom, calls=%fused_computation.1 | custom fusion | bytes 8404992 | tf_op jit(solution)/shard_map/jit(_take)/gather | solution.py:111
  137.7 3.1 %multiply_reduce_fusion = f32[4096]{0:T(1024)S(1)} fusion(f32[4096,256]{1,0:T(8,128)} %gather_fusion.1, f32[256]{0:T(256)S(1)} %broadcast_divide_fusion, pred[4096]{0:T(1024)(128)(4,1)S(1)} %get-tuple-element.4), kind=kLoop, calls=%fused_computation.11 | loop fusion | flops 4190208 | bytes 4215808 | tf_op jit(solution)/shard_map/reduce_sum | solution.py:44
  140.8 0.0 collective-permute-done
  140.8 0.1 multiply_reduce_fusion.1
  140.9 0.2 copy-done.1
  141.1 3.5 %convolution_multiply_fusion.1 = f32[4096,128]{1,0:T(8,128)S(1)} fusion(f32[4096,256]{1,0:T(8,128)S(1)} %copy-done.1, f32[256]{0:T(256)S(1)} %broadcast_divide_fusion, pred[4096]{0:T(1024)(128)(4,1)S(1)} %get-tuple-element.4, f32[128,256]{1,0:T(8,128)S(1)} %collective-permute-done), kind=kOutput, calls=%fused_computation.7 | convolution fusion | flops 1613266944 | bytes 6427648 | tf_op jit(solution)/shard_map/dot_general | solution.py:46
  144.6 8.0 %all-gather.5.cloned.1.call-done = f32[16,64,256]{2,1,0:T(8,128)} async-done(((f32[1,64,256]{2,1,0:T(8,128)}), f32[16,64,256]{2,1,0:T(8,128)}) %all-gather.5.cloned.1.call-update) | async-done | bytes 1048592 | tf_op jit(solution)/shard_map/all_gather | solution.py:124
  152.6 0.9 multiply_reduce_fusion.2
  153.6 1.8 select_add_fusion.a_ref
  155.4 7.6 %shard_map.59 = (f32[64,64]{1,0:T(8,128)}, f32[64,64]{1,0:T(8,128)}) custom-call(f32[64,64]{1,0:T(8,128)} %select_add_fusion.a_ref), custom_call_target="tpu_custom_call" | custom-call | tf_op jit(solution)/shard_map/pallas_call | solution.py:79
  162.9 6.4 %fusion.1 = f32[4096,64]{0,1:T(8,128)S(1)} fusion(f32[4096,256]{1,0:T(8,128)} %gather_fusion.1, f32[256]{0:T(256)S(1)} %broadcast_divide_fusion, pred[4096]{0:T(1024)(128)(4,1)S(1)} %get-tuple-element.4, f32[64]{0:T(128)S(1)} %multiply_reduce_fusion.2, f32[4096]{0:T(1024)S(1)} %multiply_reduce_fusion, f32[16,64,256]{2,1,0:T(8,128)} %all-gather.5.cloned.1.call-done, ...), kind=kOutput, calls=%fused_computation.10 | convolution fusion | flops 808468480 | bytes 5331460 | tf_op jit(solution)/shard_map/dot_general | solution.py:46
  169.3 0.0 copy-done.3
  169.3 1.7 fusion.15
  171.0 0.0 copy-start.4
  171.0 1.2 convolution_multiply_fusion.3
  172.2 0.3 fusion.44
  172.5 6.0 %convolution_subtract_fusion = f32[4096,128]{1,0:T(8,128)} fusion(f32[4096,64]{0,1:T(8,128)S(1)} %fusion.15, f32[128,64]{0,1:T(8,128)S(1)} %fusion.44, f32[4096,128]{1,0:T(8,128)S(1)} %convolution_multiply_fusion.1, s32[128]{0:T(128)S(1)} %add.414, f32[128]{0:T(128)S(1)} %multiply_reduce_fusion.1, f32[4096]{0:T(1024)S(1)} %multiply_reduce_fusion, ...), kind=kOutput, calls=%fused_computation.6 | convolution fusion | flops 409468928 | bytes 5309440 | tf_op jit(solution)/shard_map/dot_general | solution.py:137
  178.5 0.0 copy-done.4
  (24 shorter events, 0.2 us)
Async XLA Ops:
  7.2 3.5 %copy-start = (f32[256,256]{1,0:T(8,128)S(1)}, f32[256,256]{1,0:T(8,128)}, u32[]{:S(2)}) copy-start(f32[256,256]{1,0:T(8,128)} %param.4) | copy-start | bytes 786436
  7.2 97.8 %all-gather.3.cloned.1.call-start = ((), (), s32[]{:S(2)}) async-start(), calls=%async_computation | async-start | bytes 5406720 | tf_op jit(solution)/shard_map/all_gather | solution.py:107
  7.2 101.7 %copy-start.2 = (f32[256]{0:T(256)S(1)}, f32[256]{0:T(256)}, u32[]{:S(2)}) copy-start(f32[256]{0:T(256)} %param.6) | copy-start | bytes 3076
  12.3 140.4 %all-gather.5.cloned.1.call-start = ((), (), s32[]{:S(2)}) async-start(), calls=%async_computation.1 | async-start | bytes 1114112 | tf_op jit(solution)/shard_map/all_gather | solution.py:124
  112.3 28.5 %collective-permute-start = (f32[128,256]{1,0:T(8,128)S(1)}, f32[128,256]{1,0:T(8,128)S(1)}, u32[]{:S(2)}, u32[]{:S(2)}) collective-permute-start(f32[128,256]{1,0:T(8,128)S(1)} %broadcast_select_fusion.1), channel_id=1, source_target_pairs={{0,0},{1,32},{2,64},{3,96},{4,128},{5,160},{6,192},{7,224},{8,256}... | collective-permute-start | bytes 393224 | tf_op jit(solution)/shard_map/ppermute | solution.py:119
  137.7 3.4 %copy-start.1 = (f32[4096,256]{1,0:T(8,128)S(1)}, f32[4096,256]{1,0:T(8,128)}, u32[]{:S(2)}) copy-start(f32[4096,256]{1,0:T(8,128)} %gather_fusion.1) | copy-start | bytes 12582916
  162.9 6.4 %copy-start.3 = (f32[64,64]{1,0:T(8,128)S(1)}, f32[64,64]{1,0:T(8,128)}, u32[]{:S(2)}) copy-start(f32[64,64]{1,0:T(8,128)} %get-tuple-element.3) | copy-start | bytes 49156
  171.0 7.5 %copy-start.4 = (f32[4096,64]{0,1:T(8,128)}, f32[4096,64]{0,1:T(8,128)S(1)}, u32[]{:S(2)}) copy-start(f32[4096,64]{0,1:T(8,128)S(1)} %fusion.15) | copy-start | bytes 3145732
Sparse Core Ops, SparseCore 0:
  12.4 92.5 all-gather.2
  109.0 43.6 all-gather.4

commit v8 on v7

--- a/solution.py
+++ b/solution.py
@@ -63,12 +63,12 @@
     low = jnp.zeros((n, n), jnp.float32)
     inv = (rows == cols).astype(jnp.float32)
     for k in range(n):
-        d = jnp.sqrt(m[k : k + 1, k : k + 1])
-        lc = jnp.where(rcol >= k, m[:, k : k + 1] / d, 0.0)
-        lr = jnp.where(ccol >= k, m[k : k + 1, :] / d, 0.0)
+        r = 1.0 / jnp.sqrt(m[k : k + 1, k : k + 1])
+        lc = jnp.where(rcol >= k, m[:, k : k + 1] * r, 0.0)
+        lr = jnp.where(ccol >= k, m[k : k + 1, :] * r, 0.0)
         m = m - lc * lr
         low = jnp.where(cols == k, lc, low)
-        xk = inv[k : k + 1, :] / d
+        xk = inv[k : k + 1, :] * r
         inv = jnp.where(rows == k, xk, inv) - jnp.where(rcol > k, lc, 0.0) * xk
     low_ref[...] = low
     inv_ref[...] = inv

time: 187 us -> 187 us (level)
  no operation moved by 1% of the time
where the time goes in v8:
time: 187 us; the launch traced here: 185 us
  waiting for transfers between devices  97.2 us (52%)
  local copies, waits for them, and re-layouts  27.6 us (15%)
  matrix products  22.7 us (12%)
  between operations  15 us (8%)
  other arithmetic  8.37 us (4%)
  Pallas kernels  7.57 us (4%)
  starting transfers between devices  6.9 us (4%)
    all_gather x1, waiting for transfers between devices, body(): gathered = lax.all_gather(compact, 'col', axis=0, tiled=True)  89.1 us
    gather x1, local copies, waits for them, and re-layouts, body(): features = jnp.take(gathered, pick_idx, axis=0)  18.6 us
    dot_general x4, matrix products, kernel(): jnp.dot(left, right.T, precision=lax.Precision.HIGHEST, preferred_element...  12.8 us
    all_gather x1, waiting for transfers between devices, body(): lax.all_gather(panel_rows, 'row', axis=0)  8.02 us
    pallas_call x1, Pallas kernels, factor_and_inverse(): return pl.pallas_call(factor_kernel, out_shape=(shape, shape))(a)  7.57 us
    ppermute x1, starting transfers between devices, body(): lax.ppermute(col_local, ('row', 'col'), window_perm(rows_count, cols_count))  6.82 us
    dot_general x1, matrix products, body(): jnp.dot(row_panel, col_panel.T, precision=lax.Precision.HIGHEST, preferre...  6.04 us
    gather x2, local copies, waits for them, and re-layouts, body(): col_local = jnp.take(gathered, jnp.take(pick_idx, col_source), axis=0)  4.39 us
  transfers between devices with their start and end apart: 3, of which 2 were waited for; matrix products, arithmetic and copies ran while one was open for 17% of the time, Pallas kernels for 0%

profile of v8, /device:TPU:1, one launch (start us, length us, event | category | flops | bytes accessed | tf_op | source)
XLA Modules:
  0.0 185.4 jit_solution(9043902169588485186)
XLA Ops:
  7.2 0.0 copy-start
  7.2 0.0 all-gather.3.cloned.1.call-start
  7.2 0.0 copy-start.2
  7.2 0.8 add_select_fusion.2
  8.0 0.7 add_select_fusion.1
  8.7 0.8 fusion.12
  9.6 0.6 reduce-window.6
  10.2 0.2 slice_reduce_fusion
  10.4 0.1 copy_bitcast_fusion
  10.5 0.1 convert_reduce_fusion
  10.6 0.0 copy-done
  10.6 0.8 gather_fusion
  11.5 0.8 broadcast_select_fusion
  12.2 0.0 all-gather.3.cloned.1.call-update
  12.3 0.0 all-gather.5.cloned.1.call-start
  13.1 0.1 iota_add_fusion.1
  13.1 0.1 add.391
  13.2 0.1 add.388
  13.3 0.1 iota_add_fusion
  13.4 0.1 add.414
  13.5 1.1 fusion.11
  14.6 1.1 gather_fusion.2
  15.7 0.1 compare_and_fusion.1
  15.8 89.1 %all-gather.3.cloned.1.call-done = f32[5120,256]{1,0:T(8,128)} async-done(((f32[160,256]{1,0:T(8,128)}), f32[5120,256]{1,0:T(8,128)}) %all-gather.3.cloned.1.call-update) | async-done | bytes 5242896 | tf_op jit(solution)/shard_map/all_gather | solution.py:107
  105.0 3.1 %gather_fusion.4 = f32[64,256]{1,0:T(8,128)S(1)} fusion(f32[5120,256]{1,0:T(8,128)} %all-gather.3.cloned.1.call-done, s32[1024]{0:T(1024)S(1)} %pad_clamp_fusion), kind=kCustom, calls=%fused_computation.4 | custom fusion | bytes 131328 | tf_op jit(solution)/shard_map/jit(_take)/gather | solution.py:122
  108.1 0.7 bitcast_select_fusion
  108.8 0.0 all-gather.5.cloned.1.call-update
  108.9 3.2 %gather_fusion.3 = f32[128,256]{1,0:T(8,128)S(1)} fusion(f32[5120,256]{1,0:T(8,128)} %all-gather.3.cloned.1.call-done, s32[1024]{0:T(1024)S(1)} %pad_clamp_fusion.1), kind=kCustom, calls=%fused_computation.3 | custom fusion | bytes 262656 | tf_op jit(solution)/shard_map/jit(_take)/gather | solution.py:118
  112.2 0.1 broadcast_select_fusion.1
  112.3 6.8 %collective-permute-start = (f32[128,256]{1,0:T(8,128)S(1)}, f32[128,256]{1,0:T(8,128)S(1)}, u32[]{:S(2)}, u32[]{:S(2)}) collective-permute-start(f32[128,256]{1,0:T(8,128)S(1)} %broadcast_select_fusion.1), channel_id=1, source_target_pairs={{0,0},{1,32},{2,64},{3,96},{4,128},{5,160},{6,192},{7,224},{8,256}... | collective-permute-start | bytes 393224 | tf_op jit(solution)/shard_map/ppermute | solution.py:119
  119.1 18.6 %gather_fusion.1 = f32[4096,256]{1,0:T(8,128)} fusion(f32[5120,256]{1,0:T(8,128)} %all-gather.3.cloned.1.call-done, s32[4096]{0:T(1024)S(1)} %fusion.87), kind=kCustom, calls=%fused_computation.1 | custom fusion | bytes 8404992 | tf_op jit(solution)/shard_map/jit(_take)/gather | solution.py:111
  137.7 3.1 %multiply_reduce_fusion = f32[4096]{0:T(1024)S(1)} fusion(f32[4096,256]{1,0:T(8,128)} %gather_fusion.1, f32[256]{0:T(256)S(1)} %broadcast_divide_fusion, pred[4096]{0:T(1024)(128)(4,1)S(1)} %get-tuple-element.4), kind=kLoop, calls=%fused_computation.11 | loop fusion | flops 4190208 | bytes 4215808 | tf_op jit(solution)/shard_map/reduce_sum | solution.py:44
  140.8 0.0 collective-permute-done
  140.8 0.1 multiply_reduce_fusion.1
  140.9 0.2 copy-done.1
  141.1 3.5 %convolution_multiply_fusion.1 = f32[4096,128]{1,0:T(8,128)S(1)} fusion(f32[4096,256]{1,0:T(8,128)S(1)} %copy-done.1, f32[256]{0:T(256)S(1)} %broadcast_divide_fusion, pred[4096]{0:T(1024)(128)(4,1)S(1)} %get-tuple-element.4, f32[128,256]{1,0:T(8,128)S(1)} %collective-permute-done), kind=kOutput, calls=%fused_computation.7 | convolution fusion | flops 1613266944 | bytes 6427648 | tf_op jit(solution)/shard_map/dot_general | solution.py:46
  144.6 8.0 %all-gather.5.cloned.1.call-done = f32[16,64,256]{2,1,0:T(8,128)} async-done(((f32[1,64,256]{2,1,0:T(8,128)}), f32[16,64,256]{2,1,0:T(8,128)}) %all-gather.5.cloned.1.call-update) | async-done | bytes 1048592 | tf_op jit(solution)/shard_map/all_gather | solution.py:124
  152.6 0.9 multiply_reduce_fusion.2
  153.6 1.8 select_add_fusion.a_ref
  155.4 7.6 %shard_map.59 = (f32[64,64]{1,0:T(8,128)}, f32[64,64]{1,0:T(8,128)}) custom-call(f32[64,64]{1,0:T(8,128)} %select_add_fusion.a_ref), custom_call_target="tpu_custom_call" | custom-call | tf_op jit(solution)/shard_map/pallas_call | solution.py:79
  162.9 6.4 %fusion.1 = f32[4096,64]{0,1:T(8,128)S(1)} fusion(f32[4096,256]{1,0:T(8,128)} %gather_fusion.1, f32[256]{0:T(256)S(1)} %broadcast_divide_fusion, pred[4096]{0:T(1024)(128)(4,1)S(1)} %get-tuple-element.4, f32[64]{0:T(128)S(1)} %multiply_reduce_fusion.2, f32[4096]{0:T(1024)S(1)} %multiply_reduce_fusion, f32[16,64,256]{2,1,0:T(8,128)} %all-gather.5.cloned.1.call-done, ...), kind=kOutput, calls=%fused_computation.10 | convolution fusion | flops 808468480 | bytes 5331460 | tf_op jit(solution)/shard_map/dot_general | solution.py:46
  169.3 0.0 copy-done.3
  169.3 1.7 fusion.15
  171.0 0.0 copy-start.4
  171.0 1.2 convolution_multiply_fusion.3
  172.2 0.3 fusion.44
  172.5 6.0 %convolution_subtract_fusion = f32[4096,128]{1,0:T(8,128)} fusion(f32[4096,64]{0,1:T(8,128)S(1)} %fusion.15, f32[128,64]{0,1:T(8,128)S(1)} %fusion.44, f32[4096,128]{1,0:T(8,128)S(1)} %convolution_multiply_fusion.1, s32[128]{0:T(128)S(1)} %add.414, f32[128]{0:T(128)S(1)} %multiply_reduce_fusion.1, f32[4096]{0:T(1024)S(1)} %multiply_reduce_fusion, ...), kind=kOutput, calls=%fused_computation.6 | convolution fusion | flops 409468928 | bytes 5309440 | tf_op jit(solution)/shard_map/dot_general | solution.py:137
  178.5 0.0 copy-done.4
  (24 shorter events, 0.2 us)
Async XLA Ops:
  7.2 3.5 %copy-start = (f32[256,256]{1,0:T(8,128)S(1)}, f32[256,256]{1,0:T(8,128)}, u32[]{:S(2)}) copy-start(f32[256,256]{1,0:T(8,128)} %param.4) | copy-start | bytes 786436
  7.2 97.8 %all-gather.3.cloned.1.call-start = ((), (), s32[]{:S(2)}) async-start(), calls=%async_computation | async-start | bytes 5406720 | tf_op jit(solution)/shard_map/all_gather | solution.py:107
  7.2 101.7 %copy-start.2 = (f32[256]{0:T(256)S(1)}, f32[256]{0:T(256)}, u32[]{:S(2)}) copy-start(f32[256]{0:T(256)} %param.6) | copy-start | bytes 3076
  12.3 140.4 %all-gather.5.cloned.1.call-start = ((), (), s32[]{:S(2)}) async-start(), calls=%async_computation.1 | async-start | bytes 1114112 | tf_op jit(solution)/shard_map/all_gather | solution.py:124
  112.3 28.5 %collective-permute-start = (f32[128,256]{1,0:T(8,128)S(1)}, f32[128,256]{1,0:T(8,128)S(1)}, u32[]{:S(2)}, u32[]{:S(2)}) collective-permute-start(f32[128,256]{1,0:T(8,128)S(1)} %broadcast_select_fusion.1), channel_id=1, source_target_pairs={{0,0},{1,32},{2,64},{3,96},{4,128},{5,160},{6,192},{7,224},{8,256}... | collective-permute-start | bytes 393224 | tf_op jit(solution)/shard_map/ppermute | solution.py:119
  137.7 3.4 %copy-start.1 = (f32[4096,256]{1,0:T(8,128)S(1)}, f32[4096,256]{1,0:T(8,128)}, u32[]{:S(2)}) copy-start(f32[4096,256]{1,0:T(8,128)} %gather_fusion.1) | copy-start | bytes 12582916
  162.9 6.4 %copy-start.3 = (f32[64,64]{1,0:T(8,128)S(1)}, f32[64,64]{1,0:T(8,128)}, u32[]{:S(2)}) copy-start(f32[64,64]{1,0:T(8,128)} %get-tuple-element.3) | copy-start | bytes 49156
  171.0 7.5 %copy-start.4 = (f32[4096,64]{0,1:T(8,128)}, f32[4096,64]{0,1:T(8,128)S(1)}, u32[]{:S(2)}) copy-start(f32[4096,64]{0,1:T(8,128)S(1)} %fusion.15) | copy-start | bytes 3145732
Sparse Core Ops, SparseCore 0:
  12.4 92.5 all-gather.2
  109.0 43.6 all-gather.4

commit v9 on v8

--- a/solution.py
+++ b/solution.py
@@ -27,6 +27,15 @@
             new = jnp.where((dist >= shift) & (dist < shift + step), got, new)
         x = new
         step *= radix
+    return x
+
+
+def sum_broadcast(x, axis, size):
+    step = 1
+    while step < size:
+        perm = [(i, (i + step) % size) for i in range(size)]
+        x = x + lax.ppermute(x, axis, perm)
+        step *= 2
     return x
 
 
@@ -119,10 +128,11 @@
     col_feats = lax.ppermute(col_local, ("row", "col"), window_perm(rows_count, cols_count))
     panel_row = panel % rows_count
     panel_local = panel // rows_count
-    panel_rows = jnp.take(gathered, lax.dynamic_slice_in_dim(pick_idx, panel_local * TB, TB), axis=0)
-    panel_feats = lax.dynamic_index_in_dim(
-        lax.all_gather(panel_rows, "row", axis=0), panel_row, axis=0, keepdims=False
-    )
+    panel_pick = lax.dynamic_slice_in_dim(row_pick, panel_row * local_rows + panel_local * TB, TB)
+    held = (panel_pick // pool_rows == my_col) & (my_row == panel_row)
+    panel_part = jnp.where(held[:, None], jnp.take(pool, panel_pick % pool_rows, axis=0), 0.0)
+    panel_rows = sum_broadcast(sum_broadcast(panel_part, "col", cols_count), "row", rows_count)
+    panel_feats = panel_rows
     inverse_scale = 1.0 / length_scale
     scaled_rows = features * inverse_scale
     scaled_cols = col_feats * inverse_scale

time: 187 us -> 166 us (0.89)
  the two profiles are of different devices: /device:TPU:1 before, /device:TPU:3 now
where the time goes in v9:
time: 166 us; the launch traced here: 165 us
  starting transfers between devices  46.2 us (28%)
  waiting for transfers between devices  44.3 us (27%)
  local copies, waits for them, and re-layouts  25.2 us (15%)
  matrix products  19.1 us (12%)
  between operations  15.2 us (9%)
  other arithmetic  7.74 us (5%)
  Pallas kernels  7.58 us (5%)
    ppermute x9, waiting for transfers between devices, sum_broadcast(): x = x + lax.ppermute(x, axis, perm)  40.8 us
    ppermute x9, starting transfers between devices, sum_broadcast(): x = x + lax.ppermute(x, axis, perm)  32.6 us
    gather x1, local copies, waits for them, and re-layouts, body(): features = jnp.take(gathered, pick_idx, axis=0)  18.6 us
    ppermute x1, starting transfers between devices, body(): lax.ppermute(col_local, ('row', 'col'), window_perm(rows_count, cols_count))  13.6 us
    dot_general x4, matrix products, kernel(): jnp.dot(left, right.T, precision=lax.Precision.HIGHEST, preferred_element...  9.19 us
    pallas_call x1, Pallas kernels, factor_and_inverse(): return pl.pallas_call(factor_kernel, out_shape=(shape, shape))(a)  7.58 us
    dot_general x1, matrix products, body(): jnp.dot(row_panel, col_panel.T, precision=lax.Precision.HIGHEST, preferre...  6.07 us
    gather x2, local copies, waits for them, and re-layouts, body(): col_local = jnp.take(gathered, jnp.take(pick_idx, col_source), axis=0)  4.39 us
  transfers between devices with their start and end apart: 11, of which 10 were waited for; matrix products, arithmetic and copies ran while one was open for 20% of the time, Pallas kernels for 5%

profile of v9, /device:TPU:3, one launch (start us, length us, event | category | flops | bytes accessed | tf_op | source)
XLA Modules:
  0.0 165.4 jit_solution(16358799139869930323)
XLA Ops:
  7.2 0.8 add_select_fusion.2
  8.0 0.7 add_select_fusion.1
  8.7 0.8 fusion.12
  9.6 0.6 reduce-window.6
  10.2 0.2 slice_reduce_fusion
  10.5 0.1 convert_reduce_fusion
  10.6 0.8 gather_fusion
  11.5 0.8 broadcast_select_fusion
  12.9 0.8 compare_and_fusion.1
  13.7 0.7 gather_fusion.4
  14.5 3.2 %collective-permute-start.1 = (f32[64,256]{1,0:T(8,128)S(1)}, f32[64,256]{1,0:T(8,128)S(1)}, u32[]{:S(2)}, u32[]{:S(2)}) collective-permute-start(f32[64,256]{1,0:T(8,128)S(1)} %select_select_fusion), channel_id=1, source_target_pairs={{0,1},{1,2},{2,3},{3,4},{4,5},{5,6},{6,7},{7,8},{8,9},{9,10},{10,1... | collective-permute-start | bytes 196616 | tf_op jit(solution)/shard_map/ppermute | solution.py:37
  17.8 0.1 add.422
  17.9 1.1 fusion.11
  19.0 2.6 %collective-permute-done.1 = f32[64,256]{1,0:T(8,128)S(1)} collective-permute-done((f32[64,256]{1,0:T(8,128)S(1)}, f32[64,256]{1,0:T(8,128)S(1)}, u32[]{:S(2)}, u32[]{:S(2)}) %collective-permute-start.1) | collective-permute-done | bytes 65568 | tf_op jit(solution)/shard_map/ppermute | solution.py:37
  21.7 2.1 %collective-permute-start.2 = (f32[64,256]{1,0:T(8,128)S(1)}, f32[64,256]{1,0:T(8,128)S(1)}, u32[]{:S(2)}, u32[]{:S(2)}) collective-permute-start(f32[64,256]{1,0:T(8,128)S(1)} %fusion.106), channel_id=1, source_target_pairs={{0,2},{1,3},{2,4},{3,5},{4,6},{5,7},{6,8},{7,9},{8,10},{9,11},{10,... | collective-permute-start | bytes 196616 | tf_op jit(solution)/shard_map/ppermute | solution.py:37
  23.8 1.1 gather_fusion.2
  25.0 4.8 %collective-permute-done.2 = f32[64,256]{1,0:T(8,128)S(1)} collective-permute-done((f32[64,256]{1,0:T(8,128)S(1)}, f32[64,256]{1,0:T(8,128)S(1)}, u32[]{:S(2)}, u32[]{:S(2)}) %collective-permute-start.2) | collective-permute-done | bytes 65568 | tf_op jit(solution)/shard_map/ppermute | solution.py:37
  29.8 5.7 %collective-permute-start.3 = (f32[64,256]{1,0:T(8,128)S(1)}, f32[64,256]{1,0:T(8,128)S(1)}, u32[]{:S(2)}, u32[]{:S(2)}) collective-permute-start(f32[64,256]{1,0:T(8,128)S(1)} %add.454), channel_id=1, source_target_pairs={{0,4},{1,5},{2,6},{3,7},{4,8},{5,9},{6,10},{7,11},{8,12},{9,13},{1... | collective-permute-start | bytes 196616 | tf_op jit(solution)/shard_map/ppermute | solution.py:37
  35.6 4.9 %collective-permute-done.3 = f32[64,256]{1,0:T(8,128)S(1)} collective-permute-done((f32[64,256]{1,0:T(8,128)S(1)}, f32[64,256]{1,0:T(8,128)S(1)}, u32[]{:S(2)}, u32[]{:S(2)}) %collective-permute-start.3) | collective-permute-done | bytes 65568 | tf_op jit(solution)/shard_map/ppermute | solution.py:37
  40.5 3.2 %collective-permute-start.4 = (f32[64,256]{1,0:T(8,128)S(1)}, f32[64,256]{1,0:T(8,128)S(1)}, u32[]{:S(2)}, u32[]{:S(2)}) collective-permute-start(f32[64,256]{1,0:T(8,128)S(1)} %add.455), channel_id=1, source_target_pairs={{0,8},{1,9},{2,10},{3,11},{4,12},{5,13},{6,14},{7,15},{8,16},{9,17... | collective-permute-start | bytes 196616 | tf_op jit(solution)/shard_map/ppermute | solution.py:37
  43.7 4.8 %collective-permute-done.4 = f32[64,256]{1,0:T(8,128)S(1)} collective-permute-done((f32[64,256]{1,0:T(8,128)S(1)}, f32[64,256]{1,0:T(8,128)S(1)}, u32[]{:S(2)}, u32[]{:S(2)}) %collective-permute-start.4) | collective-permute-done | bytes 65568 | tf_op jit(solution)/shard_map/ppermute | solution.py:37
  48.5 3.0 %collective-permute-start.5 = (f32[64,256]{1,0:T(8,128)S(1)}, f32[64,256]{1,0:T(8,128)S(1)}, u32[]{:S(2)}, u32[]{:S(2)}) collective-permute-start(f32[64,256]{1,0:T(8,128)S(1)} %add.456), channel_id=1, source_target_pairs={{0,16},{1,17},{2,18},{3,19},{4,20},{5,21},{6,22},{7,23},{8,24},{9,... | collective-permute-start | bytes 196616 | tf_op jit(solution)/shard_map/ppermute | solution.py:37
  51.5 3.8 %collective-permute-done.5 = f32[64,256]{1,0:T(8,128)S(1)} collective-permute-done((f32[64,256]{1,0:T(8,128)S(1)}, f32[64,256]{1,0:T(8,128)S(1)}, u32[]{:S(2)}, u32[]{:S(2)}) %collective-permute-start.5) | collective-permute-done | bytes 65568 | tf_op jit(solution)/shard_map/ppermute | solution.py:37
  55.4 6.8 %collective-permute-start.6 = (f32[64,256]{1,0:T(8,128)S(1)}, f32[64,256]{1,0:T(8,128)S(1)}, u32[]{:S(2)}, u32[]{:S(2)}) collective-permute-start(f32[64,256]{1,0:T(8,128)S(1)} %add.457), channel_id=1, source_target_pairs={{0,32},{32,64},{64,96},{96,128},{128,160},{160,192},{192,224},{224... | collective-permute-start | bytes 196616 | tf_op jit(solution)/shard_map/ppermute | solution.py:37
  62.2 0.1 add.445
  62.3 5.1 %collective-permute-done.6 = f32[64,256]{1,0:T(8,128)S(1)} collective-permute-done((f32[64,256]{1,0:T(8,128)S(1)}, f32[64,256]{1,0:T(8,128)S(1)}, u32[]{:S(2)}, u32[]{:S(2)}) %collective-permute-start.6) | collective-permute-done | bytes 65568 | tf_op jit(solution)/shard_map/ppermute | solution.py:37
  67.4 1.9 %collective-permute-start.7 = (f32[64,256]{1,0:T(8,128)S(1)}, f32[64,256]{1,0:T(8,128)S(1)}, u32[]{:S(2)}, u32[]{:S(2)}) collective-permute-start(f32[64,256]{1,0:T(8,128)S(1)} %add.458), channel_id=1, source_target_pairs={{0,64},{32,96},{64,128},{96,160},{128,192},{160,224},{192,256},{22... | collective-permute-start | bytes 196616 | tf_op jit(solution)/shard_map/ppermute | solution.py:37
  69.4 4.8 %collective-permute-done.7 = f32[64,256]{1,0:T(8,128)S(1)} collective-permute-done((f32[64,256]{1,0:T(8,128)S(1)}, f32[64,256]{1,0:T(8,128)S(1)}, u32[]{:S(2)}, u32[]{:S(2)}) %collective-permute-start.7) | collective-permute-done | bytes 65568 | tf_op jit(solution)/shard_map/ppermute | solution.py:37
  74.2 1.9 %collective-permute-start.8 = (f32[64,256]{1,0:T(8,128)S(1)}, f32[64,256]{1,0:T(8,128)S(1)}, u32[]{:S(2)}, u32[]{:S(2)}) collective-permute-start(f32[64,256]{1,0:T(8,128)S(1)} %add.459), channel_id=1, source_target_pairs={{0,128},{32,160},{64,192},{96,224},{128,256},{160,288},{192,320},{... | collective-permute-start | bytes 196616 | tf_op jit(solution)/shard_map/ppermute | solution.py:37
  76.2 5.9 %collective-permute-done.8 = f32[64,256]{1,0:T(8,128)S(1)} collective-permute-done((f32[64,256]{1,0:T(8,128)S(1)}, f32[64,256]{1,0:T(8,128)S(1)}, u32[]{:S(2)}, u32[]{:S(2)}) %collective-permute-start.8) | collective-permute-done | bytes 65568 | tf_op jit(solution)/shard_map/ppermute | solution.py:37
  82.1 4.7 %collective-permute-start.9 = (f32[64,256]{1,0:T(8,128)S(1)}, f32[64,256]{1,0:T(8,128)S(1)}, u32[]{:S(2)}, u32[]{:S(2)}) collective-permute-start(f32[64,256]{1,0:T(8,128)S(1)} %add.460), channel_id=1, source_target_pairs={{0,256},{32,288},{64,320},{96,352},{128,384},{160,416},{192,448},{... | collective-permute-start | bytes 196616 | tf_op jit(solution)/shard_map/ppermute | solution.py:37
  86.8 4.2 %collective-permute-done.9 = f32[64,256]{1,0:T(8,128)S(1)} collective-permute-done((f32[64,256]{1,0:T(8,128)S(1)}, f32[64,256]{1,0:T(8,128)S(1)}, u32[]{:S(2)}, u32[]{:S(2)}) %collective-permute-start.9) | collective-permute-done | bytes 65568 | tf_op jit(solution)/shard_map/ppermute | solution.py:37
  91.0 0.1 multiply_reduce_fusion.2
  91.1 0.9 select_add_fusion.a_ref
  92.0 7.6 %shard_map.59 = (f32[64,64]{1,0:T(8,128)}, f32[64,64]{1,0:T(8,128)}) custom-call(f32[64,64]{1,0:T(8,128)} %select_add_fusion.a_ref), custom_call_target="tpu_custom_call" | custom-call | tf_op jit(solution)/shard_map/pallas_call | solution.py:88
  99.5 3.5 %all-gather.2.cloned.1.call-done = f32[5120,256]{1,0:T(8,128)} async-done(((f32[160,256]{1,0:T(8,128)}), f32[5120,256]{1,0:T(8,128)}) %all-gather.2.cloned.1.call-update) | async-done | bytes 5242896 | tf_op jit(solution)/shard_map/all_gather | solution.py:116
  103.0 3.2 %gather_fusion.3 = f32[128,256]{1,0:T(8,128)S(1)} fusion(f32[5120,256]{1,0:T(8,128)} %all-gather.2.cloned.1.call-done, s32[1024]{0:T(1024)S(1)} %pad_clamp_fusion.1), kind=kCustom, calls=%fused_computation.3 | custom fusion | bytes 262656 | tf_op jit(solution)/shard_map/jit(_take)/gather | solution.py:127
  106.4 13.6 %collective-permute-start = (f32[128,256]{1,0:T(8,128)S(1)}, f32[128,256]{1,0:T(8,128)S(1)}, u32[]{:S(2)}, u32[]{:S(2)}) collective-permute-start(f32[128,256]{1,0:T(8,128)S(1)} %broadcast_select_fusion.1), channel_id=1, source_target_pairs={{0,0},{1,32},{2,64},{3,96},{4,128},{5,160},{6,192},{7,224},{8,256}... | collective-permute-start | bytes 393224 | tf_op jit(solution)/shard_map/ppermute | solution.py:128
  120.0 18.6 %gather_fusion.1 = f32[4096,256]{1,0:T(8,128)} fusion(f32[5120,256]{1,0:T(8,128)} %all-gather.2.cloned.1.call-done, s32[4096]{0:T(1024)S(1)} %fusion.79), kind=kCustom, calls=%fused_computation.1 | custom fusion | bytes 8404992 | tf_op jit(solution)/shard_map/jit(_take)/gather | solution.py:120
  138.5 3.1 %multiply_reduce_fusion = f32[4096]{0:T(1024)S(1)} fusion(f32[4096,256]{1,0:T(8,128)} %gather_fusion.1, f32[256]{0:T(256)S(1)} %broadcast_divide_fusion, pred[4096]{0:T(1024)(128)(4,1)S(1)} %get-tuple-element.4), kind=kLoop, calls=%fused_computation.11 | loop fusion | flops 4190208 | bytes 4215808 | tf_op jit(solution)/shard_map/reduce_sum | solution.py:53
  141.6 0.4 copy-done.1
  142.0 4.6 %fusion.1 = f32[4096,64]{0,1:T(8,128)S(1)} fusion(f32[64,256]{1,0:T(8,128)S(1)} %get-tuple-element.9, f32[4096,256]{1,0:T(8,128)S(1)} %copy-done.1, f32[256]{0:T(256)S(1)} %broadcast_divide_fusion, pred[4096]{0:T(1024)(128)(4,1)S(1)} %get-tuple-element.4, f32[64]{0:T(128)S(1)} %get-tuple-element.8, f32[4096]{0:T(1024)S(1)} %multiply_reduce_fusion), kind=kOutput, calls=%fused_computation.10 | convolution fusion | flops 808452096 | bytes 5330176 | tf_op jit(solution)/shard_map/dot_general | solution.py:55
  146.6 1.7 %fusion.15 = f32[4096,64]{0,1:T(8,128)S(1)} fusion(f32[64,64]{1,0:T(8,128)S(1)} %copy-done.3, f32[4096,64]{0,1:T(8,128)S(1)} %fusion.1, s32[4096]{0:T(1024)S(1)} %fusion.65, s32[64]{0:T(128)S(1)} %iota_add_fusion.2), kind=kOutput, calls=%fused_computation.29 | convolution fusion | flops 203685888 | bytes 2130176 | tf_op jit(solution)/shard_map/dot_general | solution.py:92
  148.3 0.3 convolution_multiply_fusion.3
  148.5 0.1 multiply_reduce_fusion.1
  148.7 0.3 fusion.41
  148.9 3.5 %convolution_multiply_fusion.1 = f32[4096,128]{1,0:T(8,128)S(1)} fusion(f32[4096,256]{1,0:T(8,128)S(1)} %copy-done.1, f32[256]{0:T(256)S(1)} %broadcast_divide_fusion, pred[4096]{0:T(1024)(128)(4,1)S(1)} %get-tuple-element.4, f32[128,256]{1,0:T(8,128)S(1)} %collective-permute-done), kind=kOutput, calls=%fused_computation.7 | convolution fusion | flops 1613266944 | bytes 6427648 | tf_op jit(solution)/shard_map/dot_general | solution.py:55
  152.4 6.1 %convolution_subtract_fusion = f32[4096,128]{1,0:T(8,128)} fusion(f32[4096,64]{0,1:T(8,128)S(1)} %fusion.15, f32[128,64]{0,1:T(8,128)S(1)} %fusion.41, f32[4096,128]{1,0:T(8,128)S(1)} %convolution_multiply_fusion.1, s32[128]{0:T(128)S(1)} %add.445, f32[128]{0:T(128)S(1)} %multiply_reduce_fusion.1, f32[4096]{0:T(1024)S(1)} %multiply_reduce_fusion, ...), kind=kOutput, calls=%fused_computation.6 | convolution fusion | flops 409468928 | bytes 5309440 | tf_op jit(solution)/shard_map/dot_general | solution.py:147
  (47 shorter events, 0.9 us)
Async XLA Ops:
  7.2 3.5 %copy-start = (f32[256,256]{1,0:T(8,128)S(1)}, f32[256,256]{1,0:T(8,128)}, u32[]{:S(2)}) copy-start(f32[256,256]{1,0:T(8,128)} %param.4) | copy-start | bytes 786436
  7.2 11.8 %copy-start.2 = (f32[256]{0:T(256)S(1)}, f32[256]{0:T(256)}, u32[]{:S(2)}) copy-start(f32[256]{0:T(256)} %param.6) | copy-start | bytes 3076
  7.2 95.8 %all-gather.2.cloned.1.call-start = ((), (), s32[]{:S(2)}) async-start(), calls=%async_computation | async-start | bytes 5406720 | tf_op jit(solution)/shard_map/all_gather | solution.py:116
  14.5 7.1 %collective-permute-start.1 = (f32[64,256]{1,0:T(8,128)S(1)}, f32[64,256]{1,0:T(8,128)S(1)}, u32[]{:S(2)}, u32[]{:S(2)}) collective-permute-start(f32[64,256]{1,0:T(8,128)S(1)} %select_select_fusion), channel_id=1, source_target_pairs={{0,1},{1,2},{2,3},{3,4},{4,5},{5,6},{6,7},{7,8},{8,9},{9,10},{10,1... | collective-permute-start | bytes 196616 | tf_op jit(solution)/shard_map/ppermute | solution.py:37
  21.7 8.1 %collective-permute-start.2 = (f32[64,256]{1,0:T(8,128)S(1)}, f32[64,256]{1,0:T(8,128)S(1)}, u32[]{:S(2)}, u32[]{:S(2)}) collective-permute-start(f32[64,256]{1,0:T(8,128)S(1)} %fusion.106), channel_id=1, source_target_pairs={{0,2},{1,3},{2,4},{3,5},{4,6},{5,7},{6,8},{7,9},{8,10},{9,11},{10,... | collective-permute-start | bytes 196616 | tf_op jit(solution)/shard_map/ppermute | solution.py:37
  29.8 10.7 %collective-permute-start.3 = (f32[64,256]{1,0:T(8,128)S(1)}, f32[64,256]{1,0:T(8,128)S(1)}, u32[]{:S(2)}, u32[]{:S(2)}) collective-permute-start(f32[64,256]{1,0:T(8,128)S(1)} %add.454), channel_id=1, source_target_pairs={{0,4},{1,5},{2,6},{3,7},{4,8},{5,9},{6,10},{7,11},{8,12},{9,13},{1... | collective-permute-start | bytes 196616 | tf_op jit(solution)/shard_map/ppermute | solution.py:37
  40.5 8.0 %collective-permute-start.4 = (f32[64,256]{1,0:T(8,128)S(1)}, f32[64,256]{1,0:T(8,128)S(1)}, u32[]{:S(2)}, u32[]{:S(2)}) collective-permute-start(f32[64,256]{1,0:T(8,128)S(1)} %add.455), channel_id=1, source_target_pairs={{0,8},{1,9},{2,10},{3,11},{4,12},{5,13},{6,14},{7,15},{8,16},{9,17... | collective-permute-start | bytes 196616 | tf_op jit(solution)/shard_map/ppermute | solution.py:37
  48.5 6.8 %collective-permute-start.5 = (f32[64,256]{1,0:T(8,128)S(1)}, f32[64,256]{1,0:T(8,128)S(1)}, u32[]{:S(2)}, u32[]{:S(2)}) collective-permute-start(f32[64,256]{1,0:T(8,128)S(1)} %add.456), channel_id=1, source_target_pairs={{0,16},{1,17},{2,18},{3,19},{4,20},{5,21},{6,22},{7,23},{8,24},{9,... | collective-permute-start | bytes 196616 | tf_op jit(solution)/shard_map/ppermute | solution.py:37
  55.4 12.0 %collective-permute-start.6 = (f32[64,256]{1,0:T(8,128)S(1)}, f32[64,256]{1,0:T(8,128)S(1)}, u32[]{:S(2)}, u32[]{:S(2)}) collective-permute-start(f32[64,256]{1,0:T(8,128)S(1)} %add.457), channel_id=1, source_target_pairs={{0,32},{32,64},{64,96},{96,128},{128,160},{160,192},{192,224},{224... | collective-permute-start | bytes 196616 | tf_op jit(solution)/shard_map/ppermute | solution.py:37
  67.4 6.8 %collective-permute-start.7 = (f32[64,256]{1,0:T(8,128)S(1)}, f32[64,256]{1,0:T(8,128)S(1)}, u32[]{:S(2)}, u32[]{:S(2)}) collective-permute-start(f32[64,256]{1,0:T(8,128)S(1)} %add.458), channel_id=1, source_target_pairs={{0,64},{32,96},{64,128},{96,160},{128,192},{160,224},{192,256},{22... | collective-permute-start | bytes 196616 | tf_op jit(solution)/shard_map/ppermute | solution.py:37
  74.2 7.8 %collective-permute-start.8 = (f32[64,256]{1,0:T(8,128)S(1)}, f32[64,256]{1,0:T(8,128)S(1)}, u32[]{:S(2)}, u32[]{:S(2)}) collective-permute-start(f32[64,256]{1,0:T(8,128)S(1)} %add.459), channel_id=1, source_target_pairs={{0,128},{32,160},{64,192},{96,224},{128,256},{160,288},{192,320},{... | collective-permute-start | bytes 196616 | tf_op jit(solution)/shard_map/ppermute | solution.py:37
  82.1 8.9 %collective-permute-start.9 = (f32[64,256]{1,0:T(8,128)S(1)}, f32[64,256]{1,0:T(8,128)S(1)}, u32[]{:S(2)}, u32[]{:S(2)}) collective-permute-start(f32[64,256]{1,0:T(8,128)S(1)} %add.460), channel_id=1, source_target_pairs={{0,256},{32,288},{64,320},{96,352},{128,384},{160,416},{192,448},{... | collective-permute-start | bytes 196616 | tf_op jit(solution)/shard_map/ppermute | solution.py:37
  106.4 41.9 %collective-permute-start = (f32[128,256]{1,0:T(8,128)S(1)}, f32[128,256]{1,0:T(8,128)S(1)}, u32[]{:S(2)}, u32[]{:S(2)}) collective-permute-start(f32[128,256]{1,0:T(8,128)S(1)} %broadcast_select_fusion.1), channel_id=1, source_target_pairs={{0,0},{1,32},{2,64},{3,96},{4,128},{5,160},{6,192},{7,224},{8,256}... | collective-permute-start | bytes 393224 | tf_op jit(solution)/shard_map/ppermute | solution.py:128
  138.5 3.4 %copy-start.1 = (f32[4096,256]{1,0:T(8,128)S(1)}, f32[4096,256]{1,0:T(8,128)}, u32[]{:S(2)}) copy-start(f32[4096,256]{1,0:T(8,128)} %gather_fusion.1) | copy-start | bytes 12582916
  138.5 8.0 %copy-start.3 = (f32[64,64]{1,0:T(8,128)S(1)}, f32[64,64]{1,0:T(8,128)}, u32[]{:S(2)}) copy-start(f32[64,64]{1,0:T(8,128)} %get-tuple-element.3) | copy-start | bytes 49156
  148.3 10.3 %copy-start.4 = (f32[4096,64]{0,1:T(8,128)}, f32[4096,64]{0,1:T(8,128)S(1)}, u32[]{:S(2)}) copy-start(f32[4096,64]{0,1:T(8,128)S(1)} %fusion.15) | copy-start | bytes 3145732
Sparse Core Ops, SparseCore 0:
  12.4 90.6 all-gather.1

commit v10 on v9

--- a/solution.py
+++ b/solution.py
@@ -117,14 +117,14 @@
     row_counts = jnp.dot(owner_hot, counts.astype(jnp.bfloat16), preferred_element_type=jnp.float32)
     slot = jnp.sum(row_counts * pixel_hot.astype(jnp.float32), axis=1).astype(jnp.int32) - 1
     pick_idx = owner * CAP + slot
-    features = jnp.take(gathered, pick_idx, axis=0)
     panel = panel_tile[0]
     tiles = panel + 1 + jnp.mod(my_col - panel - 1, cols_count) + cols_count * jnp.arange(WT)
     served = my_row + rows_count * (my_col // rows_count)
     served_tiles = panel + 1 + jnp.mod(served - panel - 1, cols_count) + cols_count * jnp.arange(WT)
     local_tiles = served_tiles // rows_count
     col_source = (local_tiles[:, None] * TB + jnp.arange(TB)[None, :]).reshape(-1)
-    col_local = jnp.take(gathered, jnp.take(pick_idx, col_source), axis=0)
+    all_rows = jnp.take(gathered, jnp.concatenate([pick_idx, jnp.take(pick_idx, col_source)]), axis=0)
+    col_local = all_rows[local_rows:]
     col_feats = lax.ppermute(col_local, ("row", "col"), window_perm(rows_count, cols_count))
     panel_row = panel % rows_count
     panel_local = panel // rows_count
@@ -133,6 +133,7 @@
     panel_part = jnp.where(held[:, None], jnp.take(pool, panel_pick % pool_rows, axis=0), 0.0)
     panel_rows = sum_broadcast(sum_broadcast(panel_part, "col", cols_count), "row", rows_count)
     panel_feats = panel_rows
+    features = all_rows[:local_rows]
     inverse_scale = 1.0 / length_scale
     scaled_rows = features * inverse_scale
     scaled_cols = col_feats * inverse_scale

time: 166 us -> 160 us (0.964)
  the two profiles are of different devices: /device:TPU:3 before, /device:TPU:66 now
where the time goes in v10:
time: 160 us
  waiting for transfers between devices  50.9 us (32%)
  starting transfers between devices  40.9 us (26%)
  matrix products  18.9 us (12%)
  local copies, waits for them, and re-layouts  16.8 us (10%)
  between operations  15.1 us (9%)
  other arithmetic  9.4 us (6%)
  Pallas kernels  7.58 us (5%)
    ppermute x9, waiting for transfers between devices, sum_broadcast(): x = x + lax.ppermute(x, axis, perm)  44.3 us
    ppermute x9, starting transfers between devices, sum_broadcast(): x = x + lax.ppermute(x, axis, perm)  31.6 us
    gather x1, local copies, waits for them, and re-layouts, body(): jnp.take(gathered, jnp.concatenate([pick_idx, jnp.take(pick_idx, col_sour...  13.7 us
    ppermute x1, starting transfers between devices, body(): lax.ppermute(col_local, ('row', 'col'), window_perm(rows_count, cols_count))  9.24 us
    dot_general x4, matrix products, kernel(): jnp.dot(left, right.T, precision=lax.Precision.HIGHEST, preferred_element...  8.99 us
    pallas_call x1, Pallas kernels, factor_and_inverse(): return pl.pallas_call(factor_kernel, out_shape=(shape, shape))(a)  7.58 us
    dot_general x1, matrix products, body(): jnp.dot(row_panel, col_panel.T, precision=lax.Precision.HIGHEST, preferre...  6.08 us
    select_n x2, other arithmetic, body(): jnp.take(gathered, jnp.concatenate([pick_idx, jnp.take(pick_idx, col_sour...  4.21 us
  transfers between devices with their start and end apart: 11, of which 11 were waited for; matrix products, arithmetic and copies ran while one was open for 7% of the time, Pallas kernels for 5%

profile of v10, /device:TPU:66, one launch (start us, length us, event | category | flops | bytes accessed | tf_op | source)
XLA Modules:
  0.0 159.6 jit_solution(2753229650069567316)
XLA Ops:
  7.2 0.8 add_select_fusion.2
  8.0 0.7 add_select_fusion.1
  8.7 0.8 fusion.8
  9.6 0.6 reduce-window.6
  10.2 0.2 slice_reduce_fusion
  10.5 0.1 convert_reduce_fusion
  10.6 0.8 gather_fusion.1
  11.5 0.8 broadcast_select_fusion.1
  12.9 0.8 compare_and_fusion.1
  13.7 0.7 gather_fusion.3
  14.4 0.1 select_select_fusion
  14.5 3.5 %collective-permute-start.1 = (f32[64,256]{1,0:T(8,128)S(1)}, f32[64,256]{1,0:T(8,128)S(1)}, u32[]{:S(2)}, u32[]{:S(2)}) collective-permute-start(f32[64,256]{1,0:T(8,128)S(1)} %select_select_fusion), channel_id=1, source_target_pairs={{0,1},{1,2},{2,3},{3,4},{4,5},{5,6},{6,7},{7,8},{8,9},{9,10},{10,1... | collective-permute-start | bytes 196616 | tf_op jit(solution)/shard_map/ppermute | solution.py:37
  18.0 1.1 fusion.7
  19.2 3.5 %collective-permute-done.1 = f32[64,256]{1,0:T(8,128)S(1)} collective-permute-done((f32[64,256]{1,0:T(8,128)S(1)}, f32[64,256]{1,0:T(8,128)S(1)}, u32[]{:S(2)}, u32[]{:S(2)}) %collective-permute-start.1) | collective-permute-done | bytes 65568 | tf_op jit(solution)/shard_map/ppermute | solution.py:37
  22.7 0.1 fusion.99
  22.8 2.4 %collective-permute-start.2 = (f32[64,256]{1,0:T(8,128)S(1)}, f32[64,256]{1,0:T(8,128)S(1)}, u32[]{:S(2)}, u32[]{:S(2)}) collective-permute-start(f32[64,256]{1,0:T(8,128)S(1)} %fusion.99), channel_id=1, source_target_pairs={{0,2},{1,3},{2,4},{3,5},{4,6},{5,7},{6,8},{7,9},{8,10},{9,11},{10,... | collective-permute-start | bytes 196616 | tf_op jit(solution)/shard_map/ppermute | solution.py:37
  25.4 6.6 %collective-permute-done.2 = f32[64,256]{1,0:T(8,128)S(1)} collective-permute-done((f32[64,256]{1,0:T(8,128)S(1)}, f32[64,256]{1,0:T(8,128)S(1)}, u32[]{:S(2)}, u32[]{:S(2)}) %collective-permute-start.2) | collective-permute-done | bytes 65568 | tf_op jit(solution)/shard_map/ppermute | solution.py:37
  32.0 5.9 %collective-permute-start.3 = (f32[64,256]{1,0:T(8,128)S(1)}, f32[64,256]{1,0:T(8,128)S(1)}, u32[]{:S(2)}, u32[]{:S(2)}) collective-permute-start(f32[64,256]{1,0:T(8,128)S(1)} %add.456), channel_id=1, source_target_pairs={{0,4},{1,5},{2,6},{3,7},{4,8},{5,9},{6,10},{7,11},{8,12},{9,13},{1... | collective-permute-start | bytes 196616 | tf_op jit(solution)/shard_map/ppermute | solution.py:37
  38.0 0.1 add.415
  38.1 5.3 %collective-permute-done.3 = f32[64,256]{1,0:T(8,128)S(1)} collective-permute-done((f32[64,256]{1,0:T(8,128)S(1)}, f32[64,256]{1,0:T(8,128)S(1)}, u32[]{:S(2)}, u32[]{:S(2)}) %collective-permute-start.3) | collective-permute-done | bytes 65568 | tf_op jit(solution)/shard_map/ppermute | solution.py:37
  43.3 4.0 %collective-permute-start.4 = (f32[64,256]{1,0:T(8,128)S(1)}, f32[64,256]{1,0:T(8,128)S(1)}, u32[]{:S(2)}, u32[]{:S(2)}) collective-permute-start(f32[64,256]{1,0:T(8,128)S(1)} %add.457), channel_id=1, source_target_pairs={{0,8},{1,9},{2,10},{3,11},{4,12},{5,13},{6,14},{7,15},{8,16},{9,17... | collective-permute-start | bytes 196616 | tf_op jit(solution)/shard_map/ppermute | solution.py:37
  47.4 1.1 gather_fusion
  48.5 3.3 %collective-permute-done.4 = f32[64,256]{1,0:T(8,128)S(1)} collective-permute-done((f32[64,256]{1,0:T(8,128)S(1)}, f32[64,256]{1,0:T(8,128)S(1)}, u32[]{:S(2)}, u32[]{:S(2)}) %collective-permute-start.4) | collective-permute-done | bytes 65568 | tf_op jit(solution)/shard_map/ppermute | solution.py:37
  51.8 3.6 %collective-permute-start.5 = (f32[64,256]{1,0:T(8,128)S(1)}, f32[64,256]{1,0:T(8,128)S(1)}, u32[]{:S(2)}, u32[]{:S(2)}) collective-permute-start(f32[64,256]{1,0:T(8,128)S(1)} %add.458), channel_id=1, source_target_pairs={{0,16},{1,17},{2,18},{3,19},{4,20},{5,21},{6,22},{7,23},{8,24},{9,... | collective-permute-start | bytes 196616 | tf_op jit(solution)/shard_map/ppermute | solution.py:37
  55.6 3.9 %collective-permute-done.5 = f32[64,256]{1,0:T(8,128)S(1)} collective-permute-done((f32[64,256]{1,0:T(8,128)S(1)}, f32[64,256]{1,0:T(8,128)S(1)}, u32[]{:S(2)}, u32[]{:S(2)}) %collective-permute-start.5) | collective-permute-done | bytes 65568 | tf_op jit(solution)/shard_map/ppermute | solution.py:37
  59.5 3.7 %collective-permute-done.6 = f32[64,256]{1,0:T(8,128)S(1)} collective-permute-done((f32[64,256]{1,0:T(8,128)S(1)}, f32[64,256]{1,0:T(8,128)S(1)}, u32[]{:S(2)}, u32[]{:S(2)}) %collective-permute-start.6) | collective-permute-done | bytes 65568 | tf_op jit(solution)/shard_map/ppermute | solution.py:37
  63.2 4.2 %collective-permute-start.7 = (f32[64,256]{1,0:T(8,128)S(1)}, f32[64,256]{1,0:T(8,128)S(1)}, u32[]{:S(2)}, u32[]{:S(2)}) collective-permute-start(f32[64,256]{1,0:T(8,128)S(1)} %add.460), channel_id=1, source_target_pairs={{0,64},{32,96},{64,128},{96,160},{128,192},{160,224},{192,256},{22... | collective-permute-start | bytes 196616 | tf_op jit(solution)/shard_map/ppermute | solution.py:37
  67.4 7.3 %collective-permute-done.7 = f32[64,256]{1,0:T(8,128)S(1)} collective-permute-done((f32[64,256]{1,0:T(8,128)S(1)}, f32[64,256]{1,0:T(8,128)S(1)}, u32[]{:S(2)}, u32[]{:S(2)}) %collective-permute-start.7) | collective-permute-done | bytes 65568 | tf_op jit(solution)/shard_map/ppermute | solution.py:37
  74.7 3.1 %collective-permute-start.8 = (f32[64,256]{1,0:T(8,128)S(1)}, f32[64,256]{1,0:T(8,128)S(1)}, u32[]{:S(2)}, u32[]{:S(2)}) collective-permute-start(f32[64,256]{1,0:T(8,128)S(1)} %add.461), channel_id=1, source_target_pairs={{0,128},{32,160},{64,192},{96,224},{128,256},{160,288},{192,320},{... | collective-permute-start | bytes 196616 | tf_op jit(solution)/shard_map/ppermute | solution.py:37
  77.9 5.1 %collective-permute-done.8 = f32[64,256]{1,0:T(8,128)S(1)} collective-permute-done((f32[64,256]{1,0:T(8,128)S(1)}, f32[64,256]{1,0:T(8,128)S(1)}, u32[]{:S(2)}, u32[]{:S(2)}) %collective-permute-start.8) | collective-permute-done | bytes 65568 | tf_op jit(solution)/shard_map/ppermute | solution.py:37
  83.0 4.8 %collective-permute-start.9 = (f32[64,256]{1,0:T(8,128)S(1)}, f32[64,256]{1,0:T(8,128)S(1)}, u32[]{:S(2)}, u32[]{:S(2)}) collective-permute-start(f32[64,256]{1,0:T(8,128)S(1)} %add.462), channel_id=1, source_target_pairs={{0,256},{32,288},{64,320},{96,352},{128,384},{160,416},{192,448},{... | collective-permute-start | bytes 196616 | tf_op jit(solution)/shard_map/ppermute | solution.py:37
  87.9 5.6 %collective-permute-done.9 = f32[64,256]{1,0:T(8,128)S(1)} collective-permute-done((f32[64,256]{1,0:T(8,128)S(1)}, f32[64,256]{1,0:T(8,128)S(1)}, u32[]{:S(2)}, u32[]{:S(2)}) %collective-permute-start.9) | collective-permute-done | bytes 65568 | tf_op jit(solution)/shard_map/ppermute | solution.py:37
  93.5 0.1 multiply_reduce_fusion.2
  93.6 0.9 select_add_fusion.a_ref
  94.5 7.6 %shard_map.59 = (f32[64,64]{1,0:T(8,128)}, f32[64,64]{1,0:T(8,128)}) custom-call(f32[64,64]{1,0:T(8,128)} %select_add_fusion.a_ref), custom_call_target="tpu_custom_call" | custom-call | tf_op jit(solution)/shard_map/pallas_call | solution.py:88
  102.0 3.2 %all-gather.2.cloned.1.call-done = f32[5120,256]{1,0:T(8,128)} async-done(((f32[160,256]{1,0:T(8,128)}), f32[5120,256]{1,0:T(8,128)}) %all-gather.2.cloned.1.call-update) | async-done | bytes 5242896 | tf_op jit(solution)/shard_map/all_gather | solution.py:116
  105.2 13.7 %gather_fusion.2 = f32[4224,256]{1,0:T(8,128)} fusion(f32[5120,256]{1,0:T(8,128)} %all-gather.2.cloned.1.call-done, s32[5120]{0:T(1024)S(1)} %pad_clamp_fusion), kind=kCustom, calls=%fused_computation.2 | custom fusion | bytes 8667648 | tf_op jit(solution)/shard_map/jit(_take)/gather | solution.py:126
  118.9 4.2 %broadcast_select_fusion = f32[4224,256]{1,0:T(8,128)S(1)} fusion(f32[4224,256]{1,0:T(8,128)} %gather_fusion.2, pred[4224]{0:T(1024)(128)(4,1)S(1)} %compare_and_fusion), kind=kLoop, calls=%fused_computation.15 | loop fusion | flops 1081344 | bytes 8654976 | tf_op jit(solution)/shard_map/jit(_take)/select_n | solution.py:126
  123.1 0.6 multiply_reduce_fusion
  123.7 9.2 %collective-permute-start = (f32[128,256]{1,0:T(8,128)S(1)}, f32[128,256]{1,0:T(8,128)S(1)}, u32[]{:S(2)}, u32[]{:S(2)}) collective-permute-start(f32[128,256]{1,0:T(8,128)S(1)} %slice.26), channel_id=1, source_target_pairs={{0,0},{1,32},{2,64},{3,96},{4,128},{5,160},{6,192},{7,224},{8,256}... | collective-permute-start | bytes 393224 | tf_op jit(solution)/shard_map/ppermute | solution.py:128
  133.0 4.3 %fusion.1 = f32[4096,64]{0,1:T(8,128)S(1)} fusion(f32[64,256]{1,0:T(8,128)S(1)} %get-tuple-element.7, f32[4224,256]{1,0:T(8,128)S(1)} %broadcast_select_fusion, f32[256]{0:T(256)S(1)} %broadcast_divide_fusion, f32[64]{0:T(128)S(1)} %get-tuple-element.6, f32[4096]{0:T(1024)S(1)} %multiply_reduce_fusion), kind=kOutput, calls=%fused_computation.9 | convolution fusion | flops 807403520 | bytes 5326336 | tf_op jit(solution)/shard_map/dot_general | solution.py:55
  137.3 1.7 %fusion.11 = f32[4096,64]{0,1:T(8,128)S(1)} fusion(f32[64,64]{1,0:T(8,128)S(1)} %copy-done.2, f32[4096,64]{0,1:T(8,128)S(1)} %fusion.1, s32[4096]{0:T(1024)S(1)} %fusion.62, s32[64]{0:T(128)S(1)} %iota_add_fusion.2), kind=kOutput, calls=%fused_computation.25 | convolution fusion | flops 203685888 | bytes 2130176 | tf_op jit(solution)/shard_map/dot_general | solution.py:92
  139.0 3.4 %collective-permute-done = f32[128,256]{1,0:T(8,128)S(1)} collective-permute-done((f32[128,256]{1,0:T(8,128)S(1)}, f32[128,256]{1,0:T(8,128)S(1)}, u32[]{:S(2)}, u32[]{:S(2)}) %collective-permute-start) | collective-permute-done | bytes 131104 | tf_op jit(solution)/shard_map/ppermute | solution.py:128
  142.4 0.3 convolution_multiply_fusion.3
  142.7 0.1 multiply_reduce_fusion.1
  142.8 0.3 fusion.37
  143.1 3.5 %convolution_multiply_fusion.1 = f32[4096,128]{1,0:T(8,128)S(1)} fusion(f32[4224,256]{1,0:T(8,128)S(1)} %broadcast_select_fusion, f32[256]{0:T(256)S(1)} %broadcast_divide_fusion, f32[128,256]{1,0:T(8,128)S(1)} %collective-permute-done), kind=kOutput, calls=%fused_computation.6 | convolution fusion | flops 1612218368 | bytes 6424576 | tf_op jit(solution)/shard_map/dot_general | solution.py:55
  146.6 6.1 %convolution_subtract_fusion = f32[4096,128]{1,0:T(8,128)} fusion(f32[4096,64]{0,1:T(8,128)S(1)} %fusion.11, f32[128,64]{0,1:T(8,128)S(1)} %fusion.37, f32[4096,128]{1,0:T(8,128)S(1)} %convolution_multiply_fusion.1, s32[128]{0:T(128)S(1)} %add.447, f32[128]{0:T(128)S(1)} %multiply_reduce_fusion.1, f32[4096]{0:T(1024)S(1)} %multiply_reduce_fusion, ...), kind=kOutput, calls=%fused_computation.5 | convolution fusion | flops 409468928 | bytes 5309440 | tf_op jit(solution)/shard_map/dot_general | solution.py:148
  (45 shorter events, 0.8 us)
Async XLA Ops:
  7.2 3.5 %copy-start = (f32[256,256]{1,0:T(8,128)S(1)}, f32[256,256]{1,0:T(8,128)}, u32[]{:S(2)}) copy-start(f32[256,256]{1,0:T(8,128)} %param.4) | copy-start | bytes 786436
  7.2 12.0 %copy-start.1 = (f32[256]{0:T(256)S(1)}, f32[256]{0:T(256)}, u32[]{:S(2)}) copy-start(f32[256]{0:T(256)} %param.6) | copy-start | bytes 3076
  7.2 98.0 %all-gather.2.cloned.1.call-start = ((), (), s32[]{:S(2)}) async-start(), calls=%async_computation | async-start | bytes 5406720 | tf_op jit(solution)/shard_map/all_gather | solution.py:116
  14.5 8.3 %collective-permute-start.1 = (f32[64,256]{1,0:T(8,128)S(1)}, f32[64,256]{1,0:T(8,128)S(1)}, u32[]{:S(2)}, u32[]{:S(2)}) collective-permute-start(f32[64,256]{1,0:T(8,128)S(1)} %select_select_fusion), channel_id=1, source_target_pairs={{0,1},{1,2},{2,3},{3,4},{4,5},{5,6},{6,7},{7,8},{8,9},{9,10},{10,1... | collective-permute-start | bytes 196616 | tf_op jit(solution)/shard_map/ppermute | solution.py:37
  22.8 9.2 %collective-permute-start.2 = (f32[64,256]{1,0:T(8,128)S(1)}, f32[64,256]{1,0:T(8,128)S(1)}, u32[]{:S(2)}, u32[]{:S(2)}) collective-permute-start(f32[64,256]{1,0:T(8,128)S(1)} %fusion.99), channel_id=1, source_target_pairs={{0,2},{1,3},{2,4},{3,5},{4,6},{5,7},{6,8},{7,9},{8,10},{9,11},{10,... | collective-permute-start | bytes 196616 | tf_op jit(solution)/shard_map/ppermute | solution.py:37
  32.0 11.3 %collective-permute-start.3 = (f32[64,256]{1,0:T(8,128)S(1)}, f32[64,256]{1,0:T(8,128)S(1)}, u32[]{:S(2)}, u32[]{:S(2)}) collective-permute-start(f32[64,256]{1,0:T(8,128)S(1)} %add.456), channel_id=1, source_target_pairs={{0,4},{1,5},{2,6},{3,7},{4,8},{5,9},{6,10},{7,11},{8,12},{9,13},{1... | collective-permute-start | bytes 196616 | tf_op jit(solution)/shard_map/ppermute | solution.py:37
  43.3 8.5 %collective-permute-start.4 = (f32[64,256]{1,0:T(8,128)S(1)}, f32[64,256]{1,0:T(8,128)S(1)}, u32[]{:S(2)}, u32[]{:S(2)}) collective-permute-start(f32[64,256]{1,0:T(8,128)S(1)} %add.457), channel_id=1, source_target_pairs={{0,8},{1,9},{2,10},{3,11},{4,12},{5,13},{6,14},{7,15},{8,16},{9,17... | collective-permute-start | bytes 196616 | tf_op jit(solution)/shard_map/ppermute | solution.py:37
  51.8 7.7 %collective-permute-start.5 = (f32[64,256]{1,0:T(8,128)S(1)}, f32[64,256]{1,0:T(8,128)S(1)}, u32[]{:S(2)}, u32[]{:S(2)}) collective-permute-start(f32[64,256]{1,0:T(8,128)S(1)} %add.458), channel_id=1, source_target_pairs={{0,16},{1,17},{2,18},{3,19},{4,20},{5,21},{6,22},{7,23},{8,24},{9,... | collective-permute-start | bytes 196616 | tf_op jit(solution)/shard_map/ppermute | solution.py:37
  59.5 3.7 %collective-permute-start.6 = (f32[64,256]{1,0:T(8,128)S(1)}, f32[64,256]{1,0:T(8,128)S(1)}, u32[]{:S(2)}, u32[]{:S(2)}) collective-permute-start(f32[64,256]{1,0:T(8,128)S(1)} %add.459), channel_id=1, source_target_pairs={{0,32},{32,64},{64,96},{96,128},{128,160},{160,192},{192,224},{224... | collective-permute-start | bytes 196616 | tf_op jit(solution)/shard_map/ppermute | solution.py:37
  63.2 11.5 %collective-permute-start.7 = (f32[64,256]{1,0:T(8,128)S(1)}, f32[64,256]{1,0:T(8,128)S(1)}, u32[]{:S(2)}, u32[]{:S(2)}) collective-permute-start(f32[64,256]{1,0:T(8,128)S(1)} %add.460), channel_id=1, source_target_pairs={{0,64},{32,96},{64,128},{96,160},{128,192},{160,224},{192,256},{22... | collective-permute-start | bytes 196616 | tf_op jit(solution)/shard_map/ppermute | solution.py:37
  74.7 8.3 %collective-permute-start.8 = (f32[64,256]{1,0:T(8,128)S(1)}, f32[64,256]{1,0:T(8,128)S(1)}, u32[]{:S(2)}, u32[]{:S(2)}) collective-permute-start(f32[64,256]{1,0:T(8,128)S(1)} %add.461), channel_id=1, source_target_pairs={{0,128},{32,160},{64,192},{96,224},{128,256},{160,288},{192,320},{... | collective-permute-start | bytes 196616 | tf_op jit(solution)/shard_map/ppermute | solution.py:37
  83.0 10.5 %collective-permute-start.9 = (f32[64,256]{1,0:T(8,128)S(1)}, f32[64,256]{1,0:T(8,128)S(1)}, u32[]{:S(2)}, u32[]{:S(2)}) collective-permute-start(f32[64,256]{1,0:T(8,128)S(1)} %add.462), channel_id=1, source_target_pairs={{0,256},{32,288},{64,320},{96,352},{128,384},{160,416},{192,448},{... | collective-permute-start | bytes 196616 | tf_op jit(solution)/shard_map/ppermute | solution.py:37
  123.1 14.2 %copy-start.2 = (f32[64,64]{1,0:T(8,128)S(1)}, f32[64,64]{1,0:T(8,128)}, u32[]{:S(2)}) copy-start(f32[64,64]{1,0:T(8,128)} %get-tuple-element.3) | copy-start | bytes 49156
  123.7 18.7 %collective-permute-start = (f32[128,256]{1,0:T(8,128)S(1)}, f32[128,256]{1,0:T(8,128)S(1)}, u32[]{:S(2)}, u32[]{:S(2)}) collective-permute-start(f32[128,256]{1,0:T(8,128)S(1)} %slice.26), channel_id=1, source_target_pairs={{0,0},{1,32},{2,64},{3,96},{4,128},{5,160},{6,192},{7,224},{8,256}... | collective-permute-start | bytes 393224 | tf_op jit(solution)/shard_map/ppermute | solution.py:128
  139.0 13.7 %copy-start.3 = (f32[4096,64]{0,1:T(8,128)}, f32[4096,64]{0,1:T(8,128)S(1)}, u32[]{:S(2)}) copy-start(f32[4096,64]{0,1:T(8,128)S(1)} %fusion.11) | copy-start | bytes 3145732
Sparse Core Ops, SparseCore 0:
  12.4 92.7 all-gather.1

commit v11 on v10

--- a/solution.py
+++ b/solution.py
@@ -123,7 +123,9 @@
     served_tiles = panel + 1 + jnp.mod(served - panel - 1, cols_count) + cols_count * jnp.arange(WT)
     local_tiles = served_tiles // rows_count
     col_source = (local_tiles[:, None] * TB + jnp.arange(TB)[None, :]).reshape(-1)
-    all_rows = jnp.take(gathered, jnp.concatenate([pick_idx, jnp.take(pick_idx, col_source)]), axis=0)
+    all_rows = jnp.take(
+        gathered, jnp.concatenate([pick_idx, jnp.take(pick_idx, col_source, mode="clip")]), axis=0, mode="clip"
+    )
     col_local = all_rows[local_rows:]
     col_feats = lax.ppermute(col_local, ("row", "col"), window_perm(rows_count, cols_count))
     panel_row = panel % rows_count

time: 160 us -> 160 us (level)
  other arithmetic: 9.4 us -> 7.64 us
    select_n x4 -> x0, other arithmetic: 4.22 us -> none  [the longest x2 4.21 us: body(): jnp.take(gathered, jnp.concatenate([pick_idx, jnp.take(pick_idx, col_sour...]
    reduce_sum x1, other arithmetic: 0.62 us -> 3.08 us  [kernel(): left_sq = jnp.sum(left * left, axis=1)]
where the time goes in v11:
time: 160 us; the launch traced here: 159 us
  waiting for transfers between devices  51.1 us (32%)
  starting transfers between devices  40.8 us (25%)
  matrix products  18.9 us (12%)
  local copies, waits for them, and re-layouts  17.8 us (11%)
  between operations  15.1 us (9%)
  other arithmetic  7.64 us (5%)
  Pallas kernels  7.57 us (5%)
    ppermute x9, waiting for transfers between devices, sum_broadcast(): x = x + lax.ppermute(x, axis, perm)  44.4 us
    ppermute x9, starting transfers between devices, sum_broadcast(): x = x + lax.ppermute(x, axis, perm)  31.5 us
    gather x1, local copies, waits for them, and re-layouts, body(): jnp.take(gathered, jnp.concatenate([pick_idx, jnp.take(pick_idx, col_sour...  13.7 us
    ppermute x1, starting transfers between devices, body(): lax.ppermute(col_local, ('row', 'col'), window_perm(rows_count, cols_count))  9.23 us
    dot_general x4, matrix products, kernel(): jnp.dot(left, right.T, precision=lax.Precision.HIGHEST, preferred_element...  8.99 us
    pallas_call x1, Pallas kernels, factor_and_inverse(): return pl.pallas_call(factor_kernel, out_shape=(shape, shape))(a)  7.57 us
    dot_general x1, matrix products, body(): jnp.dot(row_panel, col_panel.T, precision=lax.Precision.HIGHEST, preferre...  6.08 us
    ppermute x1, waiting for transfers between devices, body(): lax.ppermute(col_local, ('row', 'col'), window_perm(rows_count, cols_count))  3.41 us
  transfers between devices with their start and end apart: 11, of which 11 were waited for; matrix products, arithmetic and copies ran while one was open for 7% of the time, Pallas kernels for 5%

profile of v11, /device:TPU:66, one launch (start us, length us, event | category | flops | bytes accessed | tf_op | source)
XLA Modules:
  0.0 158.9 jit_solution(12338677869513856428)
XLA Ops:
  7.2 0.8 add_select_fusion.2
  8.0 0.7 add_select_fusion.1
  8.7 0.8 fusion.8
  9.6 0.6 reduce-window.6
  10.1 0.2 slice_reduce_fusion
  10.5 0.1 convert_reduce_fusion
  10.6 0.8 gather_fusion
  11.5 0.8 broadcast_select_fusion
  12.9 0.8 compare_and_fusion
  13.7 0.7 gather_fusion.3
  14.4 0.1 select_select_fusion
  14.5 3.5 %collective-permute-start.1 = (f32[64,256]{1,0:T(8,128)S(1)}, f32[64,256]{1,0:T(8,128)S(1)}, u32[]{:S(2)}, u32[]{:S(2)}) collective-permute-start(f32[64,256]{1,0:T(8,128)S(1)} %select_select_fusion), channel_id=1, source_target_pairs={{0,1},{1,2},{2,3},{3,4},{4,5},{5,6},{6,7},{7,8},{8,9},{9,10},{10,1... | collective-permute-start | bytes 196616 | tf_op jit(solution)/shard_map/ppermute | solution.py:37
  18.0 1.1 fusion.7
  19.1 3.6 %collective-permute-done.1 = f32[64,256]{1,0:T(8,128)S(1)} collective-permute-done((f32[64,256]{1,0:T(8,128)S(1)}, f32[64,256]{1,0:T(8,128)S(1)}, u32[]{:S(2)}, u32[]{:S(2)}) %collective-permute-start.1) | collective-permute-done | bytes 65568 | tf_op jit(solution)/shard_map/ppermute | solution.py:37
  22.7 0.1 fusion.97
  22.8 2.4 %collective-permute-start.2 = (f32[64,256]{1,0:T(8,128)S(1)}, f32[64,256]{1,0:T(8,128)S(1)}, u32[]{:S(2)}, u32[]{:S(2)}) collective-permute-start(f32[64,256]{1,0:T(8,128)S(1)} %fusion.97), channel_id=1, source_target_pairs={{0,2},{1,3},{2,4},{3,5},{4,6},{5,7},{6,8},{7,9},{8,10},{9,11},{10,... | collective-permute-start | bytes 196616 | tf_op jit(solution)/shard_map/ppermute | solution.py:37
  25.3 6.7 %collective-permute-done.2 = f32[64,256]{1,0:T(8,128)S(1)} collective-permute-done((f32[64,256]{1,0:T(8,128)S(1)}, f32[64,256]{1,0:T(8,128)S(1)}, u32[]{:S(2)}, u32[]{:S(2)}) %collective-permute-start.2) | collective-permute-done | bytes 65568 | tf_op jit(solution)/shard_map/ppermute | solution.py:37
  32.0 5.9 %collective-permute-start.3 = (f32[64,256]{1,0:T(8,128)S(1)}, f32[64,256]{1,0:T(8,128)S(1)}, u32[]{:S(2)}, u32[]{:S(2)}) collective-permute-start(f32[64,256]{1,0:T(8,128)S(1)} %add.375), channel_id=1, source_target_pairs={{0,4},{1,5},{2,6},{3,7},{4,8},{5,9},{6,10},{7,11},{8,12},{9,13},{1... | collective-permute-start | bytes 196616 | tf_op jit(solution)/shard_map/ppermute | solution.py:37
  38.0 5.3 %collective-permute-done.3 = f32[64,256]{1,0:T(8,128)S(1)} collective-permute-done((f32[64,256]{1,0:T(8,128)S(1)}, f32[64,256]{1,0:T(8,128)S(1)}, u32[]{:S(2)}, u32[]{:S(2)}) %collective-permute-start.3) | collective-permute-done | bytes 65568 | tf_op jit(solution)/shard_map/ppermute | solution.py:37
  43.3 4.0 %collective-permute-start.4 = (f32[64,256]{1,0:T(8,128)S(1)}, f32[64,256]{1,0:T(8,128)S(1)}, u32[]{:S(2)}, u32[]{:S(2)}) collective-permute-start(f32[64,256]{1,0:T(8,128)S(1)} %add.376), channel_id=1, source_target_pairs={{0,8},{1,9},{2,10},{3,11},{4,12},{5,13},{6,14},{7,15},{8,16},{9,17... | collective-permute-start | bytes 196616 | tf_op jit(solution)/shard_map/ppermute | solution.py:37
  47.4 0.1 reshape.179
  47.5 4.3 %collective-permute-done.4 = f32[64,256]{1,0:T(8,128)S(1)} collective-permute-done((f32[64,256]{1,0:T(8,128)S(1)}, f32[64,256]{1,0:T(8,128)S(1)}, u32[]{:S(2)}, u32[]{:S(2)}) %collective-permute-start.4) | collective-permute-done | bytes 65568 | tf_op jit(solution)/shard_map/ppermute | solution.py:37
  51.9 3.6 %collective-permute-start.5 = (f32[64,256]{1,0:T(8,128)S(1)}, f32[64,256]{1,0:T(8,128)S(1)}, u32[]{:S(2)}, u32[]{:S(2)}) collective-permute-start(f32[64,256]{1,0:T(8,128)S(1)} %add.377), channel_id=1, source_target_pairs={{0,16},{1,17},{2,18},{3,19},{4,20},{5,21},{6,22},{7,23},{8,24},{9,... | collective-permute-start | bytes 196616 | tf_op jit(solution)/shard_map/ppermute | solution.py:37
  55.5 1.1 gather_fusion.1
  56.7 2.9 %collective-permute-done.5 = f32[64,256]{1,0:T(8,128)S(1)} collective-permute-done((f32[64,256]{1,0:T(8,128)S(1)}, f32[64,256]{1,0:T(8,128)S(1)}, u32[]{:S(2)}, u32[]{:S(2)}) %collective-permute-start.5) | collective-permute-done | bytes 65568 | tf_op jit(solution)/shard_map/ppermute | solution.py:37
  59.6 3.7 %collective-permute-done.6 = f32[64,256]{1,0:T(8,128)S(1)} collective-permute-done((f32[64,256]{1,0:T(8,128)S(1)}, f32[64,256]{1,0:T(8,128)S(1)}, u32[]{:S(2)}, u32[]{:S(2)}) %collective-permute-start.6) | collective-permute-done | bytes 65568 | tf_op jit(solution)/shard_map/ppermute | solution.py:37
  63.3 4.1 %collective-permute-start.7 = (f32[64,256]{1,0:T(8,128)S(1)}, f32[64,256]{1,0:T(8,128)S(1)}, u32[]{:S(2)}, u32[]{:S(2)}) collective-permute-start(f32[64,256]{1,0:T(8,128)S(1)} %add.379), channel_id=1, source_target_pairs={{0,64},{32,96},{64,128},{96,160},{128,192},{160,224},{192,256},{22... | collective-permute-start | bytes 196616 | tf_op jit(solution)/shard_map/ppermute | solution.py:37
  67.4 7.3 %collective-permute-done.7 = f32[64,256]{1,0:T(8,128)S(1)} collective-permute-done((f32[64,256]{1,0:T(8,128)S(1)}, f32[64,256]{1,0:T(8,128)S(1)}, u32[]{:S(2)}, u32[]{:S(2)}) %collective-permute-start.7) | collective-permute-done | bytes 65568 | tf_op jit(solution)/shard_map/ppermute | solution.py:37
  74.7 3.1 %collective-permute-start.8 = (f32[64,256]{1,0:T(8,128)S(1)}, f32[64,256]{1,0:T(8,128)S(1)}, u32[]{:S(2)}, u32[]{:S(2)}) collective-permute-start(f32[64,256]{1,0:T(8,128)S(1)} %add.380), channel_id=1, source_target_pairs={{0,128},{32,160},{64,192},{96,224},{128,256},{160,288},{192,320},{... | collective-permute-start | bytes 196616 | tf_op jit(solution)/shard_map/ppermute | solution.py:37
  77.9 5.1 %collective-permute-done.8 = f32[64,256]{1,0:T(8,128)S(1)} collective-permute-done((f32[64,256]{1,0:T(8,128)S(1)}, f32[64,256]{1,0:T(8,128)S(1)}, u32[]{:S(2)}, u32[]{:S(2)}) %collective-permute-start.8) | collective-permute-done | bytes 65568 | tf_op jit(solution)/shard_map/ppermute | solution.py:37
  83.0 4.8 %collective-permute-start.9 = (f32[64,256]{1,0:T(8,128)S(1)}, f32[64,256]{1,0:T(8,128)S(1)}, u32[]{:S(2)}, u32[]{:S(2)}) collective-permute-start(f32[64,256]{1,0:T(8,128)S(1)} %add.381), channel_id=1, source_target_pairs={{0,256},{32,288},{64,320},{96,352},{128,384},{160,416},{192,448},{... | collective-permute-start | bytes 196616 | tf_op jit(solution)/shard_map/ppermute | solution.py:37
  87.9 5.5 %collective-permute-done.9 = f32[64,256]{1,0:T(8,128)S(1)} collective-permute-done((f32[64,256]{1,0:T(8,128)S(1)}, f32[64,256]{1,0:T(8,128)S(1)}, u32[]{:S(2)}, u32[]{:S(2)}) %collective-permute-start.9) | collective-permute-done | bytes 65568 | tf_op jit(solution)/shard_map/ppermute | solution.py:37
  93.4 0.1 multiply_reduce_fusion.2
  93.5 0.9 select_add_fusion.a_ref
  94.3 7.6 %shard_map.59 = (f32[64,64]{1,0:T(8,128)}, f32[64,64]{1,0:T(8,128)}) custom-call(f32[64,64]{1,0:T(8,128)} %select_add_fusion.a_ref), custom_call_target="tpu_custom_call" | custom-call | tf_op jit(solution)/shard_map/pallas_call | solution.py:88
  101.9 3.3 %all-gather.2.cloned.1.call-done = f32[5120,256]{1,0:T(8,128)} async-done(((f32[160,256]{1,0:T(8,128)}), f32[5120,256]{1,0:T(8,128)}) %all-gather.2.cloned.1.call-update) | async-done | bytes 5242896 | tf_op jit(solution)/shard_map/all_gather | solution.py:116
  105.2 13.7 %gather_fusion.2 = f32[4224,256]{1,0:T(8,128)} fusion(f32[5120,256]{1,0:T(8,128)} %all-gather.2.cloned.1.call-done, s32[5120]{0:T(1024)S(1)} %pad_clamp_fusion), kind=kCustom, calls=%fused_computation.2 | custom fusion | bytes 8667648 | tf_op jit(solution)/shard_map/jit(_take)/gather | solution.py:126
  118.9 1.1 slice.26
  120.0 3.1 %multiply_reduce_fusion = f32[4096]{0:T(1024)S(1)} fusion(f32[4224,256]{1,0:T(8,128)} %gather_fusion.2, f32[256]{0:T(256)S(1)} %broadcast_divide_fusion), kind=kLoop, calls=%fused_computation.11 | loop fusion | flops 3141632 | bytes 4211712 | tf_op jit(solution)/shard_map/reduce_sum | solution.py:53
  123.1 9.2 %collective-permute-start = (f32[128,256]{1,0:T(8,128)S(1)}, f32[128,256]{1,0:T(8,128)S(1)}, u32[]{:S(2)}, u32[]{:S(2)}) collective-permute-start(f32[128,256]{1,0:T(8,128)S(1)} %slice.26), channel_id=1, source_target_pairs={{0,0},{1,32},{2,64},{3,96},{4,128},{5,160},{6,192},{7,224},{8,256}... | collective-permute-start | bytes 393224 | tf_op jit(solution)/shard_map/ppermute | solution.py:130
  132.3 4.3 %fusion.1 = f32[4096,64]{0,1:T(8,128)S(1)} fusion(f32[64,256]{1,0:T(8,128)S(1)} %get-tuple-element.7, f32[4224,256]{1,0:T(8,128)S(1)} %copy-done.1, f32[256]{0:T(256)S(1)} %broadcast_divide_fusion, f32[64]{0:T(128)S(1)} %get-tuple-element.6, f32[4096]{0:T(1024)S(1)} %multiply_reduce_fusion), kind=kOutput, calls=%fused_computation.9 | convolution fusion | flops 807403520 | bytes 5326336 | tf_op jit(solution)/shard_map/dot_general | solution.py:55
  136.7 1.7 %fusion.11 = f32[4096,64]{0,1:T(8,128)S(1)} fusion(f32[64,64]{1,0:T(8,128)S(1)} %copy-done.3, f32[4096,64]{0,1:T(8,128)S(1)} %fusion.1, s32[4096]{0:T(1024)S(1)} %fusion.61, s32[64]{0:T(128)S(1)} %iota_add_fusion.2), kind=kOutput, calls=%fused_computation.24 | convolution fusion | flops 203685888 | bytes 2130176 | tf_op jit(solution)/shard_map/dot_general | solution.py:92
  138.4 3.4 %collective-permute-done = f32[128,256]{1,0:T(8,128)S(1)} collective-permute-done((f32[128,256]{1,0:T(8,128)S(1)}, f32[128,256]{1,0:T(8,128)S(1)}, u32[]{:S(2)}, u32[]{:S(2)}) %collective-permute-start) | collective-permute-done | bytes 131104 | tf_op jit(solution)/shard_map/ppermute | solution.py:130
  141.8 0.3 convolution_multiply_fusion.3
  142.1 0.1 multiply_reduce_fusion.1
  142.2 0.3 fusion.37
  142.4 3.5 %convolution_multiply_fusion.1 = f32[4096,128]{1,0:T(8,128)S(1)} fusion(f32[4224,256]{1,0:T(8,128)S(1)} %copy-done.1, f32[256]{0:T(256)S(1)} %broadcast_divide_fusion, f32[128,256]{1,0:T(8,128)S(1)} %collective-permute-done), kind=kOutput, calls=%fused_computation.6 | convolution fusion | flops 1612218368 | bytes 6424576 | tf_op jit(solution)/shard_map/dot_general | solution.py:55
  146.0 6.1 %convolution_subtract_fusion = f32[4096,128]{1,0:T(8,128)} fusion(f32[4096,64]{0,1:T(8,128)S(1)} %fusion.11, f32[128,64]{0,1:T(8,128)S(1)} %fusion.37, f32[4096,128]{1,0:T(8,128)S(1)} %convolution_multiply_fusion.1, s32[128]{0:T(128)S(1)} %add.366, f32[128]{0:T(128)S(1)} %multiply_reduce_fusion.1, f32[4096]{0:T(1024)S(1)} %multiply_reduce_fusion, ...), kind=kOutput, calls=%fused_computation.5 | convolution fusion | flops 409468928 | bytes 5309440 | tf_op jit(solution)/shard_map/dot_general | solution.py:150
  (42 shorter events, 0.6 us)
Async XLA Ops:
  7.2 3.5 %copy-start = (f32[256,256]{1,0:T(8,128)S(1)}, f32[256,256]{1,0:T(8,128)}, u32[]{:S(2)}) copy-start(f32[256,256]{1,0:T(8,128)} %param.4) | copy-start | bytes 786436
  7.2 98.0 %all-gather.2.cloned.1.call-start = ((), (), s32[]{:S(2)}) async-start(), calls=%async_computation | async-start | bytes 5406720 | tf_op jit(solution)/shard_map/all_gather | solution.py:116
  12.2 6.9 %copy-start.2 = (f32[256]{0:T(256)S(1)}, f32[256]{0:T(256)}, u32[]{:S(2)}) copy-start(f32[256]{0:T(256)} %param.6) | copy-start | bytes 3076
  14.5 8.3 %collective-permute-start.1 = (f32[64,256]{1,0:T(8,128)S(1)}, f32[64,256]{1,0:T(8,128)S(1)}, u32[]{:S(2)}, u32[]{:S(2)}) collective-permute-start(f32[64,256]{1,0:T(8,128)S(1)} %select_select_fusion), channel_id=1, source_target_pairs={{0,1},{1,2},{2,3},{3,4},{4,5},{5,6},{6,7},{7,8},{8,9},{9,10},{10,1... | collective-permute-start | bytes 196616 | tf_op jit(solution)/shard_map/ppermute | solution.py:37
  22.8 9.2 %collective-permute-start.2 = (f32[64,256]{1,0:T(8,128)S(1)}, f32[64,256]{1,0:T(8,128)S(1)}, u32[]{:S(2)}, u32[]{:S(2)}) collective-permute-start(f32[64,256]{1,0:T(8,128)S(1)} %fusion.97), channel_id=1, source_target_pairs={{0,2},{1,3},{2,4},{3,5},{4,6},{5,7},{6,8},{7,9},{8,10},{9,11},{10,... | collective-permute-start | bytes 196616 | tf_op jit(solution)/shard_map/ppermute | solution.py:37
  32.0 11.3 %collective-permute-start.3 = (f32[64,256]{1,0:T(8,128)S(1)}, f32[64,256]{1,0:T(8,128)S(1)}, u32[]{:S(2)}, u32[]{:S(2)}) collective-permute-start(f32[64,256]{1,0:T(8,128)S(1)} %add.375), channel_id=1, source_target_pairs={{0,4},{1,5},{2,6},{3,7},{4,8},{5,9},{6,10},{7,11},{8,12},{9,13},{1... | collective-permute-start | bytes 196616 | tf_op jit(solution)/shard_map/ppermute | solution.py:37
  43.3 8.5 %collective-permute-start.4 = (f32[64,256]{1,0:T(8,128)S(1)}, f32[64,256]{1,0:T(8,128)S(1)}, u32[]{:S(2)}, u32[]{:S(2)}) collective-permute-start(f32[64,256]{1,0:T(8,128)S(1)} %add.376), channel_id=1, source_target_pairs={{0,8},{1,9},{2,10},{3,11},{4,12},{5,13},{6,14},{7,15},{8,16},{9,17... | collective-permute-start | bytes 196616 | tf_op jit(solution)/shard_map/ppermute | solution.py:37
  51.9 7.7 %collective-permute-start.5 = (f32[64,256]{1,0:T(8,128)S(1)}, f32[64,256]{1,0:T(8,128)S(1)}, u32[]{:S(2)}, u32[]{:S(2)}) collective-permute-start(f32[64,256]{1,0:T(8,128)S(1)} %add.377), channel_id=1, source_target_pairs={{0,16},{1,17},{2,18},{3,19},{4,20},{5,21},{6,22},{7,23},{8,24},{9,... | collective-permute-start | bytes 196616 | tf_op jit(solution)/shard_map/ppermute | solution.py:37
  59.5 3.7 %collective-permute-start.6 = (f32[64,256]{1,0:T(8,128)S(1)}, f32[64,256]{1,0:T(8,128)S(1)}, u32[]{:S(2)}, u32[]{:S(2)}) collective-permute-start(f32[64,256]{1,0:T(8,128)S(1)} %add.378), channel_id=1, source_target_pairs={{0,32},{32,64},{64,96},{96,128},{128,160},{160,192},{192,224},{224... | collective-permute-start | bytes 196616 | tf_op jit(solution)/shard_map/ppermute | solution.py:37
  63.3 11.4 %collective-permute-start.7 = (f32[64,256]{1,0:T(8,128)S(1)}, f32[64,256]{1,0:T(8,128)S(1)}, u32[]{:S(2)}, u32[]{:S(2)}) collective-permute-start(f32[64,256]{1,0:T(8,128)S(1)} %add.379), channel_id=1, source_target_pairs={{0,64},{32,96},{64,128},{96,160},{128,192},{160,224},{192,256},{22... | collective-permute-start | bytes 196616 | tf_op jit(solution)/shard_map/ppermute | solution.py:37
  74.7 8.3 %collective-permute-start.8 = (f32[64,256]{1,0:T(8,128)S(1)}, f32[64,256]{1,0:T(8,128)S(1)}, u32[]{:S(2)}, u32[]{:S(2)}) collective-permute-start(f32[64,256]{1,0:T(8,128)S(1)} %add.380), channel_id=1, source_target_pairs={{0,128},{32,160},{64,192},{96,224},{128,256},{160,288},{192,320},{... | collective-permute-start | bytes 196616 | tf_op jit(solution)/shard_map/ppermute | solution.py:37
  83.0 10.4 %collective-permute-start.9 = (f32[64,256]{1,0:T(8,128)S(1)}, f32[64,256]{1,0:T(8,128)S(1)}, u32[]{:S(2)}, u32[]{:S(2)}) collective-permute-start(f32[64,256]{1,0:T(8,128)S(1)} %add.381), channel_id=1, source_target_pairs={{0,256},{32,288},{64,320},{96,352},{128,384},{160,416},{192,448},{... | collective-permute-start | bytes 196616 | tf_op jit(solution)/shard_map/ppermute | solution.py:37
  118.9 13.4 %copy-start.1 = (f32[4224,256]{1,0:T(8,128)S(1)}, f32[4224,256]{1,0:T(8,128)}, u32[]{:S(2)}) copy-start(f32[4224,256]{1,0:T(8,128)} %gather_fusion.2) | copy-start | bytes 12976132
  123.1 13.6 %copy-start.3 = (f32[64,64]{1,0:T(8,128)S(1)}, f32[64,64]{1,0:T(8,128)}, u32[]{:S(2)}) copy-start(f32[64,64]{1,0:T(8,128)} %get-tuple-element.3) | copy-start | bytes 49156
  123.1 18.7 %collective-permute-start = (f32[128,256]{1,0:T(8,128)S(1)}, f32[128,256]{1,0:T(8,128)S(1)}, u32[]{:S(2)}, u32[]{:S(2)}) collective-permute-start(f32[128,256]{1,0:T(8,128)S(1)} %slice.26), channel_id=1, source_target_pairs={{0,0},{1,32},{2,64},{3,96},{4,128},{5,160},{6,192},{7,224},{8,256}... | collective-permute-start | bytes 393224 | tf_op jit(solution)/shard_map/ppermute | solution.py:130
  138.4 7.6 %copy-start.4 = (f32[4096,64]{0,1:T(8,128)}, f32[4096,64]{0,1:T(8,128)S(1)}, u32[]{:S(2)}) copy-start(f32[4096,64]{0,1:T(8,128)S(1)} %fusion.11) | copy-start | bytes 3145732
Sparse Core Ops, SparseCore 0:
  12.4 92.7 all-gather.1

commit v12 on v10

--- a/solution.py
+++ b/solution.py
@@ -112,7 +112,7 @@
     mine = lax.dynamic_index_in_dim(counts, my_col, axis=0, keepdims=False)
     slots = jnp.arange(CAP, dtype=jnp.float32)
     local_idx = jnp.sum((mine[None, :] <= slots[:, None]).astype(jnp.int32), axis=1)
-    compact = jnp.take(pool, jnp.minimum(local_idx, pool_rows - 1), axis=0)
+    compact = jnp.take(pool, jnp.minimum(local_idx, pool_rows - 1), axis=0, mode="clip")
     gathered = lax.all_gather(compact, "col", axis=0, tiled=True)
     row_counts = jnp.dot(owner_hot, counts.astype(jnp.bfloat16), preferred_element_type=jnp.float32)
     slot = jnp.sum(row_counts * pixel_hot.astype(jnp.float32), axis=1).astype(jnp.int32) - 1

time: 160 us -> 160 us (level)
  no operation moved by 1% of the time
where the time goes in v12:
time: 160 us; the launch traced here: 159 us
  waiting for transfers between devices  50.9 us (32%)
  starting transfers between devices  40.9 us (26%)
  matrix products  18.9 us (12%)
  local copies, waits for them, and re-layouts  17.4 us (11%)
  between operations  15.1 us (9%)
  other arithmetic  8.63 us (5%)
  Pallas kernels  7.58 us (5%)
    ppermute x9, waiting for transfers between devices, sum_broadcast(): x = x + lax.ppermute(x, axis, perm)  44.3 us
    ppermute x9, starting transfers between devices, sum_broadcast(): x = x + lax.ppermute(x, axis, perm)  31.6 us
    gather x1, local copies, waits for them, and re-layouts, body(): jnp.take(gathered, jnp.concatenate([pick_idx, jnp.take(pick_idx, col_sour...  13.7 us
    ppermute x1, starting transfers between devices, body(): lax.ppermute(col_local, ('row', 'col'), window_perm(rows_count, cols_count))  9.24 us
    dot_general x4, matrix products, kernel(): jnp.dot(left, right.T, precision=lax.Precision.HIGHEST, preferred_element...  8.98 us
    pallas_call x1, Pallas kernels, factor_and_inverse(): return pl.pallas_call(factor_kernel, out_shape=(shape, shape))(a)  7.58 us
    dot_general x1, matrix products, body(): jnp.dot(row_panel, col_panel.T, precision=lax.Precision.HIGHEST, preferre...  6.08 us
    select_n x2, other arithmetic, body(): jnp.take(gathered, jnp.concatenate([pick_idx, jnp.take(pick_idx, col_sour...  4.21 us
  transfers between devices with their start and end apart: 11, of which 11 were waited for; matrix products, arithmetic and copies ran while one was open for 7% of the time, Pallas kernels for 5%

profile of v12, /device:TPU:66, one launch (start us, length us, event | category | flops | bytes accessed | tf_op | source)
XLA Modules:
  0.0 159.4 jit_solution(615856329838847527)
XLA Ops:
  7.2 0.8 add_select_fusion.2
  8.0 0.7 add_select_fusion.1
  8.7 0.8 fusion.8
  9.6 0.6 reduce-window.6
  10.2 0.2 slice_reduce_fusion
  10.5 0.1 convert_reduce_fusion
  10.6 1.5 gather_fusion.1
  12.8 0.8 compare_and_fusion.1
  13.6 0.7 gather_fusion.3
  14.3 0.1 select_select_fusion
  14.3 3.5 %collective-permute-start.1 = (f32[64,256]{1,0:T(8,128)S(1)}, f32[64,256]{1,0:T(8,128)S(1)}, u32[]{:S(2)}, u32[]{:S(2)}) collective-permute-start(f32[64,256]{1,0:T(8,128)S(1)} %select_select_fusion), channel_id=1, source_target_pairs={{0,1},{1,2},{2,3},{3,4},{4,5},{5,6},{6,7},{7,8},{8,9},{9,10},{10,1... | collective-permute-start | bytes 196616 | tf_op jit(solution)/shard_map/ppermute | solution.py:37
  17.9 1.1 fusion.7
  19.1 3.5 %collective-permute-done.1 = f32[64,256]{1,0:T(8,128)S(1)} collective-permute-done((f32[64,256]{1,0:T(8,128)S(1)}, f32[64,256]{1,0:T(8,128)S(1)}, u32[]{:S(2)}, u32[]{:S(2)}) %collective-permute-start.1) | collective-permute-done | bytes 65568 | tf_op jit(solution)/shard_map/ppermute | solution.py:37
  22.6 0.1 fusion.99
  22.7 2.4 %collective-permute-start.2 = (f32[64,256]{1,0:T(8,128)S(1)}, f32[64,256]{1,0:T(8,128)S(1)}, u32[]{:S(2)}, u32[]{:S(2)}) collective-permute-start(f32[64,256]{1,0:T(8,128)S(1)} %fusion.99), channel_id=1, source_target_pairs={{0,2},{1,3},{2,4},{3,5},{4,6},{5,7},{6,8},{7,9},{8,10},{9,11},{10,... | collective-permute-start | bytes 196616 | tf_op jit(solution)/shard_map/ppermute | solution.py:37
  25.3 6.6 %collective-permute-done.2 = f32[64,256]{1,0:T(8,128)S(1)} collective-permute-done((f32[64,256]{1,0:T(8,128)S(1)}, f32[64,256]{1,0:T(8,128)S(1)}, u32[]{:S(2)}, u32[]{:S(2)}) %collective-permute-start.2) | collective-permute-done | bytes 65568 | tf_op jit(solution)/shard_map/ppermute | solution.py:37
  31.9 5.9 %collective-permute-start.3 = (f32[64,256]{1,0:T(8,128)S(1)}, f32[64,256]{1,0:T(8,128)S(1)}, u32[]{:S(2)}, u32[]{:S(2)}) collective-permute-start(f32[64,256]{1,0:T(8,128)S(1)} %add.431), channel_id=1, source_target_pairs={{0,4},{1,5},{2,6},{3,7},{4,8},{5,9},{6,10},{7,11},{8,12},{9,13},{1... | collective-permute-start | bytes 196616 | tf_op jit(solution)/shard_map/ppermute | solution.py:37
  37.8 0.1 add.394
  37.9 5.3 %collective-permute-done.3 = f32[64,256]{1,0:T(8,128)S(1)} collective-permute-done((f32[64,256]{1,0:T(8,128)S(1)}, f32[64,256]{1,0:T(8,128)S(1)}, u32[]{:S(2)}, u32[]{:S(2)}) %collective-permute-start.3) | collective-permute-done | bytes 65568 | tf_op jit(solution)/shard_map/ppermute | solution.py:37
  43.2 4.0 %collective-permute-start.4 = (f32[64,256]{1,0:T(8,128)S(1)}, f32[64,256]{1,0:T(8,128)S(1)}, u32[]{:S(2)}, u32[]{:S(2)}) collective-permute-start(f32[64,256]{1,0:T(8,128)S(1)} %add.432), channel_id=1, source_target_pairs={{0,8},{1,9},{2,10},{3,11},{4,12},{5,13},{6,14},{7,15},{8,16},{9,17... | collective-permute-start | bytes 196616 | tf_op jit(solution)/shard_map/ppermute | solution.py:37
  47.2 1.1 gather_fusion
  48.4 3.3 %collective-permute-done.4 = f32[64,256]{1,0:T(8,128)S(1)} collective-permute-done((f32[64,256]{1,0:T(8,128)S(1)}, f32[64,256]{1,0:T(8,128)S(1)}, u32[]{:S(2)}, u32[]{:S(2)}) %collective-permute-start.4) | collective-permute-done | bytes 65568 | tf_op jit(solution)/shard_map/ppermute | solution.py:37
  51.7 3.6 %collective-permute-start.5 = (f32[64,256]{1,0:T(8,128)S(1)}, f32[64,256]{1,0:T(8,128)S(1)}, u32[]{:S(2)}, u32[]{:S(2)}) collective-permute-start(f32[64,256]{1,0:T(8,128)S(1)} %add.433), channel_id=1, source_target_pairs={{0,16},{1,17},{2,18},{3,19},{4,20},{5,21},{6,22},{7,23},{8,24},{9,... | collective-permute-start | bytes 196616 | tf_op jit(solution)/shard_map/ppermute | solution.py:37
  55.3 0.1 add.422
  55.5 3.9 %collective-permute-done.5 = f32[64,256]{1,0:T(8,128)S(1)} collective-permute-done((f32[64,256]{1,0:T(8,128)S(1)}, f32[64,256]{1,0:T(8,128)S(1)}, u32[]{:S(2)}, u32[]{:S(2)}) %collective-permute-start.5) | collective-permute-done | bytes 65568 | tf_op jit(solution)/shard_map/ppermute | solution.py:37
  59.4 3.7 %collective-permute-done.6 = f32[64,256]{1,0:T(8,128)S(1)} collective-permute-done((f32[64,256]{1,0:T(8,128)S(1)}, f32[64,256]{1,0:T(8,128)S(1)}, u32[]{:S(2)}, u32[]{:S(2)}) %collective-permute-start.6) | collective-permute-done | bytes 65568 | tf_op jit(solution)/shard_map/ppermute | solution.py:37
  63.1 4.2 %collective-permute-start.7 = (f32[64,256]{1,0:T(8,128)S(1)}, f32[64,256]{1,0:T(8,128)S(1)}, u32[]{:S(2)}, u32[]{:S(2)}) collective-permute-start(f32[64,256]{1,0:T(8,128)S(1)} %add.435), channel_id=1, source_target_pairs={{0,64},{32,96},{64,128},{96,160},{128,192},{160,224},{192,256},{22... | collective-permute-start | bytes 196616 | tf_op jit(solution)/shard_map/ppermute | solution.py:37
  67.3 7.3 %collective-permute-done.7 = f32[64,256]{1,0:T(8,128)S(1)} collective-permute-done((f32[64,256]{1,0:T(8,128)S(1)}, f32[64,256]{1,0:T(8,128)S(1)}, u32[]{:S(2)}, u32[]{:S(2)}) %collective-permute-start.7) | collective-permute-done | bytes 65568 | tf_op jit(solution)/shard_map/ppermute | solution.py:37
  74.6 3.1 %collective-permute-start.8 = (f32[64,256]{1,0:T(8,128)S(1)}, f32[64,256]{1,0:T(8,128)S(1)}, u32[]{:S(2)}, u32[]{:S(2)}) collective-permute-start(f32[64,256]{1,0:T(8,128)S(1)} %add.436), channel_id=1, source_target_pairs={{0,128},{32,160},{64,192},{96,224},{128,256},{160,288},{192,320},{... | collective-permute-start | bytes 196616 | tf_op jit(solution)/shard_map/ppermute | solution.py:37
  77.8 5.1 %collective-permute-done.8 = f32[64,256]{1,0:T(8,128)S(1)} collective-permute-done((f32[64,256]{1,0:T(8,128)S(1)}, f32[64,256]{1,0:T(8,128)S(1)}, u32[]{:S(2)}, u32[]{:S(2)}) %collective-permute-start.8) | collective-permute-done | bytes 65568 | tf_op jit(solution)/shard_map/ppermute | solution.py:37
  82.9 4.8 %collective-permute-start.9 = (f32[64,256]{1,0:T(8,128)S(1)}, f32[64,256]{1,0:T(8,128)S(1)}, u32[]{:S(2)}, u32[]{:S(2)}) collective-permute-start(f32[64,256]{1,0:T(8,128)S(1)} %add.437), channel_id=1, source_target_pairs={{0,256},{32,288},{64,320},{96,352},{128,384},{160,416},{192,448},{... | collective-permute-start | bytes 196616 | tf_op jit(solution)/shard_map/ppermute | solution.py:37
  87.7 5.6 %collective-permute-done.9 = f32[64,256]{1,0:T(8,128)S(1)} collective-permute-done((f32[64,256]{1,0:T(8,128)S(1)}, f32[64,256]{1,0:T(8,128)S(1)}, u32[]{:S(2)}, u32[]{:S(2)}) %collective-permute-start.9) | collective-permute-done | bytes 65568 | tf_op jit(solution)/shard_map/ppermute | solution.py:37
  93.4 0.1 multiply_reduce_fusion.2
  93.5 0.9 select_add_fusion.a_ref
  94.3 7.6 %shard_map.59 = (f32[64,64]{1,0:T(8,128)}, f32[64,64]{1,0:T(8,128)}) custom-call(f32[64,64]{1,0:T(8,128)} %select_add_fusion.a_ref), custom_call_target="tpu_custom_call" | custom-call | tf_op jit(solution)/shard_map/pallas_call | solution.py:88
  101.9 3.2 %all-gather.3.cloned.1.call-done = f32[5120,256]{1,0:T(8,128)} async-done(((f32[160,256]{1,0:T(8,128)}), f32[5120,256]{1,0:T(8,128)}) %all-gather.3.cloned.1.call-update) | async-done | bytes 5242896 | tf_op jit(solution)/shard_map/all_gather | solution.py:116
  105.1 13.7 %gather_fusion.2 = f32[4224,256]{1,0:T(8,128)} fusion(f32[5120,256]{1,0:T(8,128)} %all-gather.3.cloned.1.call-done, s32[5120]{0:T(1024)S(1)} %pad_clamp_fusion), kind=kCustom, calls=%fused_computation.2 | custom fusion | bytes 8667648 | tf_op jit(solution)/shard_map/jit(_take)/gather | solution.py:126
  118.8 4.2 %broadcast_select_fusion = f32[4224,256]{1,0:T(8,128)S(1)} fusion(f32[4224,256]{1,0:T(8,128)} %gather_fusion.2, pred[4224]{0:T(1024)(128)(4,1)S(1)} %compare_and_fusion), kind=kLoop, calls=%fused_computation.15 | loop fusion | flops 1081344 | bytes 8654976 | tf_op jit(solution)/shard_map/jit(_take)/select_n | solution.py:126
  123.0 0.6 multiply_reduce_fusion
  123.6 9.2 %collective-permute-start = (f32[128,256]{1,0:T(8,128)S(1)}, f32[128,256]{1,0:T(8,128)S(1)}, u32[]{:S(2)}, u32[]{:S(2)}) collective-permute-start(f32[128,256]{1,0:T(8,128)S(1)} %slice.26), channel_id=1, source_target_pairs={{0,0},{1,32},{2,64},{3,96},{4,128},{5,160},{6,192},{7,224},{8,256}... | collective-permute-start | bytes 393224 | tf_op jit(solution)/shard_map/ppermute | solution.py:128
  132.8 4.3 %fusion.1 = f32[4096,64]{0,1:T(8,128)S(1)} fusion(f32[64,256]{1,0:T(8,128)S(1)} %get-tuple-element.7, f32[4224,256]{1,0:T(8,128)S(1)} %broadcast_select_fusion, f32[256]{0:T(256)S(1)} %broadcast_divide_fusion, f32[64]{0:T(128)S(1)} %get-tuple-element.6, f32[4096]{0:T(1024)S(1)} %multiply_reduce_fusion), kind=kOutput, calls=%fused_computation.9 | convolution fusion | flops 807403520 | bytes 5326336 | tf_op jit(solution)/shard_map/dot_general | solution.py:55
  137.2 1.7 %fusion.11 = f32[4096,64]{0,1:T(8,128)S(1)} fusion(f32[64,64]{1,0:T(8,128)S(1)} %copy-done.2, f32[4096,64]{0,1:T(8,128)S(1)} %fusion.1, s32[4096]{0:T(1024)S(1)} %fusion.62, s32[64]{0:T(128)S(1)} %iota_add_fusion.2), kind=kOutput, calls=%fused_computation.25 | convolution fusion | flops 203685888 | bytes 2130176 | tf_op jit(solution)/shard_map/dot_general | solution.py:92
  138.9 3.4 %collective-permute-done = f32[128,256]{1,0:T(8,128)S(1)} collective-permute-done((f32[128,256]{1,0:T(8,128)S(1)}, f32[128,256]{1,0:T(8,128)S(1)}, u32[]{:S(2)}, u32[]{:S(2)}) %collective-permute-start) | collective-permute-done | bytes 131104 | tf_op jit(solution)/shard_map/ppermute | solution.py:128
  142.3 0.3 convolution_multiply_fusion.3
  142.6 0.1 multiply_reduce_fusion.1
  142.7 0.3 fusion.37
  143.0 3.5 %convolution_multiply_fusion.1 = f32[4096,128]{1,0:T(8,128)S(1)} fusion(f32[4224,256]{1,0:T(8,128)S(1)} %broadcast_select_fusion, f32[256]{0:T(256)S(1)} %broadcast_divide_fusion, f32[128,256]{1,0:T(8,128)S(1)} %collective-permute-done), kind=kOutput, calls=%fused_computation.6 | convolution fusion | flops 1612218368 | bytes 6424576 | tf_op jit(solution)/shard_map/dot_general | solution.py:55
  146.5 6.1 %convolution_subtract_fusion = f32[4096,128]{1,0:T(8,128)} fusion(f32[4096,64]{0,1:T(8,128)S(1)} %fusion.11, f32[128,64]{0,1:T(8,128)S(1)} %fusion.37, f32[4096,128]{1,0:T(8,128)S(1)} %convolution_multiply_fusion.1, s32[128]{0:T(128)S(1)} %add.422, f32[128]{0:T(128)S(1)} %multiply_reduce_fusion.1, f32[4096]{0:T(1024)S(1)} %multiply_reduce_fusion, ...), kind=kOutput, calls=%fused_computation.5 | convolution fusion | flops 409468928 | bytes 5309440 | tf_op jit(solution)/shard_map/dot_general | solution.py:148
  (42 shorter events, 0.7 us)
Async XLA Ops:
  7.2 3.5 %copy-start = (f32[256,256]{1,0:T(8,128)S(1)}, f32[256,256]{1,0:T(8,128)}, u32[]{:S(2)}) copy-start(f32[256,256]{1,0:T(8,128)} %param.4) | copy-start | bytes 786436
  7.2 11.9 %copy-start.1 = (f32[256]{0:T(256)S(1)}, f32[256]{0:T(256)}, u32[]{:S(2)}) copy-start(f32[256]{0:T(256)} %param.6) | copy-start | bytes 3076
  7.2 97.9 %all-gather.3.cloned.1.call-start = ((), (), s32[]{:S(2)}) async-start(), calls=%async_computation | async-start | bytes 5406720 | tf_op jit(solution)/shard_map/all_gather | solution.py:116
  14.3 8.3 %collective-permute-start.1 = (f32[64,256]{1,0:T(8,128)S(1)}, f32[64,256]{1,0:T(8,128)S(1)}, u32[]{:S(2)}, u32[]{:S(2)}) collective-permute-start(f32[64,256]{1,0:T(8,128)S(1)} %select_select_fusion), channel_id=1, source_target_pairs={{0,1},{1,2},{2,3},{3,4},{4,5},{5,6},{6,7},{7,8},{8,9},{9,10},{10,1... | collective-permute-start | bytes 196616 | tf_op jit(solution)/shard_map/ppermute | solution.py:37
  22.7 9.2 %collective-permute-start.2 = (f32[64,256]{1,0:T(8,128)S(1)}, f32[64,256]{1,0:T(8,128)S(1)}, u32[]{:S(2)}, u32[]{:S(2)}) collective-permute-start(f32[64,256]{1,0:T(8,128)S(1)} %fusion.99), channel_id=1, source_target_pairs={{0,2},{1,3},{2,4},{3,5},{4,6},{5,7},{6,8},{7,9},{8,10},{9,11},{10,... | collective-permute-start | bytes 196616 | tf_op jit(solution)/shard_map/ppermute | solution.py:37
  31.9 11.3 %collective-permute-start.3 = (f32[64,256]{1,0:T(8,128)S(1)}, f32[64,256]{1,0:T(8,128)S(1)}, u32[]{:S(2)}, u32[]{:S(2)}) collective-permute-start(f32[64,256]{1,0:T(8,128)S(1)} %add.431), channel_id=1, source_target_pairs={{0,4},{1,5},{2,6},{3,7},{4,8},{5,9},{6,10},{7,11},{8,12},{9,13},{1... | collective-permute-start | bytes 196616 | tf_op jit(solution)/shard_map/ppermute | solution.py:37
  43.2 8.5 %collective-permute-start.4 = (f32[64,256]{1,0:T(8,128)S(1)}, f32[64,256]{1,0:T(8,128)S(1)}, u32[]{:S(2)}, u32[]{:S(2)}) collective-permute-start(f32[64,256]{1,0:T(8,128)S(1)} %add.432), channel_id=1, source_target_pairs={{0,8},{1,9},{2,10},{3,11},{4,12},{5,13},{6,14},{7,15},{8,16},{9,17... | collective-permute-start | bytes 196616 | tf_op jit(solution)/shard_map/ppermute | solution.py:37
  51.7 7.7 %collective-permute-start.5 = (f32[64,256]{1,0:T(8,128)S(1)}, f32[64,256]{1,0:T(8,128)S(1)}, u32[]{:S(2)}, u32[]{:S(2)}) collective-permute-start(f32[64,256]{1,0:T(8,128)S(1)} %add.433), channel_id=1, source_target_pairs={{0,16},{1,17},{2,18},{3,19},{4,20},{5,21},{6,22},{7,23},{8,24},{9,... | collective-permute-start | bytes 196616 | tf_op jit(solution)/shard_map/ppermute | solution.py:37
  59.4 3.7 %collective-permute-start.6 = (f32[64,256]{1,0:T(8,128)S(1)}, f32[64,256]{1,0:T(8,128)S(1)}, u32[]{:S(2)}, u32[]{:S(2)}) collective-permute-start(f32[64,256]{1,0:T(8,128)S(1)} %add.434), channel_id=1, source_target_pairs={{0,32},{32,64},{64,96},{96,128},{128,160},{160,192},{192,224},{224... | collective-permute-start | bytes 196616 | tf_op jit(solution)/shard_map/ppermute | solution.py:37
  63.1 11.5 %collective-permute-start.7 = (f32[64,256]{1,0:T(8,128)S(1)}, f32[64,256]{1,0:T(8,128)S(1)}, u32[]{:S(2)}, u32[]{:S(2)}) collective-permute-start(f32[64,256]{1,0:T(8,128)S(1)} %add.435), channel_id=1, source_target_pairs={{0,64},{32,96},{64,128},{96,160},{128,192},{160,224},{192,256},{22... | collective-permute-start | bytes 196616 | tf_op jit(solution)/shard_map/ppermute | solution.py:37
  74.6 8.3 %collective-permute-start.8 = (f32[64,256]{1,0:T(8,128)S(1)}, f32[64,256]{1,0:T(8,128)S(1)}, u32[]{:S(2)}, u32[]{:S(2)}) collective-permute-start(f32[64,256]{1,0:T(8,128)S(1)} %add.436), channel_id=1, source_target_pairs={{0,128},{32,160},{64,192},{96,224},{128,256},{160,288},{192,320},{... | collective-permute-start | bytes 196616 | tf_op jit(solution)/shard_map/ppermute | solution.py:37
  82.9 10.5 %collective-permute-start.9 = (f32[64,256]{1,0:T(8,128)S(1)}, f32[64,256]{1,0:T(8,128)S(1)}, u32[]{:S(2)}, u32[]{:S(2)}) collective-permute-start(f32[64,256]{1,0:T(8,128)S(1)} %add.437), channel_id=1, source_target_pairs={{0,256},{32,288},{64,320},{96,352},{128,384},{160,416},{192,448},{... | collective-permute-start | bytes 196616 | tf_op jit(solution)/shard_map/ppermute | solution.py:37
  123.0 14.2 %copy-start.2 = (f32[64,64]{1,0:T(8,128)S(1)}, f32[64,64]{1,0:T(8,128)}, u32[]{:S(2)}) copy-start(f32[64,64]{1,0:T(8,128)} %get-tuple-element.3) | copy-start | bytes 49156
  123.6 18.7 %collective-permute-start = (f32[128,256]{1,0:T(8,128)S(1)}, f32[128,256]{1,0:T(8,128)S(1)}, u32[]{:S(2)}, u32[]{:S(2)}) collective-permute-start(f32[128,256]{1,0:T(8,128)S(1)} %slice.26), channel_id=1, source_target_pairs={{0,0},{1,32},{2,64},{3,96},{4,128},{5,160},{6,192},{7,224},{8,256}... | collective-permute-start | bytes 393224 | tf_op jit(solution)/shard_map/ppermute | solution.py:128
  138.9 13.7 %copy-start.3 = (f32[4096,64]{0,1:T(8,128)}, f32[4096,64]{0,1:T(8,128)S(1)}, u32[]{:S(2)}) copy-start(f32[4096,64]{0,1:T(8,128)S(1)} %fusion.11) | copy-start | bytes 3145732
Sparse Core Ops, SparseCore 0:
  12.2 92.7 all-gather.2

commit v13 on v10

--- a/solution.py
+++ b/solution.py
@@ -108,7 +108,8 @@
     owner_hot = (owner[:, None] == jnp.arange(cols_count)[None, :]).astype(jnp.bfloat16)
     pixel_hot = (my_pick[:, None] % pool_rows == jnp.arange(pool_rows)[None, :]).astype(jnp.bfloat16)
     picked = jnp.dot(owner_hot.T, pixel_hot, preferred_element_type=jnp.float32)
-    counts = jnp.cumsum(picked, axis=1)
+    upper = (jnp.arange(pool_rows)[:, None] <= jnp.arange(pool_rows)[None, :]).astype(jnp.bfloat16)
+    counts = jnp.dot(picked.astype(jnp.bfloat16), upper, preferred_element_type=jnp.float32)
     mine = lax.dynamic_index_in_dim(counts, my_col, axis=0, keepdims=False)
     slots = jnp.arange(CAP, dtype=jnp.float32)
     local_idx = jnp.sum((mine[None, :] <= slots[:, None]).astype(jnp.int32), axis=1)

time: 160 us -> 160 us (level)
  no operation moved by 1% of the time
where the time goes in v13:
time: 160 us; the launch traced here: 159 us
  waiting for transfers between devices  51.4 us (32%)
  starting transfers between devices  40.6 us (25%)
  matrix products  19 us (12%)
  local copies, waits for them, and re-layouts  16.6 us (10%)
  between operations  15.1 us (9%)
  other arithmetic  8.7 us (5%)
  Pallas kernels  7.57 us (5%)
    ppermute x9, waiting for transfers between devices, sum_broadcast(): x = x + lax.ppermute(x, axis, perm)  44.7 us
    ppermute x9, starting transfers between devices, sum_broadcast(): x = x + lax.ppermute(x, axis, perm)  31.3 us
    gather x1, local copies, waits for them, and re-layouts, body(): jnp.take(gathered, jnp.concatenate([pick_idx, jnp.take(pick_idx, col_sour...  13.7 us
    ppermute x1, starting transfers between devices, body(): lax.ppermute(col_local, ('row', 'col'), window_perm(rows_count, cols_count))  9.25 us
    dot_general x4, matrix products, kernel(): jnp.dot(left, right.T, precision=lax.Precision.HIGHEST, preferred_element...  8.99 us
    pallas_call x1, Pallas kernels, factor_and_inverse(): return pl.pallas_call(factor_kernel, out_shape=(shape, shape))(a)  7.57 us
    dot_general x1, matrix products, body(): jnp.dot(row_panel, col_panel.T, precision=lax.Precision.HIGHEST, preferre...  6.08 us
    select_n x2, other arithmetic, body(): jnp.take(gathered, jnp.concatenate([pick_idx, jnp.take(pick_idx, col_sour...  4.21 us
  transfers between devices with their start and end apart: 11, of which 11 were waited for; matrix products, arithmetic and copies ran while one was open for 7% of the time, Pallas kernels for 5%

profile of v13, /device:TPU:66, one launch (start us, length us, event | category | flops | bytes accessed | tf_op | source)
XLA Modules:
  0.0 158.9 jit_solution(17523736018479521791)
XLA Ops:
  7.2 0.8 add_select_fusion.2
  8.0 0.7 add_select_fusion.1
  8.7 0.9 fusion.11
  9.7 0.1 convert_reduce_fusion
  9.9 0.8 gather_fusion.1
  10.7 0.8 broadcast_select_fusion.1
  12.2 0.8 compare_and_fusion.1
  12.9 0.7 gather_fusion.3
  13.6 0.1 select_select_fusion
  13.7 3.5 %collective-permute-start.1 = (f32[64,256]{1,0:T(8,128)S(1)}, f32[64,256]{1,0:T(8,128)S(1)}, u32[]{:S(2)}, u32[]{:S(2)}) collective-permute-start(f32[64,256]{1,0:T(8,128)S(1)} %select_select_fusion), channel_id=1, source_target_pairs={{0,1},{1,2},{2,3},{3,4},{4,5},{5,6},{6,7},{7,8},{8,9},{9,10},{10,1... | collective-permute-start | bytes 196616 | tf_op jit(solution)/shard_map/ppermute | solution.py:37
  17.3 1.0 fusion.7
  18.4 3.6 %collective-permute-done.1 = f32[64,256]{1,0:T(8,128)S(1)} collective-permute-done((f32[64,256]{1,0:T(8,128)S(1)}, f32[64,256]{1,0:T(8,128)S(1)}, u32[]{:S(2)}, u32[]{:S(2)}) %collective-permute-start.1) | collective-permute-done | bytes 65568 | tf_op jit(solution)/shard_map/ppermute | solution.py:37
  22.0 0.1 fusion.101
  22.1 2.4 %collective-permute-start.2 = (f32[64,256]{1,0:T(8,128)S(1)}, f32[64,256]{1,0:T(8,128)S(1)}, u32[]{:S(2)}, u32[]{:S(2)}) collective-permute-start(f32[64,256]{1,0:T(8,128)S(1)} %fusion.101), channel_id=1, source_target_pairs={{0,2},{1,3},{2,4},{3,5},{4,6},{5,7},{6,8},{7,9},{8,10},{9,11},{10,... | collective-permute-start | bytes 196616 | tf_op jit(solution)/shard_map/ppermute | solution.py:37
  24.5 0.1 add.418
  24.6 6.6 %collective-permute-done.2 = f32[64,256]{1,0:T(8,128)S(1)} collective-permute-done((f32[64,256]{1,0:T(8,128)S(1)}, f32[64,256]{1,0:T(8,128)S(1)}, u32[]{:S(2)}, u32[]{:S(2)}) %collective-permute-start.2) | collective-permute-done | bytes 65568 | tf_op jit(solution)/shard_map/ppermute | solution.py:37
  31.2 5.9 %collective-permute-start.3 = (f32[64,256]{1,0:T(8,128)S(1)}, f32[64,256]{1,0:T(8,128)S(1)}, u32[]{:S(2)}, u32[]{:S(2)}) collective-permute-start(f32[64,256]{1,0:T(8,128)S(1)} %add.456), channel_id=1, source_target_pairs={{0,4},{1,5},{2,6},{3,7},{4,8},{5,9},{6,10},{7,11},{8,12},{9,13},{1... | collective-permute-start | bytes 196616 | tf_op jit(solution)/shard_map/ppermute | solution.py:37
  37.2 0.1 add.415
  37.3 5.3 %collective-permute-done.3 = f32[64,256]{1,0:T(8,128)S(1)} collective-permute-done((f32[64,256]{1,0:T(8,128)S(1)}, f32[64,256]{1,0:T(8,128)S(1)}, u32[]{:S(2)}, u32[]{:S(2)}) %collective-permute-start.3) | collective-permute-done | bytes 65568 | tf_op jit(solution)/shard_map/ppermute | solution.py:37
  42.6 4.0 %collective-permute-start.4 = (f32[64,256]{1,0:T(8,128)S(1)}, f32[64,256]{1,0:T(8,128)S(1)}, u32[]{:S(2)}, u32[]{:S(2)}) collective-permute-start(f32[64,256]{1,0:T(8,128)S(1)} %add.457), channel_id=1, source_target_pairs={{0,8},{1,9},{2,10},{3,11},{4,12},{5,13},{6,14},{7,15},{8,16},{9,17... | collective-permute-start | bytes 196616 | tf_op jit(solution)/shard_map/ppermute | solution.py:37
  46.6 1.1 gather_fusion
  47.8 3.5 %collective-permute-done.4 = f32[64,256]{1,0:T(8,128)S(1)} collective-permute-done((f32[64,256]{1,0:T(8,128)S(1)}, f32[64,256]{1,0:T(8,128)S(1)}, u32[]{:S(2)}, u32[]{:S(2)}) %collective-permute-start.4) | collective-permute-done | bytes 65568 | tf_op jit(solution)/shard_map/ppermute | solution.py:37
  51.3 3.6 %collective-permute-start.5 = (f32[64,256]{1,0:T(8,128)S(1)}, f32[64,256]{1,0:T(8,128)S(1)}, u32[]{:S(2)}, u32[]{:S(2)}) collective-permute-start(f32[64,256]{1,0:T(8,128)S(1)} %add.458), channel_id=1, source_target_pairs={{0,16},{1,17},{2,18},{3,19},{4,20},{5,21},{6,22},{7,23},{8,24},{9,... | collective-permute-start | bytes 196616 | tf_op jit(solution)/shard_map/ppermute | solution.py:37
  54.9 0.1 add.447
  55.0 3.9 %collective-permute-done.5 = f32[64,256]{1,0:T(8,128)S(1)} collective-permute-done((f32[64,256]{1,0:T(8,128)S(1)}, f32[64,256]{1,0:T(8,128)S(1)}, u32[]{:S(2)}, u32[]{:S(2)}) %collective-permute-start.5) | collective-permute-done | bytes 65568 | tf_op jit(solution)/shard_map/ppermute | solution.py:37
  59.0 3.7 %collective-permute-done.6 = f32[64,256]{1,0:T(8,128)S(1)} collective-permute-done((f32[64,256]{1,0:T(8,128)S(1)}, f32[64,256]{1,0:T(8,128)S(1)}, u32[]{:S(2)}, u32[]{:S(2)}) %collective-permute-start.6) | collective-permute-done | bytes 65568 | tf_op jit(solution)/shard_map/ppermute | solution.py:37
  62.6 4.0 %collective-permute-start.7 = (f32[64,256]{1,0:T(8,128)S(1)}, f32[64,256]{1,0:T(8,128)S(1)}, u32[]{:S(2)}, u32[]{:S(2)}) collective-permute-start(f32[64,256]{1,0:T(8,128)S(1)} %add.460), channel_id=1, source_target_pairs={{0,64},{32,96},{64,128},{96,160},{128,192},{160,224},{192,256},{22... | collective-permute-start | bytes 196616 | tf_op jit(solution)/shard_map/ppermute | solution.py:37
  66.7 7.3 %collective-permute-done.7 = f32[64,256]{1,0:T(8,128)S(1)} collective-permute-done((f32[64,256]{1,0:T(8,128)S(1)}, f32[64,256]{1,0:T(8,128)S(1)}, u32[]{:S(2)}, u32[]{:S(2)}) %collective-permute-start.7) | collective-permute-done | bytes 65568 | tf_op jit(solution)/shard_map/ppermute | solution.py:37
  74.0 3.1 %collective-permute-start.8 = (f32[64,256]{1,0:T(8,128)S(1)}, f32[64,256]{1,0:T(8,128)S(1)}, u32[]{:S(2)}, u32[]{:S(2)}) collective-permute-start(f32[64,256]{1,0:T(8,128)S(1)} %add.461), channel_id=1, source_target_pairs={{0,128},{32,160},{64,192},{96,224},{128,256},{160,288},{192,320},{... | collective-permute-start | bytes 196616 | tf_op jit(solution)/shard_map/ppermute | solution.py:37
  77.1 5.2 %collective-permute-done.8 = f32[64,256]{1,0:T(8,128)S(1)} collective-permute-done((f32[64,256]{1,0:T(8,128)S(1)}, f32[64,256]{1,0:T(8,128)S(1)}, u32[]{:S(2)}, u32[]{:S(2)}) %collective-permute-start.8) | collective-permute-done | bytes 65568 | tf_op jit(solution)/shard_map/ppermute | solution.py:37
  82.3 4.8 %collective-permute-start.9 = (f32[64,256]{1,0:T(8,128)S(1)}, f32[64,256]{1,0:T(8,128)S(1)}, u32[]{:S(2)}, u32[]{:S(2)}) collective-permute-start(f32[64,256]{1,0:T(8,128)S(1)} %add.462), channel_id=1, source_target_pairs={{0,256},{32,288},{64,320},{96,352},{128,384},{160,416},{192,448},{... | collective-permute-start | bytes 196616 | tf_op jit(solution)/shard_map/ppermute | solution.py:37
  87.1 5.6 %collective-permute-done.9 = f32[64,256]{1,0:T(8,128)S(1)} collective-permute-done((f32[64,256]{1,0:T(8,128)S(1)}, f32[64,256]{1,0:T(8,128)S(1)}, u32[]{:S(2)}, u32[]{:S(2)}) %collective-permute-start.9) | collective-permute-done | bytes 65568 | tf_op jit(solution)/shard_map/ppermute | solution.py:37
  92.7 0.1 multiply_reduce_fusion.2
  92.8 0.9 select_add_fusion.a_ref
  93.7 7.6 %shard_map.59 = (f32[64,64]{1,0:T(8,128)}, f32[64,64]{1,0:T(8,128)}) custom-call(f32[64,64]{1,0:T(8,128)} %select_add_fusion.a_ref), custom_call_target="tpu_custom_call" | custom-call | tf_op jit(solution)/shard_map/pallas_call | solution.py:88
  101.2 3.5 %all-gather.2.cloned.1.call-done = f32[5120,256]{1,0:T(8,128)} async-done(((f32[160,256]{1,0:T(8,128)}), f32[5120,256]{1,0:T(8,128)}) %all-gather.2.cloned.1.call-update) | async-done | bytes 5242896 | tf_op jit(solution)/shard_map/all_gather | solution.py:117
  104.7 13.7 %gather_fusion.2 = f32[4224,256]{1,0:T(8,128)} fusion(f32[5120,256]{1,0:T(8,128)} %all-gather.2.cloned.1.call-done, s32[5120]{0:T(1024)S(1)} %pad_clamp_fusion), kind=kCustom, calls=%fused_computation.2 | custom fusion | bytes 8667648 | tf_op jit(solution)/shard_map/jit(_take)/gather | solution.py:127
  118.4 4.2 %broadcast_select_fusion = f32[4224,256]{1,0:T(8,128)S(1)} fusion(f32[4224,256]{1,0:T(8,128)} %gather_fusion.2, pred[4224]{0:T(1024)(128)(4,1)S(1)} %compare_and_fusion), kind=kLoop, calls=%fused_computation.15 | loop fusion | flops 1081344 | bytes 8654976 | tf_op jit(solution)/shard_map/jit(_take)/select_n | solution.py:127
  122.6 0.6 multiply_reduce_fusion
  123.2 9.3 %collective-permute-start = (f32[128,256]{1,0:T(8,128)S(1)}, f32[128,256]{1,0:T(8,128)S(1)}, u32[]{:S(2)}, u32[]{:S(2)}) collective-permute-start(f32[128,256]{1,0:T(8,128)S(1)} %slice.17), channel_id=1, source_target_pairs={{0,0},{1,32},{2,64},{3,96},{4,128},{5,160},{6,192},{7,224},{8,256}... | collective-permute-start | bytes 393224 | tf_op jit(solution)/shard_map/ppermute | solution.py:129
  132.5 4.3 %fusion.1 = f32[4096,64]{0,1:T(8,128)S(1)} fusion(f32[64,256]{1,0:T(8,128)S(1)} %get-tuple-element.7, f32[4224,256]{1,0:T(8,128)S(1)} %broadcast_select_fusion, f32[256]{0:T(256)S(1)} %broadcast_divide_fusion, f32[64]{0:T(128)S(1)} %get-tuple-element.6, f32[4096]{0:T(1024)S(1)} %multiply_reduce_fusion), kind=kOutput, calls=%fused_computation.9 | convolution fusion | flops 807403520 | bytes 5326336 | tf_op jit(solution)/shard_map/dot_general | solution.py:55
  136.8 1.7 %fusion.12 = f32[4096,64]{0,1:T(8,128)S(1)} fusion(f32[64,64]{1,0:T(8,128)S(1)} %copy-done.2, f32[4096,64]{0,1:T(8,128)S(1)} %fusion.1, s32[4096]{0:T(1024)S(1)} %fusion.64, s32[64]{0:T(128)S(1)} %iota_add_fusion.2), kind=kOutput, calls=%fused_computation.26 | convolution fusion | flops 203685888 | bytes 2130176 | tf_op jit(solution)/shard_map/dot_general | solution.py:92
  138.5 3.3 %collective-permute-done = f32[128,256]{1,0:T(8,128)S(1)} collective-permute-done((f32[128,256]{1,0:T(8,128)S(1)}, f32[128,256]{1,0:T(8,128)S(1)}, u32[]{:S(2)}, u32[]{:S(2)}) %collective-permute-start) | collective-permute-done | bytes 131104 | tf_op jit(solution)/shard_map/ppermute | solution.py:129
  141.8 0.3 convolution_multiply_fusion.3
  142.1 0.1 multiply_reduce_fusion.1
  142.2 0.3 fusion.39
  142.5 3.5 %convolution_multiply_fusion.1 = f32[4096,128]{1,0:T(8,128)S(1)} fusion(f32[4224,256]{1,0:T(8,128)S(1)} %broadcast_select_fusion, f32[256]{0:T(256)S(1)} %broadcast_divide_fusion, f32[128,256]{1,0:T(8,128)S(1)} %collective-permute-done), kind=kOutput, calls=%fused_computation.6 | convolution fusion | flops 1612218368 | bytes 6424576 | tf_op jit(solution)/shard_map/dot_general | solution.py:55
  146.0 6.1 %convolution_subtract_fusion = f32[4096,128]{1,0:T(8,128)} fusion(f32[4096,64]{0,1:T(8,128)S(1)} %fusion.12, f32[128,64]{0,1:T(8,128)S(1)} %fusion.39, f32[4096,128]{1,0:T(8,128)S(1)} %convolution_multiply_fusion.1, s32[128]{0:T(128)S(1)} %add.447, f32[128]{0:T(128)S(1)} %multiply_reduce_fusion.1, f32[4096]{0:T(1024)S(1)} %multiply_reduce_fusion, ...), kind=kOutput, calls=%fused_computation.5 | convolution fusion | flops 409468928 | bytes 5309440 | tf_op jit(solution)/shard_map/dot_general | solution.py:149
  (39 shorter events, 0.5 us)
Async XLA Ops:
  7.2 2.7 %copy-start = (f32[256,256]{1,0:T(8,128)S(1)}, f32[256,256]{1,0:T(8,128)}, u32[]{:S(2)}) copy-start(f32[256,256]{1,0:T(8,128)} %param.4) | copy-start | bytes 786436
  7.2 11.2 %copy-start.1 = (f32[256]{0:T(256)S(1)}, f32[256]{0:T(256)}, u32[]{:S(2)}) copy-start(f32[256]{0:T(256)} %param.6) | copy-start | bytes 3076
  7.2 97.5 %all-gather.2.cloned.1.call-start = ((), (), s32[]{:S(2)}) async-start(), calls=%async_computation | async-start | bytes 5406720 | tf_op jit(solution)/shard_map/all_gather | solution.py:117
  13.7 8.3 %collective-permute-start.1 = (f32[64,256]{1,0:T(8,128)S(1)}, f32[64,256]{1,0:T(8,128)S(1)}, u32[]{:S(2)}, u32[]{:S(2)}) collective-permute-start(f32[64,256]{1,0:T(8,128)S(1)} %select_select_fusion), channel_id=1, source_target_pairs={{0,1},{1,2},{2,3},{3,4},{4,5},{5,6},{6,7},{7,8},{8,9},{9,10},{10,1... | collective-permute-start | bytes 196616 | tf_op jit(solution)/shard_map/ppermute | solution.py:37
  22.1 9.2 %collective-permute-start.2 = (f32[64,256]{1,0:T(8,128)S(1)}, f32[64,256]{1,0:T(8,128)S(1)}, u32[]{:S(2)}, u32[]{:S(2)}) collective-permute-start(f32[64,256]{1,0:T(8,128)S(1)} %fusion.101), channel_id=1, source_target_pairs={{0,2},{1,3},{2,4},{3,5},{4,6},{5,7},{6,8},{7,9},{8,10},{9,11},{10,... | collective-permute-start | bytes 196616 | tf_op jit(solution)/shard_map/ppermute | solution.py:37
  31.2 11.4 %collective-permute-start.3 = (f32[64,256]{1,0:T(8,128)S(1)}, f32[64,256]{1,0:T(8,128)S(1)}, u32[]{:S(2)}, u32[]{:S(2)}) collective-permute-start(f32[64,256]{1,0:T(8,128)S(1)} %add.456), channel_id=1, source_target_pairs={{0,4},{1,5},{2,6},{3,7},{4,8},{5,9},{6,10},{7,11},{8,12},{9,13},{1... | collective-permute-start | bytes 196616 | tf_op jit(solution)/shard_map/ppermute | solution.py:37
  42.6 8.6 %collective-permute-start.4 = (f32[64,256]{1,0:T(8,128)S(1)}, f32[64,256]{1,0:T(8,128)S(1)}, u32[]{:S(2)}, u32[]{:S(2)}) collective-permute-start(f32[64,256]{1,0:T(8,128)S(1)} %add.457), channel_id=1, source_target_pairs={{0,8},{1,9},{2,10},{3,11},{4,12},{5,13},{6,14},{7,15},{8,16},{9,17... | collective-permute-start | bytes 196616 | tf_op jit(solution)/shard_map/ppermute | solution.py:37
  51.3 7.7 %collective-permute-start.5 = (f32[64,256]{1,0:T(8,128)S(1)}, f32[64,256]{1,0:T(8,128)S(1)}, u32[]{:S(2)}, u32[]{:S(2)}) collective-permute-start(f32[64,256]{1,0:T(8,128)S(1)} %add.458), channel_id=1, source_target_pairs={{0,16},{1,17},{2,18},{3,19},{4,20},{5,21},{6,22},{7,23},{8,24},{9,... | collective-permute-start | bytes 196616 | tf_op jit(solution)/shard_map/ppermute | solution.py:37
  58.9 3.7 %collective-permute-start.6 = (f32[64,256]{1,0:T(8,128)S(1)}, f32[64,256]{1,0:T(8,128)S(1)}, u32[]{:S(2)}, u32[]{:S(2)}) collective-permute-start(f32[64,256]{1,0:T(8,128)S(1)} %add.459), channel_id=1, source_target_pairs={{0,32},{32,64},{64,96},{96,128},{128,160},{160,192},{192,224},{224... | collective-permute-start | bytes 196616 | tf_op jit(solution)/shard_map/ppermute | solution.py:37
  62.6 11.4 %collective-permute-start.7 = (f32[64,256]{1,0:T(8,128)S(1)}, f32[64,256]{1,0:T(8,128)S(1)}, u32[]{:S(2)}, u32[]{:S(2)}) collective-permute-start(f32[64,256]{1,0:T(8,128)S(1)} %add.460), channel_id=1, source_target_pairs={{0,64},{32,96},{64,128},{96,160},{128,192},{160,224},{192,256},{22... | collective-permute-start | bytes 196616 | tf_op jit(solution)/shard_map/ppermute | solution.py:37
  74.0 8.3 %collective-permute-start.8 = (f32[64,256]{1,0:T(8,128)S(1)}, f32[64,256]{1,0:T(8,128)S(1)}, u32[]{:S(2)}, u32[]{:S(2)}) collective-permute-start(f32[64,256]{1,0:T(8,128)S(1)} %add.461), channel_id=1, source_target_pairs={{0,128},{32,160},{64,192},{96,224},{128,256},{160,288},{192,320},{... | collective-permute-start | bytes 196616 | tf_op jit(solution)/shard_map/ppermute | solution.py:37
  82.3 10.4 %collective-permute-start.9 = (f32[64,256]{1,0:T(8,128)S(1)}, f32[64,256]{1,0:T(8,128)S(1)}, u32[]{:S(2)}, u32[]{:S(2)}) collective-permute-start(f32[64,256]{1,0:T(8,128)S(1)} %add.462), channel_id=1, source_target_pairs={{0,256},{32,288},{64,320},{96,352},{128,384},{160,416},{192,448},{... | collective-permute-start | bytes 196616 | tf_op jit(solution)/shard_map/ppermute | solution.py:37
  122.6 14.2 %copy-start.2 = (f32[64,64]{1,0:T(8,128)S(1)}, f32[64,64]{1,0:T(8,128)}, u32[]{:S(2)}) copy-start(f32[64,64]{1,0:T(8,128)} %get-tuple-element.3) | copy-start | bytes 49156
  123.2 18.6 %collective-permute-start = (f32[128,256]{1,0:T(8,128)S(1)}, f32[128,256]{1,0:T(8,128)S(1)}, u32[]{:S(2)}, u32[]{:S(2)}) collective-permute-start(f32[128,256]{1,0:T(8,128)S(1)} %slice.17), channel_id=1, source_target_pairs={{0,0},{1,32},{2,64},{3,96},{4,128},{5,160},{6,192},{7,224},{8,256}... | collective-permute-start | bytes 393224 | tf_op jit(solution)/shard_map/ppermute | solution.py:129
  138.5 13.6 %copy-start.3 = (f32[4096,64]{0,1:T(8,128)}, f32[4096,64]{0,1:T(8,128)S(1)}, u32[]{:S(2)}) copy-start(f32[4096,64]{0,1:T(8,128)S(1)} %fusion.12) | copy-start | bytes 3145732
Sparse Core Ops, SparseCore 0:
  11.7 92.9 all-gather.1
